TPU v7x, 256 devices: a whole 4x4x8 slice. The times are simulated.
256 devices in a mesh: wall: 8 (over y_lo, x), stream: 32 (over z, y_hi, core).
Axes of the slice: x: 4, y: 4 (y_hi: 2, y_lo: 2; y = y_hi * 2 + y_lo), z: 8, core: 2. Of those that a mesh axis runs over, the one named last changes fastest.
Arguments:
- velocity: float32 [3, 64, 512, 128], P(None, 'wall', 'stream'), may hold values from -6 to 6
- sample_block: int32 [8, 256], P('wall', 'stream'), may hold values from 0 to 127
- sample_member: int32 [8, 256, 1], P('wall', 'stream'), may hold values from 0 to 7; in each aligned block of 8 rows (0 to 7, 8 to 15, ..., all dimensions but the last counted through in order) at most 2 rows name the same one
- k_first: bfloat16 [8, 54, 64], P('wall'), may hold values from -6 to 6
- k_second: bfloat16 [8, 27, 64, 64], P('wall'), may hold values from -6 to 6
- w_hidden: bfloat16 [8, 2048, 2048], P('wall'), may hold values from -6 to 6
- w_out: bfloat16 [8, 2048, 2], P('wall'), may hold values from -6 to 6
Outputs:
- new_field: float32 [3, 64, 512, 128], P(None, 'wall', 'stream')
- stress: float32 [2, 8, 256], P(None, 'wall', 'stream')
- new_k_first: float32 [8, 54, 64], P('wall')
- new_k_second: float32 [8, 27, 64, 64], P('wall')
- new_w_hidden: float32 [8, 2048, 2048], P('wall', 'stream')
- new_w_out: float32 [8, 2048, 2], P('wall')
Inputs may be any that keep to these rules, and one draw needn't show every extreme that they name: `sample_member`: in the list of one slab at most 2 samples name the same member; in every draw some slab names some member exactly 2 times.
All inputs are finite; a program needn't handle non-finite values.
Results may differ from a plain program's by a relative error of at most 0.0064.
Values may be sent and summed in bfloat16 or wider, within the bound.
No kernel may reach another device: no remote copies, remote signals or barrier semaphores. Data moves between devices by JAX's collectives and lax.ppermute only.
A program may use at most 128 MiB of HBM per device.

v0:
```python
import math

import jax
import jax.numpy as jnp
import numpy as np
from jax import lax
from jax.sharding import Mesh
from jax.sharding import PartitionSpec as P

P_SIZE = 8
PY = 4
PX = 4
PZ = 8
CH = 64
CAP = 2
FEATS = 2048
STREAM = ("stream_0", "stream_1", "stream_2")


highest = lax.Precision.HIGHEST
time_step = 0.005
relax_rate = 20.0
viscosity = 0.3
learn_rate = 0.5
rms_eps = 1e-06
def extended(shard, sides, width):
    edges = {}
    for axis, dim in sides:
        size, length = (lax.axis_size(axis), shard.shape[dim])
        up = [(i, (i + 1) % size) for i in range(size)]
        last = lax.slice_in_dim(shard, length - width, length, axis=dim)
        first = lax.slice_in_dim(shard, 0, width, axis=dim)
        edges[dim] = (
            lax.ppermute(last, axis, up),
            lax.ppermute(first, axis, [(b, a) for a, b in up]),
        )
    done = []
    for _, dim in sides:
        low, high = edges[dim]
        around = [(width, width) if d in done else (0, 0) for d in range(shard.ndim)]
        shard = jnp.concatenate([jnp.pad(low, around), shard, jnp.pad(high, around)], axis=dim)
        done.append(dim)
    return shard


def in_one_piece(arrays, axis, split_dim, concat_dim, along):
    widths = [math.prod(a.shape[along:]) for a in arrays]
    both = jnp.concatenate(
        [a.reshape(*a.shape[:along], w) for a, w in zip(arrays, widths)], axis=along
    )
    whole = lax.all_to_all(both, axis, split_axis=split_dim, concat_axis=concat_dim, tiled=True)
    tiles = jnp.split(whole, [sum(widths[:k]) for k in range(1, len(widths))], axis=along)
    return tuple((b.reshape(*whole.shape[:along], *a.shape[along:]) for a, b in zip(arrays, tiles)))


def joined_along(tiles, dim):
    lengths = list(tiles.shape[1:])
    lengths[dim] *= tiles.shape[0]
    return jnp.moveaxis(tiles, 0, dim).reshape(lengths)


def gather_in_order(shard, axes, order):
    tiles = shard
    for k in order:
        tiles = lax.all_gather(tiles, axes[k])
    done = order[::-1]
    back = [done.index(k) for k in range(len(axes))]
    tiles = tiles.transpose(*back, *range(len(axes), tiles.ndim))
    return tiles.reshape(-1, *shard.shape)


def gathered_by_axis(shard, axes, order, dim):
    return joined_along(gather_in_order(shard, axes, order), dim)


def cheb_tables(points):
    order = points - 1
    node_index = np.arange(points)
    nodes = -np.cos(np.pi * node_index / order)
    end_weight = np.where((node_index == 0) | (node_index == order), 2.0, 1.0)
    parity = (-1.0) ** (node_index[:, None] + node_index[None, :])
    offdiag = 1.0 - np.eye(points)
    spread = nodes[:, None] - nodes[None, :] + np.eye(points)
    deriv = end_weight[:, None] / end_weight[None, :] * parity / spread * offdiag
    deriv = deriv - np.eye(points) * deriv.sum(axis=1)[:, None]
    highpass = parity / (order * end_weight[None, :])
    return (deriv, highpass, 0.5 * order * order)


def axis_matrices(count, periodic):
    deriv, highpass, lift_half = cheb_tables(P_SIZE)
    length = count * P_SIZE
    slope = np.kron(np.eye(count), deriv)
    upper = np.kron(np.eye(count), highpass)
    faces = count if periodic else count - 1
    for element in range(faces):
        last_node = element * P_SIZE + P_SIZE - 1
        next_node = (element + 1) % count * P_SIZE
        slope[last_node, next_node] += lift_half
        slope[last_node, last_node] -= lift_half
        slope[next_node, last_node] -= lift_half
        slope[next_node, next_node] += lift_half
    if not periodic:
        slope[0, 0] += lift_half
        slope[length - 1, length - 1] -= lift_half
    paired = jnp.asarray(np.concatenate([slope, upper], axis=0), jnp.float32)
    return (paired, lift_half)


def slot_matrix(members, member_count):
    member_hot = (members[..., None] == jnp.arange(member_count, dtype=jnp.int32)).astype(jnp.int32)
    before = jnp.cumsum(member_hot, axis=-2) - member_hot
    ranks = jnp.sum(before * member_hot, axis=-1)
    slots = members * CAP + ranks
    return (slots[..., None, :] == jnp.arange(member_count * CAP, dtype=jnp.int32)[:, None]).astype(
        jnp.float32
    )


DIMS = ("NDHWC", "DHWIO", "NDHWC")
FILTER_DIMS = ("CDHWN", "IDHWO", "NDHWC")
SAME = ((1, 1), (1, 1), (1, 1))


def silu_slope(value):
    gate = jax.nn.sigmoid(value)
    return gate * (1.0 + value * (1.0 - gate))


def conv_taps(grid, kernel):
    return lax.conv_general_dilated(
        grid, kernel, (1, 1, 1), SAME, dimension_numbers=DIMS,
        preferred_element_type=jnp.float32,
    )


def conv_filter(grid, delta):
    taps = lax.conv_general_dilated(
        grid, delta, (1, 1, 1), SAME, dimension_numbers=FILTER_DIMS,
        preferred_element_type=jnp.float32,
    )
    return jnp.moveaxis(taps, 0, 3)


def forward_back(patches, aim_rows, valid, k_first, k_second, w_hidden, w_out):
    batch = patches.shape[0]
    channels = k_second.shape[-1]
    inputs = patches.reshape(batch, 2, PY, PX, PZ).transpose(0, 2, 3, 4, 1)
    first_taps = k_first.reshape(3, 3, 3, 2, channels)
    second_taps = k_second.reshape(3, 3, 3, channels, channels)
    scale_one = 1.0 / math.sqrt(54.0)
    scale_two = 1.0 / math.sqrt(27.0 * channels)
    scale_three = 1.0 / math.sqrt(1.0 * w_hidden.shape[0])
    scale_four = 1.0 / math.sqrt(1.0 * w_hidden.shape[1])
    pre_one = conv_taps(inputs, first_taps) * scale_one
    hidden_one = jax.nn.silu(pre_one).astype(jnp.bfloat16)
    pre_two = conv_taps(hidden_one, second_taps) * scale_two
    pooled = jax.nn.silu(pre_two).reshape(batch, PY // 2, 2, PX // 2, 2, PZ, channels).mean(axis=(2, 4))
    features = pooled.reshape(batch, -1).astype(jnp.bfloat16)
    pre_three = jnp.dot(features, w_hidden, preferred_element_type=jnp.float32) * scale_three
    hidden_three = jax.nn.silu(pre_three).astype(jnp.bfloat16)
    pred = jnp.dot(hidden_three, w_out, preferred_element_type=jnp.float32) * scale_four
    error = valid.astype(jnp.float32)[:, None] * (pred - aim_rows.astype(jnp.float32))
    grad_out = jnp.dot(hidden_three.astype(jnp.float32).T, error, precision=highest) * scale_four
    delta_three = (
        jnp.dot(error, w_out.astype(jnp.float32).T, precision=highest) * scale_four * silu_slope(pre_three)
    ).astype(jnp.bfloat16)
    back_feat = jnp.dot(delta_three, w_hidden.T, preferred_element_type=jnp.float32) * scale_three
    back_grid = back_feat.reshape(batch, PY // 2, 1, PX // 2, 1, PZ, channels)
    spread_back = jnp.broadcast_to(back_grid, (batch, PY // 2, 2, PX // 2, 2, PZ, channels)).reshape(pre_two.shape) * 0.25
    delta_two = (spread_back * silu_slope(pre_two)).astype(jnp.bfloat16)
    grad_two = (conv_filter(hidden_one, delta_two) * scale_two).reshape(27, channels, channels)
    mirrored = jnp.flip(second_taps, axis=(0, 1, 2)).swapaxes(3, 4)
    back_one = conv_taps(delta_two, mirrored)
    delta_one = (back_one * scale_two * silu_slope(pre_one)).astype(jnp.bfloat16)
    grad_one = (conv_filter(inputs, delta_one) * scale_one).reshape(54, channels)
    return (pred, grad_one, grad_two, grad_out, features, delta_three)


def row_update(weight, grad):
    scale = jnp.sqrt(jnp.mean(grad * grad, axis=-1, keepdims=True) + rms_eps)
    return weight.astype(jnp.float32) - learn_rate * grad / scale


def whole_update(weight, grad):
    scale = jnp.sqrt(jnp.mean(grad * grad) + rms_eps)
    return weight.astype(jnp.float32) - learn_rate * grad / scale


def body(velocity, sample_block, sample_member, k_first, k_second, w_hidden, w_out):
    wall_count = lax.axis_size("wall")
    wall_place = lax.axis_index("wall")
    flow_count = lax.axis_size(STREAM)
    flow_place = lax.axis_index(STREAM)
    padded = extended(velocity, (("wall", 1), (STREAM, 2)), 1)
    keep_low = (wall_place > 0).astype(jnp.float32)
    keep_high = (wall_place < wall_count - 1).astype(jnp.float32)
    below = padded[:, 0, 1:-1, :] * keep_low
    above = padded[:, -1, 1:-1, :] * keep_high
    left_face = padded[:, 1:-1, 0, :]
    right_face = padded[:, 1:-1, -1, :]
    size_y, size_x, size_z = (velocity.shape[1], velocity.shape[2], velocity.shape[3])
    pair_y, lift_half = axis_matrices(size_y // P_SIZE, False)
    pair_x, lift_same = axis_matrices(size_x // P_SIZE, False)
    pair_z, lift_again = axis_matrices(size_z // P_SIZE, True)
    along_y = jnp.einsum("cyxz,wy->cwxz", velocity, pair_y, precision=highest)
    grad_y = (
        along_y[:, :size_y]
        .at[:, 0]
        .add(-lift_half * below)
        .at[:, size_y - 1]
        .add(lift_half * above)
    )
    high_y = along_y[:, size_y:]
    along_x = jnp.einsum("cyxz,wx->cywz", velocity, pair_x, precision=highest)
    grad_x = (
        along_x[:, :, :size_x]
        .at[:, :, 0]
        .add(-lift_half * left_face)
        .at[:, :, size_x - 1]
        .add(lift_half * right_face)
    )
    high_x = along_x[:, :, size_x:]
    along_z = jnp.einsum("cyxz,wz->cyxw", velocity, pair_z, precision=highest)
    grad_z = along_z[..., :size_z]
    high_z = along_z[..., size_z:]
    advect = velocity[0][None] * grad_x + velocity[1][None] * grad_y + velocity[2][None] * grad_z
    new_field = velocity + time_step * (-advect - relax_rate * (high_x + high_y + high_z))
    rows_y, rows_x, rows_z = (size_y // PY, size_x // PX, size_z // PZ)
    tangent = jnp.stack([velocity[0], velocity[2]]).reshape(2, rows_y, PY, rows_x, PX, rows_z, PZ)
    blocks = tangent.transpose(1, 3, 5, 0, 2, 4, 6).reshape(-1, 2 * PY * PX * PZ)
    slope_wall = jnp.stack([grad_y[0], grad_y[2]]).reshape(2, rows_y, PY, rows_x, PX, rows_z, PZ)
    stress_true = (
        (viscosity * jnp.mean(slope_wall, axis=(2, 4, 6))).transpose(1, 2, 3, 0).reshape(-1, 2)
    )
    picked = sample_block.reshape(-1)
    members = sample_member.reshape(-1)
    patch_rows = jnp.take(blocks, picked, axis=0).astype(jnp.bfloat16)
    aim_rows = jnp.take(stress_true, picked, axis=0).astype(jnp.bfloat16)
    select = slot_matrix(members, wall_count)
    select_half = select.astype(jnp.bfloat16)
    send_rows = jnp.dot(select_half, patch_rows, preferred_element_type=jnp.float32).astype(
        jnp.bfloat16
    )
    send_aims = jnp.dot(select_half, aim_rows, preferred_element_type=jnp.float32).astype(
        jnp.bfloat16
    )
    send_valid = jnp.sum(select, axis=1).astype(jnp.bfloat16)
    recv_rows, recv_aims, recv_valid = in_one_piece(
        (send_rows, send_aims, send_valid), "wall", 0, 0, 1
    )
    pred, grad_one, grad_two, grad_out, features, delta_three = forward_back(
        recv_rows, recv_aims, recv_valid, k_first[0], k_second[0], w_hidden[0], w_out[0]
    )
    back = lax.all_to_all(pred, "wall", split_axis=0, concat_axis=0, tiled=True)
    stress_local = jnp.dot(select.T, back, precision=highest)
    stress = stress_local.T[:, None, :]
    share_rows = FEATS // flow_count
    dense_scale = 1.0 / math.sqrt(1.0 * FEATS)
    columns_here = lax.all_to_all(features, STREAM, split_axis=1, concat_axis=0, tiled=True)
    grad_hidden = (
        jnp.dot(
            columns_here.T,
            gathered_by_axis(delta_three, STREAM, (1, 0, 2), 0),
            preferred_element_type=jnp.float32,
        )
        * dense_scale
    )
    own_rows = lax.dynamic_slice_in_dim(w_hidden[0], flow_place * share_rows, share_rows, 0)
    new_w_hidden = row_update(own_rows, grad_hidden)[None]
    grad_one, grad_two, grad_out = lax.psum((grad_one, grad_two, grad_out), STREAM)
    new_k_second = row_update(k_second[0], grad_two)
    new_k_first = row_update(k_first[0], grad_one)
    new_w_out = whole_update(w_out[0], grad_out)
    return (new_field, stress, new_k_first[None], new_k_second[None], new_w_hidden, new_w_out[None])


def solution(mesh):
    torus = Mesh(
        mesh.devices.reshape(mesh.shape["wall"], 8, 2, 2),
        ("wall", "stream_0", "stream_1", "stream_2"),
    )
    in_specs = (
        P(None, "wall", STREAM, None),
        P("wall", STREAM),
        P("wall", STREAM, None),
        P("wall", None, None),
        P("wall", None, None, None),
        P("wall", None, None),
        P("wall", None, None),
    )
    out_specs = (
        P(None, "wall", STREAM, None),
        P(None, "wall", STREAM),
        P("wall", None, None),
        P("wall", None, None, None),
        P("wall", STREAM, None),
        P("wall", None, None),
    )
    return jax.shard_map(body, mesh=torus, in_specs=in_specs, out_specs=out_specs, check_vma=False)
```

profile of v0, /device:TPU:2, one launch (start us, length us, event | category | flops | bytes accessed | tf_op | source)
XLA Modules:
  0.0 358.0 jit_solution(1956748719228689826)
XLA Ops:
  8.8 1.5 collective-permute-start.2
  10.3 0.9 collective-permute-start.3
  11.2 1.6 fusion.46
  12.7 7.0 %collective-permute-start.1 = (f32[3,8,1,128]{3,2,1,0:T(1,128)S(1)}, f32[3,8,1,128]{3,2,1,0:T(1,128)}, u32[]{:S(2)}, u32[]{:S(2)}) collective-permute-start(f32[3,8,1,128]{3,2,1,0:T(1,128)S(1)} %get-tuple-element.93), channel_id=1, source_target_pairs={{1,0},{2,1},{3,2},{4,3},{5,4},{6,5},{7,6},{8,7},{9,8},{10,9},{11,1... | collective-permute-start | bytes 36872 | tf_op jit(solution)/shard_map/ppermute | solution.py:35
  21.1 0.9 fusion.44
  22.0 1.5 convolution_bitcast_fusion
  23.5 1.5 fusion.23
  24.9 1.5 convolution_bitcast_fusion.1
  27.1 0.8 select_reduce_fusion
  28.7 1.2 reshape.297
  33.5 2.1 reshape.300
  36.6 0.9 convolution_convert_fusion.1
  38.3 5.9 %all-to-all-start = ((bf16[8,2,259]{2,1,0:T(2,128)(2,1)}), bf16[8,2,259]{2,1,0:T(2,128)(2,1)S(1)}, u32[]{:S(2)}, u32[]{:S(2)}) async-start(bf16[8,2,259]{2,1,0:T(2,128)(2,1)} %pad_maximum_fusion.2), calls=%async_computation | async-start | bytes 24576 | tf_op jit(solution)/shard_map/all_to_all | solution.py:51
  44.3 4.7 %all-to-all-done = bf16[8,2,259]{2,1,0:T(2,128)(2,1)S(1)} async-done(((bf16[8,2,259]{2,1,0:T(2,128)(2,1)}), bf16[8,2,259]{2,1,0:T(2,128)(2,1)S(1)}, u32[]{:S(2)}, u32[]{:S(2)}) %all-to-all-start) | async-done | bytes 8320 | tf_op jit(solution)/shard_map/all_to_all | solution.py:51
  49.3 0.9 convolution_multiply_fusion.4
  50.2 4.5 %fusion.14 = (f32[16,4,4,8,64]{4,0,3,2,1:T(8,128)}, f32[16,4,4,8,64]{4,0,3,2,1:T(8,128)}) fusion(bf16[3,3,3,64,64]{4,3,2,1,0:T(8,128)(2,1)} %bitcast.138, f32[16,4,4,8,64]{4,0,3,2,1:T(8,128)S(1)} %convolution_multiply_fusion.4), kind=kOutput, calls=%fused_computation.26 | convolution fusion | flops 289669120 | bytes 1794048 | tf_op jit(solution)/shard_map/conv_general_dilated | solution.py:131
  54.7 1.3 reduce_sum.75
  56.4 4.6 %multiply_convert_fusion.3 = (bf16[16,2048]{1,0:T(8,128)(2,1)S(1)}, f32[16,2048]{1,0:T(8,128)S(1)}) fusion(bf16[16,2048]{1,0:T(8,128)(2,1)S(1)} %convert_element_type.116, bf16[1,2048,2048]{2,1,0:T(8,128)(2,1)} %param.23), kind=kOutput, calls=%fused_computation.50 | convolution fusion | flops 134414336 | bytes 8650752 | tf_op jit(solution)/shard_map/dot_general | solution.py:160
  62.0 6.6 %all-gather = bf16[32,2048]{1,0:T(8,128)(2,1)} all-gather(bf16[16,2048]{1,0:T(8,128)(2,1)S(1)} %fusion.11), channel_id=2, replica_groups=mesh['wall'=8,'stream_0'=8,'stream_1'=2,'stream_2'=2] {'stream_1'}, dimensions={0}, use_global_device_ids=true | all-gather | bytes 196608 | tf_op jit(solution)/shard_map/all_gather | solution.py:65
  71.0 5.7 %fusion.8 = f32[16,2048]{1,0:T(8,128)S(1)} fusion(bf16[16,2048]{1,0:T(8,128)(2,1)S(1)} %fusion.11, bf16[1,2048,2048]{2,1,0:T(8,128)(2,1)} %param.23), kind=kOutput, calls=%fused_computation.9 | convolution fusion | flops 134250496 | bytes 8585216 | tf_op jit(solution)/shard_map/dot_general | solution.py:168
  77.6 3.6 %convolution_multiply_fusion.5 = f32[3,3,3,64,64]{4,3,2,1,0:T(8,128)} fusion(bf16[16,4,4,8,64]{4,0,3,2,1:T(8,128)(2,1)S(1)} %multiply_convert_fusion, f32[16,4,4,8,64]{4,0,3,2,1:T(8,128)S(1)} %convolution_multiply_fusion.4), kind=kOutput, calls=%fused_computation.16 | convolution fusion | flops 289124352 | bytes 1228800 | tf_op jit(solution)/shard_map/transpose | solution.py:142
  81.6 4.2 %convolution_multiply_fusion.6 = f32[3,3,3,2,64]{4,3,2,1,0:T(2,128)S(1)} fusion(bf16[16,2,4,4,8]{0,4,3,2,1:T(8,128)(2,1)S(1)} %bitcast.141, bf16[16,4,4,8,64]{4,0,3,2,1:T(8,128)(2,1)S(1)} %multiply_convert_fusion, bf16[3,3,3,64,64]{4,3,2,1,0:T(8,128)(2,1)S(1)} %bitcast.139, f32[16,4,4,8,64]{4,0,3,2,1:T(8,128)S(1)} %convolution_multiply_fusion.4), kind=kOutput, calls=%fused_computation.20 | convolution fusion | flops 298683776 | bytes 1029632 | tf_op jit(solution)/shard_map/transpose | solution.py:142
  85.8 19.4 %all-gather.6.cloned.1.call-done = bf16[16,16,2048]{2,1,0:T(8,128)(2,1)} async-done(((bf16[2,16,2048]{2,1,0:T(8,128)(2,1)}), bf16[16,16,2048]{2,1,0:T(8,128)(2,1)}) %all-gather.6.cloned.1.call-update) | async-done | bytes 1048592 | tf_op jit(solution)/shard_map/all_gather | solution.py:65
  106.2 5.7 %all-to-all-start.1 = ((f32[8,2,2]{1,2,0:T(2,128)}), f32[8,2,2]{1,2,0:T(2,128)S(1)}, u32[]{:S(2)}, u32[]{:S(2)}) async-start(f32[8,2,2]{1,2,0:T(2,128)} %copy.77), calls=%async_computation.1 | async-start | bytes 16384 | tf_op jit(solution)/shard_map/all_to_all | solution.py:255
  111.9 128.6 %all-reduce = (f32[54,64]{1,0:T(8,128)S(1)}, f32[2048,2]{0,1:T(2,128)S(1)}) all-reduce(f32[54,64]{1,0:T(8,128)S(1)} %reshape.304, f32[2048,2]{0,1:T(2,128)S(1)} %convolution_multiply_fusion.1), channel_id=1, replica_groups=mesh['wall'=8,'stream_0'=8,'stream_1'=2,'stream_2'=2] {'stream_0','strea..., use_global_device_ids=true, to_apply=%region_5.6 | all-reduce | flops 7552 | bytes 60416 | tf_op jit(solution)/shard_map/psum | solution.py:271
  244.1 4.5 %all-to-all-start.2 = ((bf16[32,2,512]{2,1,0:T(2,128)(2,1)}), bf16[32,2,512]{2,1,0:T(2,128)(2,1)S(1)}, u32[]{:S(2)}, u32[]{:S(2)}) async-start(bf16[32,2,512]{2,1,0:T(2,128)(2,1)} %reshape.333), calls=%async_computation.2 | async-start | bytes 131072 | tf_op jit(solution)/shard_map/all_to_all | solution.py:260
  249.4 9.1 %all-to-all-done.2 = bf16[32,2,512]{2,1,0:T(2,128)(2,1)S(1)} async-done(((bf16[32,2,512]{2,1,0:T(2,128)(2,1)}), bf16[32,2,512]{2,1,0:T(2,128)(2,1)S(1)}, u32[]{:S(2)}, u32[]{:S(2)}) %all-to-all-start.2) | async-done | bytes 65568 | tf_op jit(solution)/shard_map/all_to_all | solution.py:260
  258.7 83.8 %all-reduce.3.cloned.1.call-done = f32[27,64,64]{2,1,0:T(8,128)} async-done(((f32[27,64,64]{2,1,0:T(8,128)}), f32[27,64,64]{2,1,0:T(8,128)}) %all-reduce.3.cloned.1.call-update) | async-done | bytes 442384 | tf_op jit(solution)/shard_map/psum | solution.py:271
  342.5 1.5 multiply_reduce_fusion
  344.0 2.4 fusion.15
  346.3 1.7 copy.82
  348.7 1.9 fusion.16
  (120 shorter events, 19.3 us)
Async XLA Ops:
  8.0 36.2 %copy-start = (f32[3,8,16,128]{3,2,1,0:T(8,128)S(1)}, f32[3,8,16,128]{3,2,1,0:T(8,128)}, u32[]{:S(2)}) copy-start(f32[3,8,16,128]{3,2,1,0:T(8,128)} %param.18) | copy-start | bytes 589828
  8.0 36.2 %copy-start.9 = (bf16[1,54,64]{2,1,0:T(8,128)(2,1)S(1)}, bf16[1,54,64]{2,1,0:T(8,128)(2,1)}, u32[]{:S(2)}) copy-start(bf16[1,54,64]{2,1,0:T(8,128)(2,1)} %param.21) | copy-start | bytes 20740
  8.8 23.3 %collective-permute-start.2 = (f32[3,1,16,128]{3,2,1,0:T(8,128)S(1)}, f32[3,1,16,128]{3,2,1,0:T(8,128)S(1)}, u32[]{:S(2)}, u32[]{:S(2)}) collective-permute-start(f32[3,1,16,128]{3,2,1,0:T(8,128)S(1)} %get-tuple-element.96), channel_id=1, source_target_pairs={{0,32},{32,64},{64,96},{96,128},{128,160},{160,192},{192,224},{224... | collective-permute-start | bytes 73736 | tf_op jit(solution)/shard_map/ppermute | solution.py:34
  10.3 21.8 %collective-permute-start.3 = (f32[3,1,16,128]{3,2,1,0:T(8,128)S(1)}, f32[3,1,16,128]{3,2,1,0:T(8,128)S(1)}, u32[]{:S(2)}, u32[]{:S(2)}) collective-permute-start(f32[3,1,16,128]{3,2,1,0:T(8,128)S(1)} %get-tuple-element.95), channel_id=1, source_target_pairs={{32,0},{64,32},{96,64},{128,96},{160,128},{192,160},{224,192},{0,2... | collective-permute-start | bytes 73736 | tf_op jit(solution)/shard_map/ppermute | solution.py:35
  12.7 55.9 %collective-permute-start = (f32[3,8,1,128]{3,2,1,0:T(1,128)}, f32[3,8,1,128]{3,2,1,0:T(1,128)}, u32[]{:S(2)}, u32[]{:S(2)}) collective-permute-start(f32[3,8,1,128]{3,2,1,0:T(1,128)} %get-tuple-element.94), channel_id=1, source_target_pairs={{0,1},{1,2},{2,3},{3,4},{4,5},{5,6},{6,7},{7,8},{8,9},{9,10},{10,1... | collective-permute-start | bytes 36872 | tf_op jit(solution)/shard_map/ppermute | solution.py:34
  12.7 56.7 %collective-permute-start.1 = (f32[3,8,1,128]{3,2,1,0:T(1,128)S(1)}, f32[3,8,1,128]{3,2,1,0:T(1,128)}, u32[]{:S(2)}, u32[]{:S(2)}) collective-permute-start(f32[3,8,1,128]{3,2,1,0:T(1,128)S(1)} %get-tuple-element.93), channel_id=1, source_target_pairs={{1,0},{2,1},{3,2},{4,3},{5,4},{6,5},{7,6},{8,7},{9,8},{10,9},{11,1... | collective-permute-start | bytes 36872 | tf_op jit(solution)/shard_map/ppermute | solution.py:35
  21.1 10.4 %copy-start.18 = (pred[8]{0:T(512)(128)(4,1)}, pred[8]{0:T(512)(128)(4,1)S(1)}, u32[]{:S(2)}) copy-start(pred[8]{0:T(512)(128)(4,1)S(1)} %compare_and_fusion) | copy-start | bytes 28
  28.6 26.1 %copy-start.16 = (s32[8]{0:T(128)}, s32[8]{0:T(128)S(1)}, u32[]{:S(2)}) copy-start(s32[8]{0:T(128)S(1)} %multiply_add_fusion) | copy-start | bytes 100
  32.2 0.7 copy-start.1
  38.3 10.7 %all-to-all-start = ((bf16[8,2,259]{2,1,0:T(2,128)(2,1)}), bf16[8,2,259]{2,1,0:T(2,128)(2,1)S(1)}, u32[]{:S(2)}, u32[]{:S(2)}) async-start(bf16[8,2,259]{2,1,0:T(2,128)(2,1)} %pad_maximum_fusion.2), calls=%async_computation | async-start | bytes 24576 | tf_op jit(solution)/shard_map/all_to_all | solution.py:51
  44.2 61.1 %all-gather.6.cloned.1.call-start = ((), (), s32[]{:S(2)}) async-start(), calls=%async_computation.4 | async-start | bytes 1179648 | tf_op jit(solution)/shard_map/all_gather | solution.py:65
  49.2 12.5 %copy-start.12 = (f32[16]{0:T(128)}, f32[16]{0:T(128)S(1)}, u32[]{:S(2)}) copy-start(f32[16]{0:T(128)S(1)} %convert_reduce_fusion) | copy-start | bytes 196
  49.3 5.4 %copy-start.7 = (bf16[16,256]{0,1:T(8,128)(2,1)}, bf16[16,256]{0,1:T(8,128)(2,1)S(1)}, u32[]{:S(2)}) copy-start(bf16[16,256]{0,1:T(8,128)(2,1)S(1)} %copy.74) | copy-start | bytes 24580
  56.0 5.0 %copy-start.10 = (bf16[1,2048,2]{1,2,0:T(2,128)(2,1)S(1)}, bf16[1,2048,2]{1,2,0:T(2,128)(2,1)}, u32[]{:S(2)}) copy-start(bf16[1,2048,2]{1,2,0:T(2,128)(2,1)} %param.24) | copy-start | bytes 24580
  56.4 5.6 %copy-start.14 = (bf16[16,2]{0,1:T(2,128)(2,1)}, bf16[16,2]{0,1:T(2,128)(2,1)S(1)}, u32[]{:S(2)}) copy-start(bf16[16,2]{0,1:T(2,128)(2,1)S(1)} %copy.88) | copy-start | bytes 196
  56.4 13.8 %copy-start.2 = (f32[3,8,16,128]{3,2,1,0:T(8,128)S(1)}, f32[3,8,16,128]{3,2,1,0:T(8,128)}, u32[]{:S(2)}) copy-start(f32[3,8,16,128]{3,2,1,0:T(8,128)} %copy-done.1) | copy-start | bytes 589828
  61.0 0.6 copy-start.5
  68.5 273.9 %all-reduce.3.cloned.1.call-start = ((), (), s32[]{:S(2)}) async-start(), calls=%async_computation.3 | async-start | bytes 1769472 | tf_op jit(solution)/shard_map/psum | solution.py:271
  71.0 6.1 %copy-start.3 = (f32[16,4,4,8,64]{4,0,3,2,1:T(8,128)S(1)}, f32[16,4,4,8,64]{4,0,3,2,1:T(8,128)}, u32[]{:S(2)}) copy-start(f32[16,4,4,8,64]{4,0,3,2,1:T(8,128)} %get-tuple-element.98) | copy-start | bytes 1572868
  77.2 4.4 %copy-start.4 = (bf16[1,27,64,64]{3,2,1,0:T(8,128)(2,1)S(1)}, bf16[1,27,64,64]{3,2,1,0:T(8,128)(2,1)}, u32[]{:S(2)}) copy-start(bf16[1,27,64,64]{3,2,1,0:T(8,128)(2,1)} %param.22) | copy-start | bytes 663556
  77.2 4.4 %copy-start.8 = (bf16[16,256]{0,1:T(8,128)(2,1)S(1)}, bf16[16,256]{0,1:T(8,128)(2,1)}, u32[]{:S(2)}) copy-start(bf16[16,256]{0,1:T(8,128)(2,1)} %copy-done.7) | copy-start | bytes 24580
  81.2 24.1 %copy-start.6 = (bf16[16,2048]{1,0:T(8,128)(2,1)S(1)}, bf16[16,2048]{1,0:T(8,128)(2,1)}, u32[]{:S(2)}) copy-start(bf16[16,2048]{1,0:T(8,128)(2,1)} %copy-done.5) | copy-start | bytes 196612
  81.2 24.1 %copy-start.13 = (f32[16]{0:T(128)S(1)}, f32[16]{0:T(128)}, u32[]{:S(2)}) copy-start(f32[16]{0:T(128)} %copy-done.12) | copy-start | bytes 196
  81.3 24.0 %copy-start.15 = (bf16[16,2]{0,1:T(2,128)(2,1)S(1)}, bf16[16,2]{0,1:T(2,128)(2,1)}, u32[]{:S(2)}) copy-start(bf16[16,2]{0,1:T(2,128)(2,1)} %copy-done.14) | copy-start | bytes 196
  81.3 161.4 %copy-start.11 = (bf16[1,2048,2]{1,2,0:T(2,128)(2,1)S(1)}, bf16[1,2048,2]{1,2,0:T(2,128)(2,1)}, u32[]{:S(2)}) copy-start(bf16[1,2048,2]{1,2,0:T(2,128)(2,1)} %param.24) | copy-start | bytes 24580
  81.3 167.4 %copy-start.17 = (s32[8]{0:T(128)S(1)}, s32[8]{0:T(128)}, u32[]{:S(2)}) copy-start(s32[8]{0:T(128)} %copy-done.16) | copy-start | bytes 100
  81.3 265.0 %all-gather.8.cloned.1.call-start = ((), (), s32[]{:S(2)}) async-start(), calls=%async_computation.5 | async-start | bytes 3145728 | tf_op jit(solution)/shard_map/all_gather | solution.py:65
  106.2 137.9 %all-to-all-start.1 = ((f32[8,2,2]{1,2,0:T(2,128)}), f32[8,2,2]{1,2,0:T(2,128)S(1)}, u32[]{:S(2)}, u32[]{:S(2)}) async-start(f32[8,2,2]{1,2,0:T(2,128)} %copy.77), calls=%async_computation.1 | async-start | bytes 16384 | tf_op jit(solution)/shard_map/all_to_all | solution.py:255
  244.1 14.4 %all-to-all-start.2 = ((bf16[32,2,512]{2,1,0:T(2,128)(2,1)}), bf16[32,2,512]{2,1,0:T(2,128)(2,1)S(1)}, u32[]{:S(2)}, u32[]{:S(2)}) async-start(bf16[32,2,512]{2,1,0:T(2,128)(2,1)} %reshape.333), calls=%async_computation.2 | async-start | bytes 131072 | tf_op jit(solution)/shard_map/all_to_all | solution.py:260
Sparse Core Ops, SparseCore 0:
  68.7 36.5 all-gather.5
  107.2 14.2 all-gather.7
Sparse Core Ops, SparseCore 1:
  81.3 261.1 all-reduce.2
where the time goes:
time: 360 us; the launch traced here: 358 us
  blocking collectives  135 us (38%)
  waiting for transfers between devices  117 us (32%)
  matrix products  31 us (9%)
  starting transfers between devices  25.8 us (7%)
  between operations  16.8 us (5%)
  other arithmetic  16.6 us (5%)
  local copies, waits for them, and re-layouts  15.5 us (4%)
    psum x1, blocking collectives, body(): lax.psum((grad_one, grad_two, grad_out), STREAM)  129 us
    psum x1, waiting for transfers between devices, body(): lax.psum((grad_one, grad_two, grad_out), STREAM)  83.8 us
    all_gather x2, waiting for transfers between devices, gather_in_order(): tiles = lax.all_gather(tiles, axes[k])  19.4 us
    all_to_all x1, waiting for transfers between devices, body(): lax.all_to_all(features, STREAM, split_axis=1, concat_axis=0, tiled=True)  9.09 us
    ppermute x2, starting transfers between devices, extended(): lax.ppermute(first, axis, [(b, a) for a, b in up])  7.9 us
    transpose x2, matrix products, conv_filter(): return jnp.moveaxis(taps, 0, 3)  7.84 us
  transfers between devices with their start and end apart: 10, of which 4 were waited for; matrix products, arithmetic and copies ran while one was open for 16% of the time, Pallas kernels for 0%

commit v1 on v0

--- a/solution.py
+++ b/solution.py
@@ -71,6 +71,24 @@
 
 def gathered_by_axis(shard, axes, order, dim):
     return joined_along(gather_in_order(shard, axes, order), dim)
+
+
+def from_everyone(shard, axis):
+    copies = jnp.broadcast_to(shard, (lax.axis_size(axis), *shard.shape))
+    return lax.all_to_all(copies, axis, split_axis=0, concat_axis=0, tiled=True)
+
+
+def collect(shard, axis, dim):
+    return joined_along(from_everyone(shard, axis), dim)
+
+
+def summed_and_owned(whole, shared, axis):
+    count = lax.axis_size(axis)
+    copies = jnp.broadcast_to(whole.ravel(), (count, whole.size))
+    tiles = shared.reshape(count, -1)
+    both = jnp.concatenate([copies, tiles], axis=1)
+    arrived = lax.all_to_all(both, axis, split_axis=0, concat_axis=0, tiled=True).sum(axis=0)
+    return arrived[: whole.size].reshape(whole.shape), arrived[whole.size :].reshape(-1, shared.shape[-1])
 
 
 def cheb_tables(points):
@@ -268,8 +286,16 @@
     )
     own_rows = lax.dynamic_slice_in_dim(w_hidden[0], flow_place * share_rows, share_rows, 0)
     new_w_hidden = row_update(own_rows, grad_hidden)[None]
-    grad_one, grad_two, grad_out = lax.psum((grad_one, grad_two, grad_out), STREAM)
-    new_k_second = row_update(k_second[0], grad_two)
+    small = jnp.concatenate([grad_one.ravel(), grad_out.ravel()])
+    small, grad_share = summed_and_owned(small, grad_two.reshape(-1, CH), STREAM)
+    grad_one = small[: grad_one.size].reshape(grad_one.shape)
+    grad_out = small[grad_one.size :].reshape(grad_out.shape)
+    share_count = grad_share.shape[0]
+    kernel_own = lax.dynamic_slice_in_dim(
+        k_second[0].reshape(-1, CH), flow_place * share_count, share_count, 0
+    )
+    updated_rows = row_update(kernel_own, grad_share)
+    new_k_second = collect(updated_rows, STREAM, 0).reshape(k_second.shape[1:])
     new_k_first = row_update(k_first[0], grad_one)
     new_w_out = whole_update(w_out[0], grad_out)
     return (new_field, stress, new_k_first[None], new_k_second[None], new_w_hidden, new_w_out[None])

time: 360 us -> 199 us (0.55)
  blocking collectives: 135 us -> 7.63 us
  waiting for transfers between devices: 117 us -> 60.7 us
  starting transfers between devices: 25.8 us -> 40.5 us
  local copies, waits for them, and re-layouts: 15.5 us -> 27 us
    psum x1 -> x0, blocking collectives: 129 us -> none  [body(): lax.psum((grad_one, grad_two, grad_out), STREAM)]
    psum x1 -> x0, waiting for transfers between devices: 83.8 us -> none  [body(): lax.psum((grad_one, grad_two, grad_out), STREAM)]
    ppermute x2, waiting for transfers between devices: 0.01 us -> 20.5 us  [extended(): lax.ppermute(last, axis, up)]
    all_to_all x0 -> x2, waiting for transfers between devices: none -> 14 us  [the longest x1 14 us: from_everyone(): return lax.all_to_all(copies, axis, split_axis=0, concat_axis=0, tiled=True)]
    all_to_all x0 -> x2, starting transfers between devices: none -> 10.9 us  [the longest x1 6.98 us: from_everyone(): return lax.all_to_all(copies, axis, split_axis=0, concat_axis=0, tiled=True)]
    all_gather x2, waiting for transfers between devices: 19.4 us -> 9.56 us  [gather_in_order(): tiles = lax.all_gather(tiles, axes[k])]
    all_to_all x1, starting transfers between devices: 4.49 us -> 9.75 us  [body(): lax.all_to_all(features, STREAM, split_axis=1, concat_axis=0, tiled=True)]
    unnamed x41 -> x29, local copies, waits for them, and re-layouts: 2.22 us -> 6.51 us
  transfers between devices with their start and end apart: 10 -> 11, of which waited for: 4 -> 6; matrix products, arithmetic and copies ran while one was open for 16% -> 17% of each run, Pallas kernels for 0% -> 0%
where the time goes in v1:
time: 199 us; the launch traced here: 197 us
  waiting for transfers between devices  60.7 us (31%)
  starting transfers between devices  40.5 us (20%)
  matrix products  29.2 us (15%)
  local copies, waits for them, and re-layouts  27 us (14%)
  other arithmetic  17 us (9%)
  between operations  15.3 us (8%)
  blocking collectives  7.63 us (4%)
    ppermute x2, waiting for transfers between devices, extended(): lax.ppermute(last, axis, up)  20.5 us
    all_to_all x1, waiting for transfers between devices, from_everyone(): return lax.all_to_all(copies, axis, split_axis=0, concat_axis=0, tiled=True)  14 us
    all_to_all x1, starting transfers between devices, body(): lax.all_to_all(features, STREAM, split_axis=1, concat_axis=0, tiled=True)  9.75 us
    all_gather x2, waiting for transfers between devices, gather_in_order(): tiles = lax.all_gather(tiles, axes[k])  9.56 us
    transpose x2, matrix products, conv_filter(): return jnp.moveaxis(taps, 0, 3)  8.06 us
    all_to_all x1, waiting for transfers between devices, body(): lax.all_to_all(features, STREAM, split_axis=1, concat_axis=0, tiled=True)  7.82 us
    all_gather x1, blocking collectives, gather_in_order(): tiles = lax.all_gather(tiles, axes[k])  7.63 us
    all_to_all x1, starting transfers between devices, in_one_piece(): lax.all_to_all(both, axis, split_axis=split_dim, concat_axis=concat_dim,...  7.31 us
  transfers between devices with their start and end apart: 11, of which 6 were waited for; matrix products, arithmetic and copies ran while one was open for 17% of the time, Pallas kernels for 0%

profile of v1, /device:TPU:2, one launch (start us, length us, event | category | flops | bytes accessed | tf_op | source)
XLA Modules:
  0.0 197.3 jit_solution(14930817695358404019)
XLA Ops:
  7.9 1.5 collective-permute-start.2
  12.5 1.5 fusion.22
  16.2 1.2 reshape.365
  19.8 1.1 reshape.368
  22.9 7.3 %all-to-all-start = ((bf16[8,2,259]{2,1,0:T(2,128)(2,1)}), bf16[8,2,259]{2,1,0:T(2,128)(2,1)S(1)}, u32[]{:S(2)}, u32[]{:S(2)}) async-start(bf16[8,2,259]{2,1,0:T(2,128)(2,1)} %pad_maximum_fusion.4), calls=%async_computation | async-start | bytes 24576 | tf_op jit(solution)/shard_map/all_to_all | solution.py:51
  30.2 4.8 %all-to-all-done = bf16[8,2,259]{2,1,0:T(2,128)(2,1)S(1)} async-done(((bf16[8,2,259]{2,1,0:T(2,128)(2,1)}), bf16[8,2,259]{2,1,0:T(2,128)(2,1)S(1)}, u32[]{:S(2)}, u32[]{:S(2)}) %all-to-all-start) | async-done | bytes 8320 | tf_op jit(solution)/shard_map/all_to_all | solution.py:51
  36.3 4.5 %fusion.14 = (f32[16,4,4,8,64]{4,0,3,2,1:T(8,128)}, f32[16,4,4,8,64]{4,0,3,2,1:T(8,128)}) fusion(bf16[3,3,3,64,64]{4,3,2,1,0:T(8,128)(2,1)} %bitcast.139, f32[16,4,4,8,64]{4,0,3,2,1:T(8,128)S(1)} %convolution_multiply_fusion.4), kind=kOutput, calls=%fused_computation.28 | convolution fusion | flops 289669120 | bytes 1794048 | tf_op jit(solution)/shard_map/conv_general_dilated | solution.py:149
  40.7 1.3 reduce_sum.84
  42.4 4.6 %multiply_convert_fusion.3 = (bf16[16,2048]{1,0:T(8,128)(2,1)S(1)}, f32[16,2048]{1,0:T(8,128)S(1)}) fusion(bf16[16,2048]{1,0:T(8,128)(2,1)S(1)} %convert_element_type.111, bf16[1,2048,2048]{2,1,0:T(8,128)(2,1)} %param.23), kind=kOutput, calls=%fused_computation.49 | convolution fusion | flops 134414336 | bytes 8650752 | tf_op jit(solution)/shard_map/dot_general | solution.py:178
  47.6 5.6 %fusion.8 = f32[16,2048]{1,0:T(8,128)S(1)} fusion(bf16[16,2048]{1,0:T(8,128)(2,1)S(1)} %fusion.11, bf16[1,2048,2048]{2,1,0:T(8,128)(2,1)} %param.23), kind=kOutput, calls=%fused_computation.9 | convolution fusion | flops 134250496 | bytes 8585216 | tf_op jit(solution)/shard_map/dot_general | solution.py:186
  55.1 4.2 %convolution_multiply_fusion.6 = f32[3,3,3,2,64]{4,3,2,1,0:T(2,128)S(1)} fusion(bf16[16,2,4,4,8]{0,4,3,2,1:T(8,128)(2,1)S(1)} %bitcast.134, bf16[16,4,4,8,64]{4,0,3,2,1:T(8,128)(2,1)S(1)} %multiply_convert_fusion, bf16[3,3,3,64,64]{4,3,2,1,0:T(8,128)(2,1)S(1)} %bitcast.141, f32[16,4,4,8,64]{4,0,3,2,1:T(8,128)S(1)} %convolution_multiply_fusion.4), kind=kOutput, calls=%fused_computation.21 | convolution fusion | flops 298683776 | bytes 1029632 | tf_op jit(solution)/shard_map/transpose | solution.py:160
  59.3 3.8 %convolution_multiply_fusion.5 = f32[3,3,3,64,64]{4,3,2,1,0:T(8,128)} fusion(bf16[16,4,4,8,64]{4,0,3,2,1:T(8,128)(2,1)S(1)} %multiply_convert_fusion, f32[16,4,4,8,64]{4,0,3,2,1:T(8,128)S(1)} %convolution_multiply_fusion.4), kind=kOutput, calls=%fused_computation.17 | convolution fusion | flops 289124352 | bytes 1228800 | tf_op jit(solution)/shard_map/transpose | solution.py:160
  65.1 4.7 %all-to-all-start.1 = ((f32[8,2,2]{1,2,0:T(2,128)}), f32[8,2,2]{1,2,0:T(2,128)S(1)}, u32[]{:S(2)}, u32[]{:S(2)}) async-start(f32[8,2,2]{1,2,0:T(2,128)} %copy.91), calls=%async_computation.1 | async-start | bytes 16384 | tf_op jit(solution)/shard_map/all_to_all | solution.py:273
  70.6 4.0 %all-to-all-done.1 = f32[8,2,2]{1,2,0:T(2,128)S(1)} async-done(((f32[8,2,2]{1,2,0:T(2,128)}), f32[8,2,2]{1,2,0:T(2,128)S(1)}, u32[]{:S(2)}, u32[]{:S(2)}) %all-to-all-start.1) | async-done | bytes 160 | tf_op jit(solution)/shard_map/all_to_all | solution.py:273
  74.6 9.8 %all-to-all-start.4 = ((bf16[32,2,512]{2,1,0:T(2,128)(2,1)}), bf16[32,2,512]{2,1,0:T(2,128)(2,1)S(1)}, u32[]{:S(2)}, u32[]{:S(2)}) async-start(bf16[32,2,512]{2,1,0:T(2,128)(2,1)} %reshape.401), calls=%async_computation.4 | async-start | bytes 131072 | tf_op jit(solution)/shard_map/all_to_all | solution.py:278
  84.4 2.1 %all_to_all.40 = f32[32,1,11008]{2,1,0:T(1,128)} reshape(f32[32,11008]{1,0:T(8,128)S(1)} %pad_maximum_fusion) | data formatting | bytes 2818048 | tf_op jit(solution)/shard_map/all_to_all | solution.py:90
  86.5 7.8 %all-to-all-done.4 = bf16[32,2,512]{2,1,0:T(2,128)(2,1)S(1)} async-done(((bf16[32,2,512]{2,1,0:T(2,128)(2,1)}), bf16[32,2,512]{2,1,0:T(2,128)(2,1)S(1)}, u32[]{:S(2)}, u32[]{:S(2)}) %all-to-all-start.4) | async-done | bytes 65568 | tf_op jit(solution)/shard_map/all_to_all | solution.py:278
  94.3 4.0 %all-to-all-start.2 = ((f32[32,1,11008]{2,1,0:T(1,128)}), f32[32,1,11008]{2,1,0:T(1,128)S(1)}, u32[]{:S(2)}, u32[]{:S(2)}) async-start(f32[32,1,11008]{2,1,0:T(1,128)} %all_to_all.40), calls=%async_computation.2 | async-start | bytes 2818048 | tf_op jit(solution)/shard_map/all_to_all | solution.py:90
  98.3 7.6 %all-gather = bf16[32,2048]{1,0:T(8,128)(2,1)} all-gather(bf16[16,2048]{1,0:T(8,128)(2,1)S(1)} %fusion.11), channel_id=2, replica_groups=mesh['wall'=8,'stream_0'=8,'stream_1'=2,'stream_2'=2] {'stream_1'}, dimensions={0}, use_global_device_ids=true | all-gather | bytes 196608 | tf_op jit(solution)/shard_map/all_gather | solution.py:65
  106.2 5.3 %collective-permute-start.1 = (f32[3,8,1,128]{3,2,1,0:T(1,128)S(1)}, f32[3,8,1,128]{3,2,1,0:T(1,128)}, u32[]{:S(2)}, u32[]{:S(2)}) collective-permute-start(f32[3,8,1,128]{3,2,1,0:T(1,128)S(1)} %get-tuple-element.91), channel_id=1, source_target_pairs={{1,0},{2,1},{3,2},{4,3},{5,4},{6,5},{7,6},{8,7},{9,8},{10,9},{11,1... | collective-permute-start | bytes 36872 | tf_op jit(solution)/shard_map/ppermute | solution.py:35
  114.9 20.5 %collective-permute-done = f32[3,8,1,128]{3,2,1,0:T(1,128)} collective-permute-done((f32[3,8,1,128]{3,2,1,0:T(1,128)S(1)}, f32[3,8,1,128]{3,2,1,0:T(1,128)}, u32[]{:S(2)}, u32[]{:S(2)}) %collective-permute-start) | collective-permute-done | bytes 12320 | tf_op jit(solution)/shard_map/ppermute | solution.py:34
  136.2 1.6 scatter-add.14
  138.7 1.6 scatter-add.15
  140.3 1.8 fusion.19
  142.1 9.6 %all-gather.6.cloned.1.call-done = bf16[16,16,2048]{2,1,0:T(8,128)(2,1)} async-done(((bf16[2,16,2048]{2,1,0:T(8,128)(2,1)}), bf16[16,16,2048]{2,1,0:T(8,128)(2,1)}) %all-gather.6.cloned.1.call-update) | async-done | bytes 1048592 | tf_op jit(solution)/shard_map/all_gather | solution.py:65
  151.7 1.4 fusion.31
  158.4 1.3 reshape.399
  159.7 7.0 %all-to-all-start.3 = ((f32[32,1,3456]{2,1,0:T(1,128)}), f32[32,1,3456]{2,1,0:T(1,128)S(1)}, u32[]{:S(2)}, u32[]{:S(2)}) async-start(f32[32,1,3456]{2,1,0:T(1,128)} %reshape.399), calls=%async_computation.3 | async-start | bytes 884736 | tf_op jit(solution)/shard_map/all_to_all | solution.py:78
  168.8 14.0 %all-to-all-done.3 = f32[32,1,3456]{2,1,0:T(1,128)S(1)} async-done(((f32[32,1,3456]{2,1,0:T(1,128)}), f32[32,1,3456]{2,1,0:T(1,128)S(1)}, u32[]{:S(2)}, u32[]{:S(2)}) %all-to-all-start.3) | async-done | bytes 442400 | tf_op jit(solution)/shard_map/all_to_all | solution.py:78
  183.3 1.7 reduce.12
  186.2 1.7 copy.98
  188.6 1.9 fusion.15
  (126 shorter events, 31.3 us)
Async XLA Ops:
  7.9 11.7 %collective-permute-start.2 = (f32[3,1,16,128]{3,2,1,0:T(8,128)S(1)}, f32[3,1,16,128]{3,2,1,0:T(8,128)S(1)}, u32[]{:S(2)}, u32[]{:S(2)}) collective-permute-start(f32[3,1,16,128]{3,2,1,0:T(8,128)S(1)} %get-tuple-element.94), channel_id=1, source_target_pairs={{0,32},{32,64},{64,96},{96,128},{128,160},{160,192},{192,224},{224... | collective-permute-start | bytes 73736 | tf_op jit(solution)/shard_map/ppermute | solution.py:34
  9.4 10.3 %collective-permute-start.3 = (f32[3,1,16,128]{3,2,1,0:T(8,128)S(1)}, f32[3,1,16,128]{3,2,1,0:T(8,128)S(1)}, u32[]{:S(2)}, u32[]{:S(2)}) collective-permute-start(f32[3,1,16,128]{3,2,1,0:T(8,128)S(1)} %get-tuple-element.93), channel_id=1, source_target_pairs={{32,0},{64,32},{96,64},{128,96},{160,128},{192,160},{224,192},{0,2... | collective-permute-start | bytes 73736 | tf_op jit(solution)/shard_map/ppermute | solution.py:35
  16.2 5.6 %copy-start.10 = (s32[8]{0:T(128)}, s32[8]{0:T(128)S(1)}, u32[]{:S(2)}) copy-start(s32[8]{0:T(128)S(1)} %multiply_add_fusion) | copy-start | bytes 100
  19.7 10.4 %copy-start.6 = (bf16[1,54,64]{2,1,0:T(8,128)(2,1)S(1)}, bf16[1,54,64]{2,1,0:T(8,128)(2,1)}, u32[]{:S(2)}) copy-start(bf16[1,54,64]{2,1,0:T(8,128)(2,1)} %param.21) | copy-start | bytes 20740
  22.9 12.1 %all-to-all-start = ((bf16[8,2,259]{2,1,0:T(2,128)(2,1)}), bf16[8,2,259]{2,1,0:T(2,128)(2,1)S(1)}, u32[]{:S(2)}, u32[]{:S(2)}) async-start(bf16[8,2,259]{2,1,0:T(2,128)(2,1)} %pad_maximum_fusion.4), calls=%async_computation | async-start | bytes 24576 | tf_op jit(solution)/shard_map/all_to_all | solution.py:51
  35.0 5.7 %copy-start.5 = (bf16[16,259]{1,0:T(8,128)(2,1)}, bf16[16,259]{1,0:T(8,128)(2,1)S(1)}, u32[]{:S(2)}) copy-start(bf16[16,259]{1,0:T(8,128)(2,1)S(1)} %all_to_all.36) | copy-start | bytes 24868
  40.7 1.6 slice-start
  42.4 4.6 %copy-start.7 = (bf16[1,2048,2]{1,2,0:T(2,128)(2,1)S(1)}, bf16[1,2048,2]{1,2,0:T(2,128)(2,1)}, u32[]{:S(2)}) copy-start(bf16[1,2048,2]{1,2,0:T(2,128)(2,1)} %param.24) | copy-start | bytes 24580
  53.4 1.2 copy-start.1
  53.6 1.5 copy-start.9
  63.1 1.2 copy-start.2
  65.1 9.4 %all-to-all-start.1 = ((f32[8,2,2]{1,2,0:T(2,128)}), f32[8,2,2]{1,2,0:T(2,128)S(1)}, u32[]{:S(2)}, u32[]{:S(2)}) async-start(f32[8,2,2]{1,2,0:T(2,128)} %copy.91), calls=%async_computation.1 | async-start | bytes 16384 | tf_op jit(solution)/shard_map/all_to_all | solution.py:273
  74.6 19.7 %all-to-all-start.4 = ((bf16[32,2,512]{2,1,0:T(2,128)(2,1)}), bf16[32,2,512]{2,1,0:T(2,128)(2,1)S(1)}, u32[]{:S(2)}, u32[]{:S(2)}) async-start(bf16[32,2,512]{2,1,0:T(2,128)(2,1)} %reshape.401), calls=%async_computation.4 | async-start | bytes 131072 | tf_op jit(solution)/shard_map/all_to_all | solution.py:278
  86.5 19.5 %copy-start = (f32[3,8,16,128]{3,2,1,0:T(8,128)S(1)}, f32[3,8,16,128]{3,2,1,0:T(8,128)}, u32[]{:S(2)}) copy-start(f32[3,8,16,128]{3,2,1,0:T(8,128)} %param.18) | copy-start | bytes 589828
  86.5 25.0 %copy-start.8 = (f32[32,16,1,1]{0,1,3,2:T(8,128)S(1)}, f32[32,16,1,1]{0,1,3,2:T(8,128)}, u32[]{:S(2)}) copy-start(f32[32,16,1,1]{0,1,3,2:T(8,128)} %constant.249) | copy-start | bytes 6148
  86.5 25.5 %copy-start.4 = (f32[256,128,1,1]{1,0,3,2:T(8,128)S(1)}, f32[256,128,1,1]{1,0,3,2:T(8,128)}, u32[]{:S(2)}) copy-start(f32[256,128,1,1]{1,0,3,2:T(8,128)} %constant.251) | copy-start | bytes 393220
  94.3 17.2 %copy-start.3 = (bf16[32,2,512]{2,1,0:T(2,128)(2,1)}, bf16[32,2,512]{2,1,0:T(2,128)(2,1)S(1)}, u32[]{:S(2)}) copy-start(bf16[32,2,512]{2,1,0:T(2,128)(2,1)S(1)} %all-to-all-done.4) | copy-start | bytes 196612
  94.3 59.8 %all-to-all-start.2 = ((f32[32,1,11008]{2,1,0:T(1,128)}), f32[32,1,11008]{2,1,0:T(1,128)S(1)}, u32[]{:S(2)}, u32[]{:S(2)}) async-start(f32[32,1,11008]{2,1,0:T(1,128)} %all_to_all.40), calls=%async_computation.2 | async-start | bytes 2818048 | tf_op jit(solution)/shard_map/all_to_all | solution.py:90
  98.3 53.4 %all-gather.6.cloned.1.call-start = ((), (), s32[]{:S(2)}) async-start(), calls=%async_computation.5 | async-start | bytes 1179648 | tf_op jit(solution)/shard_map/all_gather | solution.py:65
  106.0 80.2 %all-gather.8.cloned.1.call-start = ((), (), s32[]{:S(2)}) async-start(), calls=%async_computation.6 | async-start | bytes 3145728 | tf_op jit(solution)/shard_map/all_gather | solution.py:65
  106.1 29.4 %collective-permute-start = (f32[3,8,1,128]{3,2,1,0:T(1,128)S(1)}, f32[3,8,1,128]{3,2,1,0:T(1,128)}, u32[]{:S(2)}, u32[]{:S(2)}) collective-permute-start(f32[3,8,1,128]{3,2,1,0:T(1,128)S(1)} %get-tuple-element.92), channel_id=1, source_target_pairs={{0,1},{1,2},{2,3},{3,4},{4,5},{5,6},{6,7},{7,8},{8,9},{9,10},{10,1... | collective-permute-start | bytes 36872 | tf_op jit(solution)/shard_map/ppermute | solution.py:34
  106.2 31.6 %collective-permute-start.1 = (f32[3,8,1,128]{3,2,1,0:T(1,128)S(1)}, f32[3,8,1,128]{3,2,1,0:T(1,128)}, u32[]{:S(2)}, u32[]{:S(2)}) collective-permute-start(f32[3,8,1,128]{3,2,1,0:T(1,128)S(1)} %get-tuple-element.91), channel_id=1, source_target_pairs={{1,0},{2,1},{3,2},{4,3},{5,4},{6,5},{7,6},{8,7},{9,8},{10,9},{11,1... | collective-permute-start | bytes 36872 | tf_op jit(solution)/shard_map/ppermute | solution.py:35
  159.7 23.0 %all-to-all-start.3 = ((f32[32,1,3456]{2,1,0:T(1,128)}), f32[32,1,3456]{2,1,0:T(1,128)S(1)}, u32[]{:S(2)}, u32[]{:S(2)}) async-start(f32[32,1,3456]{2,1,0:T(1,128)} %reshape.399), calls=%async_computation.3 | async-start | bytes 884736 | tf_op jit(solution)/shard_map/all_to_all | solution.py:78
Sparse Core Ops, SparseCore 0:
  106.1 45.5 all-gather.5
  153.5 13.8 all-gather.7

commit v2 on v1

--- a/solution.py
+++ b/solution.py
@@ -59,20 +59,6 @@
     return jnp.moveaxis(tiles, 0, dim).reshape(lengths)
 
 
-def gather_in_order(shard, axes, order):
-    tiles = shard
-    for k in order:
-        tiles = lax.all_gather(tiles, axes[k])
-    done = order[::-1]
-    back = [done.index(k) for k in range(len(axes))]
-    tiles = tiles.transpose(*back, *range(len(axes), tiles.ndim))
-    return tiles.reshape(-1, *shard.shape)
-
-
-def gathered_by_axis(shard, axes, order, dim):
-    return joined_along(gather_in_order(shard, axes, order), dim)
-
-
 def from_everyone(shard, axis):
     copies = jnp.broadcast_to(shard, (lax.axis_size(axis), *shard.shape))
     return lax.all_to_all(copies, axis, split_axis=0, concat_axis=0, tiled=True)
@@ -89,6 +75,17 @@
     both = jnp.concatenate([copies, tiles], axis=1)
     arrived = lax.all_to_all(both, axis, split_axis=0, concat_axis=0, tiled=True).sum(axis=0)
     return arrived[: whole.size].reshape(whole.shape), arrived[whole.size :].reshape(-1, shared.shape[-1])
+
+
+def dense_inputs(features, delta, axis):
+    count = lax.axis_size(axis)
+    batch, width = features.shape
+    tiles = features.reshape(batch, count, width // count).transpose(1, 0, 2)
+    copies = jnp.broadcast_to(delta, (count, *delta.shape))
+    both = jnp.concatenate([tiles, copies], axis=2)
+    arrived = lax.all_to_all(both, axis, split_axis=0, concat_axis=0, tiled=True)
+    arrived = arrived.reshape(count * batch, -1)
+    return arrived[:, : width // count], arrived[:, width // count :]
 
 
 def cheb_tables(points):
@@ -275,14 +272,9 @@
     stress = stress_local.T[:, None, :]
     share_rows = FEATS // flow_count
     dense_scale = 1.0 / math.sqrt(1.0 * FEATS)
-    columns_here = lax.all_to_all(features, STREAM, split_axis=1, concat_axis=0, tiled=True)
+    columns_here, delta_all = dense_inputs(features, delta_three, STREAM)
     grad_hidden = (
-        jnp.dot(
-            columns_here.T,
-            gathered_by_axis(delta_three, STREAM, (1, 0, 2), 0),
-            preferred_element_type=jnp.float32,
-        )
-        * dense_scale
+        jnp.dot(columns_here.T, delta_all, preferred_element_type=jnp.float32) * dense_scale
     )
     own_rows = lax.dynamic_slice_in_dim(w_hidden[0], flow_place * share_rows, share_rows, 0)
     new_w_hidden = row_update(own_rows, grad_hidden)[None]

time: 199 us -> 223 us (1.12)
  waiting for transfers between devices: 60.7 us -> 94.7 us
  between operations: 15.3 us -> 1.77 us
  blocking collectives: 7.63 us -> 0 us
  other arithmetic: 17 us -> 24.2 us
  matrix products: 29.2 us -> 31.6 us
    all_to_all x1, waiting for transfers between devices: 0.01 us -> 35.4 us  [summed_and_owned(): lax.all_to_all(both, axis, split_axis=0, concat_axis=0, tiled=True)]
    ppermute x2, waiting for transfers between devices: 20.5 us -> 39.5 us  [extended(): lax.ppermute(last, axis, up)]
    all_gather x2 -> x0, waiting for transfers between devices: 9.56 us -> none  [gather_in_order(): tiles = lax.all_gather(tiles, axes[k])]
    all_to_all x1, waiting for transfers between devices: 7.82 us -> 0.01 us  [dense_inputs(): lax.all_to_all(both, axis, split_axis=0, concat_axis=0, tiled=True)]
    all_gather x1 -> x0, blocking collectives: 7.63 us -> none  [gather_in_order(): tiles = lax.all_gather(tiles, axes[k])]
    all_to_all x1, starting transfers between devices: 3.96 us -> 9.75 us  [summed_and_owned(): lax.all_to_all(both, axis, split_axis=0, concat_axis=0, tiled=True)]
    all_to_all x1, starting transfers between devices: 9.75 us -> 4.64 us  [dense_inputs(): lax.all_to_all(both, axis, split_axis=0, concat_axis=0, tiled=True)]
    concatenate x0 -> x1, other arithmetic: none -> 2.53 us  [dense_inputs(): both = jnp.concatenate([tiles, copies], axis=2)]
  transfers between devices with their start and end apart: 11 -> 9, of which waited for: 6 -> 5; matrix products, arithmetic and copies ran while one was open for 17% -> 20% of each run, Pallas kernels for 0% -> 0%
where the time goes in v2:
time: 223 us; the launch traced here: 220 us
  waiting for transfers between devices  94.7 us (42%)
  starting transfers between devices  39.6 us (18%)
  matrix products  31.6 us (14%)
  local copies, waits for them, and re-layouts  28.6 us (13%)
  other arithmetic  24.2 us (11%)
    ppermute x2, waiting for transfers between devices, extended(): lax.ppermute(last, axis, up)  39.5 us
    all_to_all x1, waiting for transfers between devices, summed_and_owned(): lax.all_to_all(both, axis, split_axis=0, concat_axis=0, tiled=True)  35.4 us
    all_to_all x1, waiting for transfers between devices, from_everyone(): return lax.all_to_all(copies, axis, split_axis=0, concat_axis=0, tiled=True)  13.5 us
    all_to_all x1, starting transfers between devices, summed_and_owned(): lax.all_to_all(both, axis, split_axis=0, concat_axis=0, tiled=True)  9.75 us
    transpose x2, matrix products, conv_filter(): return jnp.moveaxis(taps, 0, 3)  9.37 us
    unnamed x21, local copies, waits for them, and re-layouts  8.23 us
    all_to_all x1, starting transfers between devices, in_one_piece(): lax.all_to_all(both, axis, split_axis=split_dim, concat_axis=concat_dim,...  7.31 us
    ppermute x2, starting transfers between devices, extended(): lax.ppermute(first, axis, [(b, a) for a, b in up])  5.93 us
  transfers between devices with their start and end apart: 9, of which 5 were waited for; matrix products, arithmetic and copies ran while one was open for 20% of the time, Pallas kernels for 0%

profile of v2, /device:TPU:2, one launch (start us, length us, event | category | flops | bytes accessed | tf_op | source)
XLA Modules:
  0.0 220.5 jit_solution(9765204038398202520)
XLA Ops:
  1.4 1.5 collective-permute-start.2
  5.9 1.5 fusion.24
  16.3 7.3 %all-to-all-start = ((bf16[8,2,259]{2,1,0:T(2,128)(2,1)}), bf16[8,2,259]{2,1,0:T(2,128)(2,1)S(1)}, u32[]{:S(2)}, u32[]{:S(2)}) async-start(bf16[8,2,259]{2,1,0:T(2,128)(2,1)} %pad_maximum_fusion.5), calls=%async_computation | async-start | bytes 24576 | tf_op jit(solution)/shard_map/all_to_all | solution.py:51
  23.7 4.8 %all-to-all-done = bf16[8,2,259]{2,1,0:T(2,128)(2,1)S(1)} async-done(((bf16[8,2,259]{2,1,0:T(2,128)(2,1)}), bf16[8,2,259]{2,1,0:T(2,128)(2,1)S(1)}, u32[]{:S(2)}, u32[]{:S(2)}) %all-to-all-start) | async-done | bytes 8320 | tf_op jit(solution)/shard_map/all_to_all | solution.py:51
  29.7 4.1 %fusion.16 = (f32[16,4,4,8,64]{4,0,3,2,1:T(8,128)S(1)}, f32[16,4,4,8,64]{4,0,3,2,1:T(8,128)}) fusion(bf16[3,3,3,64,64]{4,3,2,1,0:T(8,128)(2,1)} %bitcast.125, f32[16,4,4,8,64]{4,0,3,2,1:T(8,128)S(1)} %convolution_multiply_fusion.4), kind=kOutput, calls=%fused_computation.31 | convolution fusion | flops 289669120 | bytes 1794048 | tf_op jit(solution)/shard_map/conv_general_dilated | solution.py:146
  34.3 4.6 %multiply_convert_fusion.3 = (bf16[16,2048]{1,0:T(8,128)(2,1)S(1)}, f32[16,2048]{1,0:T(8,128)S(1)}) fusion(bf16[16,2048]{1,0:T(8,128)(2,1)S(1)} %convert_element_type.111, bf16[1,2048,2048]{2,1,0:T(8,128)(2,1)} %param.23), kind=kOutput, calls=%fused_computation.53 | convolution fusion | flops 134414336 | bytes 8650752 | tf_op jit(solution)/shard_map/dot_general | solution.py:175
  39.5 5.6 %fusion.8 = f32[16,2048]{1,0:T(8,128)S(1)} fusion(bf16[16,2048]{1,0:T(8,128)(2,1)S(1)} %fusion.11, bf16[1,2048,2048]{2,1,0:T(8,128)(2,1)} %param.23), kind=kOutput, calls=%fused_computation.9 | convolution fusion | flops 134250496 | bytes 8585216 | tf_op jit(solution)/shard_map/dot_general | solution.py:183
  47.6 5.4 %convolution_multiply_fusion.6 = f32[3,3,3,2,64]{4,3,2,1,0:T(2,128)S(1)} fusion(bf16[16,2,4,4,8]{0,4,3,2,1:T(8,128)(2,1)S(1)} %bitcast.120, bf16[16,4,4,8,64]{4,0,3,2,1:T(8,128)(2,1)} %multiply_convert_fusion, bf16[3,3,3,64,64]{4,3,2,1,0:T(8,128)(2,1)} %bitcast.126, f32[16,4,4,8,64]{4,0,3,2,1:T(8,128)S(1)} %convolution_multiply_fusion.4), kind=kOutput, calls=%fused_computation.24 | convolution fusion | flops 298683776 | bytes 1029632 | tf_op jit(solution)/shard_map/transpose | solution.py:157
  53.0 4.0 %convolution_multiply_fusion.5 = f32[3,3,3,64,64]{4,3,2,1,0:T(8,128)S(1)} fusion(bf16[16,4,4,8,64]{4,0,3,2,1:T(8,128)(2,1)} %multiply_convert_fusion, f32[16,4,4,8,64]{4,0,3,2,1:T(8,128)S(1)} %convolution_multiply_fusion.4), kind=kOutput, calls=%fused_computation.20 | convolution fusion | flops 289124352 | bytes 1228800 | tf_op jit(solution)/shard_map/transpose | solution.py:157
  58.2 2.1 all_to_all.31
  60.3 9.7 %all-to-all-start.2 = ((f32[32,1,11008]{2,1,0:T(1,128)}), f32[32,1,11008]{2,1,0:T(1,128)S(1)}, u32[]{:S(2)}, u32[]{:S(2)}) async-start(f32[32,1,11008]{2,1,0:T(1,128)} %all_to_all.31), calls=%async_computation.2 | async-start | bytes 2818048 | tf_op jit(solution)/shard_map/all_to_all | solution.py:76
  70.8 35.4 %all-to-all-done.2 = f32[32,1,11008]{2,1,0:T(1,128)S(1)} async-done(((f32[32,1,11008]{2,1,0:T(1,128)}), f32[32,1,11008]{2,1,0:T(1,128)S(1)}, u32[]{:S(2)}, u32[]{:S(2)}) %all-to-all-start.2) | async-done | bytes 1409056 | tf_op jit(solution)/shard_map/all_to_all | solution.py:76
  106.1 4.7 %all-to-all-start.1 = ((f32[8,2,2]{1,2,0:T(2,128)}), f32[8,2,2]{1,2,0:T(2,128)S(1)}, u32[]{:S(2)}, u32[]{:S(2)}) async-start(f32[8,2,2]{1,2,0:T(2,128)} %copy.110), calls=%async_computation.1 | async-start | bytes 16384 | tf_op jit(solution)/shard_map/all_to_all | solution.py:270
  112.8 1.3 reshape.398
  114.1 1.5 all-to-all-done.1
  115.6 5.6 %all-to-all-start.3 = ((f32[32,1,3456]{2,1,0:T(1,128)}), f32[32,1,3456]{2,1,0:T(1,128)S(1)}, u32[]{:S(2)}, u32[]{:S(2)}) async-start(f32[32,1,3456]{2,1,0:T(1,128)} %reshape.398), calls=%async_computation.3 | async-start | bytes 884736 | tf_op jit(solution)/shard_map/all_to_all | solution.py:64
  121.4 2.5 %pad_maximum_fusion = bf16[32,16,2112]{2,1,0:T(8,128)(2,1)} fusion(bf16[32,16,2048]{2,1,0:T(8,128)(2,1)S(1)} %broadcast_in_dim.54, bf16[32,16,64]{2,1,0:T(8,128)(2,1)S(1)} %bitcast.117), kind=kLoop, calls=%fused_computation.11 | loop fusion | flops 4325376 | bytes 4325376 | tf_op jit(solution)/shard_map/concatenate | solution.py:85
  124.0 13.5 %all-to-all-done.3 = f32[32,1,3456]{2,1,0:T(1,128)S(1)} async-done(((f32[32,1,3456]{2,1,0:T(1,128)}), f32[32,1,3456]{2,1,0:T(1,128)S(1)}, u32[]{:S(2)}, u32[]{:S(2)}) %all-to-all-start.3) | async-done | bytes 442400 | tf_op jit(solution)/shard_map/all_to_all | solution.py:64
  138.2 4.6 %all-to-all-start.4 = ((bf16[32,16,2112]{2,1,0:T(8,128)(2,1)}), bf16[32,16,2112]{2,1,0:T(8,128)(2,1)S(1)}, u32[]{:S(2)}, u32[]{:S(2)}) async-start(bf16[32,16,2112]{2,1,0:T(8,128)(2,1)} %pad_maximum_fusion), calls=%async_computation.4 | async-start | bytes 4456448 | tf_op jit(solution)/shard_map/all_to_all | solution.py:86
  143.8 5.1 %collective-permute-start.1 = (f32[3,8,1,128]{3,2,1,0:T(1,128)}, f32[3,8,1,128]{3,2,1,0:T(1,128)}, u32[]{:S(2)}, u32[]{:S(2)}) collective-permute-start(f32[3,8,1,128]{3,2,1,0:T(1,128)} %get-tuple-element.97), channel_id=1, source_target_pairs={{1,0},{2,1},{3,2},{4,3},{5,4},{6,5},{7,6},{8,7},{9,8},{10,9},{11,1... | collective-permute-start | bytes 36872 | tf_op jit(solution)/shard_map/ppermute | solution.py:35
  149.4 2.1 convolution_bitcast_fusion
  152.2 1.8 copy.109
  154.6 39.5 %collective-permute-done = f32[3,8,1,128]{3,2,1,0:T(1,128)} collective-permute-done((f32[3,8,1,128]{3,2,1,0:T(1,128)}, f32[3,8,1,128]{3,2,1,0:T(1,128)}, u32[]{:S(2)}, u32[]{:S(2)}) %collective-permute-start) | collective-permute-done | bytes 12320 | tf_op jit(solution)/shard_map/ppermute | solution.py:34
  194.1 1.3 slice_add_fusion.5
  195.4 1.6 scatter-add.14
  197.0 1.5 slice_add_fusion.4
  198.5 1.6 scatter-add.15
  200.1 1.9 fusion.21
  205.9 2.1 subtract_bitcast_fusion
  208.0 2.2 copy.118
  211.8 3.5 %reduce.12 = f32[32,3456]{1,0:T(8,128)} reduce(f32[32,1,3456]{2,1,0:T(1,128)} %copy-done.1, f32[]{:T(128)} %broadcast.274), dimensions={1}, to_apply=%all_to_all.33.reduce_sub_computation | reduce | bytes 884740 | tf_op jit(solution)/shard_map/all_to_all | solution.py:64
  218.6 1.9 fusion.17
  (111 shorter events, 32.9 us)
Async XLA Ops:
  1.4 11.7 %collective-permute-start.2 = (f32[3,1,16,128]{3,2,1,0:T(8,128)S(1)}, f32[3,1,16,128]{3,2,1,0:T(8,128)S(1)}, u32[]{:S(2)}, u32[]{:S(2)}) collective-permute-start(f32[3,1,16,128]{3,2,1,0:T(8,128)S(1)} %get-tuple-element.100), channel_id=1, source_target_pairs={{0,32},{32,64},{64,96},{96,128},{128,160},{160,192},{192,224},{224... | collective-permute-start | bytes 73736 | tf_op jit(solution)/shard_map/ppermute | solution.py:34
  2.9 10.3 %collective-permute-start.3 = (f32[3,1,16,128]{3,2,1,0:T(8,128)S(1)}, f32[3,1,16,128]{3,2,1,0:T(8,128)S(1)}, u32[]{:S(2)}, u32[]{:S(2)}) collective-permute-start(f32[3,1,16,128]{3,2,1,0:T(8,128)S(1)} %get-tuple-element.99), channel_id=1, source_target_pairs={{32,0},{64,32},{96,64},{128,96},{160,128},{192,160},{224,192},{0,2... | collective-permute-start | bytes 73736 | tf_op jit(solution)/shard_map/ppermute | solution.py:35
  13.2 10.4 %copy-start.3 = (bf16[1,54,64]{2,1,0:T(8,128)(2,1)S(1)}, bf16[1,54,64]{2,1,0:T(8,128)(2,1)}, u32[]{:S(2)}) copy-start(bf16[1,54,64]{2,1,0:T(8,128)(2,1)} %param.21) | copy-start | bytes 20740
  16.3 12.1 %all-to-all-start = ((bf16[8,2,259]{2,1,0:T(2,128)(2,1)}), bf16[8,2,259]{2,1,0:T(2,128)(2,1)S(1)}, u32[]{:S(2)}, u32[]{:S(2)}) async-start(bf16[8,2,259]{2,1,0:T(2,128)(2,1)} %pad_maximum_fusion.5), calls=%async_computation | async-start | bytes 24576 | tf_op jit(solution)/shard_map/all_to_all | solution.py:51
  34.3 4.6 %copy-start.6 = (bf16[1,2048,2]{1,2,0:T(2,128)(2,1)S(1)}, bf16[1,2048,2]{1,2,0:T(2,128)(2,1)}, u32[]{:S(2)}) copy-start(bf16[1,2048,2]{1,2,0:T(2,128)(2,1)} %param.24) | copy-start | bytes 24580
  45.1 1.2 copy-start.2
  60.3 45.8 %all-to-all-start.2 = ((f32[32,1,11008]{2,1,0:T(1,128)}), f32[32,1,11008]{2,1,0:T(1,128)S(1)}, u32[]{:S(2)}, u32[]{:S(2)}) async-start(f32[32,1,11008]{2,1,0:T(1,128)} %all_to_all.31), calls=%async_computation.2 | async-start | bytes 2818048 | tf_op jit(solution)/shard_map/all_to_all | solution.py:76
  106.1 9.4 %all-to-all-start.1 = ((f32[8,2,2]{1,2,0:T(2,128)}), f32[8,2,2]{1,2,0:T(2,128)S(1)}, u32[]{:S(2)}, u32[]{:S(2)}) async-start(f32[8,2,2]{1,2,0:T(2,128)} %copy.110), calls=%async_computation.1 | async-start | bytes 16384 | tf_op jit(solution)/shard_map/all_to_all | solution.py:270
  115.6 8.4 %copy-start.5 = (f32[8,2,2]{1,2,0:T(2,128)}, f32[8,2,2]{1,2,0:T(2,128)S(1)}, u32[]{:S(2)}) copy-start(f32[8,2,2]{1,2,0:T(2,128)S(1)} %all-to-all-done.1) | copy-start | bytes 388
  115.6 21.9 %all-to-all-start.3 = ((f32[32,1,3456]{2,1,0:T(1,128)}), f32[32,1,3456]{2,1,0:T(1,128)S(1)}, u32[]{:S(2)}, u32[]{:S(2)}) async-start(f32[32,1,3456]{2,1,0:T(1,128)} %reshape.398), calls=%async_computation.3 | async-start | bytes 884736 | tf_op jit(solution)/shard_map/all_to_all | solution.py:64
  124.0 18.9 %copy-start = (f32[3,8,16,128]{3,2,1,0:T(8,128)S(1)}, f32[3,8,16,128]{3,2,1,0:T(8,128)}, u32[]{:S(2)}) copy-start(f32[3,8,16,128]{3,2,1,0:T(8,128)} %param.18) | copy-start | bytes 589828
  124.0 24.9 %copy-start.7 = (f32[32,16,1,1]{0,1,3,2:T(8,128)S(1)}, f32[32,16,1,1]{0,1,3,2:T(8,128)}, u32[]{:S(2)}) copy-start(f32[32,16,1,1]{0,1,3,2:T(8,128)} %constant.249) | copy-start | bytes 6148
  137.5 0.8 copy-start.1
  138.2 79.3 %all-to-all-start.4 = ((bf16[32,16,2112]{2,1,0:T(8,128)(2,1)}), bf16[32,16,2112]{2,1,0:T(8,128)(2,1)S(1)}, u32[]{:S(2)}, u32[]{:S(2)}) async-start(bf16[32,16,2112]{2,1,0:T(8,128)(2,1)} %pad_maximum_fusion), calls=%async_computation.4 | async-start | bytes 4456448 | tf_op jit(solution)/shard_map/all_to_all | solution.py:86
  143.5 50.6 %collective-permute-start = (f32[3,8,1,128]{3,2,1,0:T(1,128)}, f32[3,8,1,128]{3,2,1,0:T(1,128)}, u32[]{:S(2)}, u32[]{:S(2)}) collective-permute-start(f32[3,8,1,128]{3,2,1,0:T(1,128)} %get-tuple-element.98), channel_id=1, source_target_pairs={{0,1},{1,2},{2,3},{3,4},{4,5},{5,6},{6,7},{7,8},{8,9},{9,10},{10,1... | collective-permute-start | bytes 36872 | tf_op jit(solution)/shard_map/ppermute | solution.py:34
  143.8 53.2 %collective-permute-start.1 = (f32[3,8,1,128]{3,2,1,0:T(1,128)}, f32[3,8,1,128]{3,2,1,0:T(1,128)}, u32[]{:S(2)}, u32[]{:S(2)}) collective-permute-start(f32[3,8,1,128]{3,2,1,0:T(1,128)} %get-tuple-element.97), channel_id=1, source_target_pairs={{1,0},{2,1},{3,2},{4,3},{5,4},{6,5},{7,6},{8,7},{9,8},{10,9},{11,1... | collective-permute-start | bytes 36872 | tf_op jit(solution)/shard_map/ppermute | solution.py:35
  204.9 5.6 %copy-start.4 = (bf16[1,54,64]{2,1,0:T(8,128)(2,1)S(1)}, bf16[1,54,64]{2,1,0:T(8,128)(2,1)}, u32[]{:S(2)}) copy-start(bf16[1,54,64]{2,1,0:T(8,128)(2,1)} %param.21) | copy-start | bytes 20740

commit v3 on v0

--- a/solution.py
+++ b/solution.py
@@ -71,6 +71,27 @@
 
 def gathered_by_axis(shard, axes, order, dim):
     return joined_along(gather_in_order(shard, axes, order), dim)
+
+
+def from_everyone(shard, axis):
+    copies = jnp.broadcast_to(shard, (lax.axis_size(axis), *shard.shape))
+    return lax.all_to_all(copies, axis, split_axis=0, concat_axis=0, tiled=True)
+
+
+def owner_sums(rows, small, axis):
+    count = lax.axis_size(axis)
+    spare = -small.size % count
+    small = jnp.pad(small, (0, spare))
+    both = jnp.concatenate([rows.reshape(count, -1), small.reshape(count, -1)], axis=1)
+    arrived = lax.all_to_all(both, axis, split_axis=0, concat_axis=0, tiled=True).sum(axis=0)
+    part = rows.size // count
+    return arrived[:part].reshape(-1, rows.shape[-1]), arrived[part:]
+
+
+def shared_back(rows, chunk, axis):
+    everything = from_everyone(jnp.concatenate([rows.ravel(), chunk]), axis)
+    whole_rows = everything[:, : rows.size].reshape(-1, rows.shape[-1])
+    return whole_rows, everything[:, rows.size :].reshape(-1)
 
 
 def cheb_tables(points):
@@ -246,6 +267,9 @@
         jnp.bfloat16
     )
     send_valid = jnp.sum(select, axis=1).astype(jnp.bfloat16)
+    new_field, send_rows, send_aims, send_valid = lax.optimization_barrier(
+        (new_field, send_rows, send_aims, send_valid)
+    )
     recv_rows, recv_aims, recv_valid = in_one_piece(
         (send_rows, send_aims, send_valid), "wall", 0, 0, 1
     )
@@ -268,8 +292,17 @@
     )
     own_rows = lax.dynamic_slice_in_dim(w_hidden[0], flow_place * share_rows, share_rows, 0)
     new_w_hidden = row_update(own_rows, grad_hidden)[None]
-    grad_one, grad_two, grad_out = lax.psum((grad_one, grad_two, grad_out), STREAM)
-    new_k_second = row_update(k_second[0], grad_two)
+    small = jnp.concatenate([grad_one.ravel(), grad_out.ravel()])
+    grad_share, small_part = owner_sums(grad_two.reshape(-1, CH), small, STREAM)
+    share_count = grad_share.shape[0]
+    kernel_own = lax.dynamic_slice_in_dim(
+        k_second[0].reshape(-1, CH), flow_place * share_count, share_count, 0
+    )
+    updated_rows = row_update(kernel_own, grad_share)
+    kernel_rows, small = shared_back(updated_rows, small_part, STREAM)
+    new_k_second = kernel_rows.reshape(k_second.shape[1:])
+    grad_one = small[: grad_one.size].reshape(grad_one.shape)
+    grad_out = small[grad_one.size : grad_one.size + grad_out.size].reshape(grad_out.shape)
     new_k_first = row_update(k_first[0], grad_one)
     new_w_out = whole_update(w_out[0], grad_out)
     return (new_field, stress, new_k_first[None], new_k_second[None], new_w_hidden, new_w_out[None])

time: 360 us -> 187 us (0.52)
  blocking collectives: 135 us -> 6.55 us
  waiting for transfers between devices: 117 us -> 54.2 us
  local copies, waits for them, and re-layouts: 15.5 us -> 28.4 us
  starting transfers between devices: 25.8 us -> 35.8 us
    psum x1 -> x0, blocking collectives: 129 us -> none  [body(): lax.psum((grad_one, grad_two, grad_out), STREAM)]
    psum x1 -> x0, waiting for transfers between devices: 83.8 us -> none  [body(): lax.psum((grad_one, grad_two, grad_out), STREAM)]
    all_to_all x0 -> x2, waiting for transfers between devices: none -> 34.7 us  [the longest x1 20.4 us: owner_sums(): lax.all_to_all(both, axis, split_axis=0, concat_axis=0, tiled=True)]
    all_gather x2, waiting for transfers between devices: 19.4 us -> 0.02 us  [gather_in_order(): tiles = lax.all_gather(tiles, axes[k])]
    all_to_all x0 -> x2, starting transfers between devices: none -> 11.2 us  [the longest x1 7.28 us: owner_sums(): lax.all_to_all(both, axis, split_axis=0, concat_axis=0, tiled=True)]
    all_to_all x1, waiting for transfers between devices: 0.01 us -> 4.22 us  [body(): back = lax.all_to_all(pred, 'wall', split_axis=0, concat_axis=0, tiled=True)]
  transfers between devices with their start and end apart: 10 -> 11, of which waited for: 4 -> 5; matrix products, arithmetic and copies ran while one was open for 16% -> 15% of each run, Pallas kernels for 0% -> 0%
where the time goes in v3:
time: 187 us; the launch traced here: 185 us
  waiting for transfers between devices  54.2 us (29%)
  starting transfers between devices  35.8 us (19%)
  matrix products  30.6 us (16%)
  local copies, waits for them, and re-layouts  28.4 us (15%)
  between operations  15.4 us (8%)
  other arithmetic  13.8 us (7%)
  blocking collectives  6.55 us (4%)
    all_to_all x1, waiting for transfers between devices, owner_sums(): lax.all_to_all(both, axis, split_axis=0, concat_axis=0, tiled=True)  20.4 us
    all_to_all x1, waiting for transfers between devices, from_everyone(): return lax.all_to_all(copies, axis, split_axis=0, concat_axis=0, tiled=True)  14.2 us
    all_to_all x1, waiting for transfers between devices, body(): lax.all_to_all(features, STREAM, split_axis=1, concat_axis=0, tiled=True)  9.8 us
    transpose x2, matrix products, conv_filter(): return jnp.moveaxis(taps, 0, 3)  8.22 us
    ppermute x2, starting transfers between devices, extended(): lax.ppermute(first, axis, [(b, a) for a, b in up])  7.98 us
    all_to_all x1, starting transfers between devices, owner_sums(): lax.all_to_all(both, axis, split_axis=0, concat_axis=0, tiled=True)  7.28 us
    all_gather x1, blocking collectives, gather_in_order(): tiles = lax.all_gather(tiles, axes[k])  6.55 us
    all_to_all x1, starting transfers between devices, in_one_piece(): lax.all_to_all(both, axis, split_axis=split_dim, concat_axis=concat_dim,...  5.88 us
  transfers between devices with their start and end apart: 11, of which 5 were waited for; matrix products, arithmetic and copies ran while one was open for 15% of the time, Pallas kernels for 0%

profile of v3, /device:TPU:2, one launch (start us, length us, event | category | flops | bytes accessed | tf_op | source)
XLA Modules:
  0.0 184.7 jit_solution(17004997111494216310)
XLA Ops:
  7.9 1.5 collective-permute-start.2
  10.3 1.0 fusion.45
  11.3 7.1 %collective-permute-start.1 = (f32[3,8,1,128]{3,2,1,0:T(1,128)S(1)}, f32[3,8,1,128]{3,2,1,0:T(1,128)S(1)}, u32[]{:S(2)}, u32[]{:S(2)}) collective-permute-start(f32[3,8,1,128]{3,2,1,0:T(1,128)S(1)} %get-tuple-element.99), channel_id=1, source_target_pairs={{1,0},{2,1},{3,2},{4,3},{5,4},{6,5},{7,6},{8,7},{9,8},{10,9},{11,1... | collective-permute-start | bytes 36872 | tf_op jit(solution)/shard_map/ppermute | solution.py:35
  19.8 1.6 slice_bitcast_fusion.2
  22.2 1.5 fusion.22
  26.0 1.5 convolution_bitcast_fusion.1
  27.5 1.5 convolution_bitcast_fusion
  28.9 1.2 reshape.304
  35.1 2.2 %reshape.307 = f32[2,2,4,4,4,16,8]{6,5,4,3,2,1,0:T(8,128)S(1)} reshape(f32[2,8,16,128]{3,2,1,0:T(8,128)} %pad_maximum_fusion.2) | data formatting | bytes 262144 | tf_op jit(solution)/shard_map/reshape | solution.py:253
  40.6 1.8 fusion.19
  44.6 5.9 %all-to-all-start = ((bf16[8,2,259]{2,1,0:T(2,128)(2,1)}), bf16[8,2,259]{2,1,0:T(2,128)(2,1)S(1)}, u32[]{:S(2)}, u32[]{:S(2)}) async-start(bf16[8,2,259]{2,1,0:T(2,128)(2,1)} %pad_maximum_fusion.5), calls=%async_computation | async-start | bytes 24576 | tf_op jit(solution)/shard_map/all_to_all | solution.py:51
  50.6 4.8 %all-to-all-done = bf16[8,2,259]{2,1,0:T(2,128)(2,1)S(1)} async-done(((bf16[8,2,259]{2,1,0:T(2,128)(2,1)}), bf16[8,2,259]{2,1,0:T(2,128)(2,1)S(1)}, u32[]{:S(2)}, u32[]{:S(2)}) %all-to-all-start) | async-done | bytes 8320 | tf_op jit(solution)/shard_map/all_to_all | solution.py:51
  57.1 3.1 %fusion.14 = (f32[16,4,4,8,64]{4,0,3,2,1:T(8,128)S(1)}, f32[16,4,4,8,64]{4,0,3,2,1:T(8,128)S(1)}) fusion(bf16[3,3,3,64,64]{4,3,2,1,0:T(8,128)(2,1)} %bitcast.149, f32[16,4,4,8,64]{4,0,3,2,1:T(8,128)S(1)} %convolution_multiply_fusion.4), kind=kOutput, calls=%fused_computation.28 | convolution fusion | flops 289669120 | bytes 1794048 | tf_op jit(solution)/shard_map/conv_general_dilated | solution.py:152
  61.0 4.6 %multiply_convert_fusion.3 = (bf16[16,2048]{1,0:T(8,128)(2,1)S(1)}, f32[16,2048]{1,0:T(8,128)S(1)}) fusion(bf16[16,2048]{1,0:T(8,128)(2,1)S(1)} %convert_element_type.101, bf16[1,2048,2048]{2,1,0:T(8,128)(2,1)} %param.23), kind=kOutput, calls=%fused_computation.51 | convolution fusion | flops 134414336 | bytes 8650752 | tf_op jit(solution)/shard_map/dot_general | solution.py:181
  66.1 5.6 %fusion.8 = f32[16,2048]{1,0:T(8,128)S(1)} fusion(bf16[16,2048]{1,0:T(8,128)(2,1)S(1)} %fusion.11, bf16[1,2048,2048]{2,1,0:T(8,128)(2,1)} %param.23), kind=kOutput, calls=%fused_computation.9 | convolution fusion | flops 134250496 | bytes 8585216 | tf_op jit(solution)/shard_map/dot_general | solution.py:189
  73.3 2.7 %convolution_multiply_fusion.5 = f32[3,3,3,64,64]{4,3,2,1,0:T(8,128)S(1)} fusion(bf16[16,4,4,8,64]{4,0,3,2,1:T(8,128)(2,1)S(1)} %multiply_convert_fusion, f32[16,4,4,8,64]{4,0,3,2,1:T(8,128)S(1)} %convolution_multiply_fusion.4), kind=kOutput, calls=%fused_computation.16 | convolution fusion | flops 289124352 | bytes 1228800 | tf_op jit(solution)/shard_map/transpose | solution.py:163
  76.1 5.5 %convolution_multiply_fusion.6 = f32[3,3,3,2,64]{4,3,2,1,0:T(2,128)S(1)} fusion(bf16[16,2,4,4,8]{0,4,3,2,1:T(8,128)(2,1)S(1)} %bitcast.144, bf16[16,4,4,8,64]{4,0,3,2,1:T(8,128)(2,1)} %copy-done.3, bf16[3,3,3,64,64]{4,3,2,1,0:T(8,128)(2,1)S(1)} %bitcast.150, f32[16,4,4,8,64]{4,0,3,2,1:T(8,128)S(1)} %convolution_multiply_fusion.4), kind=kOutput, calls=%fused_computation.20 | convolution fusion | flops 298683776 | bytes 1029632 | tf_op jit(solution)/shard_map/transpose | solution.py:163
  81.8 6.6 %all-gather = bf16[32,2048]{1,0:T(8,128)(2,1)} all-gather(bf16[16,2048]{1,0:T(8,128)(2,1)S(1)} %fusion.11), channel_id=2, replica_groups=mesh['wall'=8,'stream_0'=8,'stream_1'=2,'stream_2'=2] {'stream_1'}, dimensions={0}, use_global_device_ids=true | all-gather | bytes 196608 | tf_op jit(solution)/shard_map/all_gather | solution.py:65
  89.7 1.1 all_to_all.43
  90.8 7.3 %all-to-all-start.2 = ((f32[32,1,3692]{2,1,0:T(1,128)}), f32[32,1,3692]{2,1,0:T(1,128)S(1)}, u32[]{:S(2)}, u32[]{:S(2)}) async-start(f32[32,1,3692]{2,1,0:T(1,128)} %all_to_all.43), calls=%async_computation.2 | async-start | bytes 950272 | tf_op jit(solution)/shard_map/all_to_all | solution.py:86
  99.6 20.4 %all-to-all-done.2 = f32[32,1,3692]{2,1,0:T(1,128)S(1)} async-done(((f32[32,1,3692]{2,1,0:T(1,128)}), f32[32,1,3692]{2,1,0:T(1,128)S(1)}, u32[]{:S(2)}, u32[]{:S(2)}) %all-to-all-start.2) | async-done | bytes 472608 | tf_op jit(solution)/shard_map/all_to_all | solution.py:86
  120.0 4.4 %all-to-all-start.1 = ((f32[8,2,2]{1,2,0:T(2,128)}), f32[8,2,2]{1,2,0:T(2,128)S(1)}, u32[]{:S(2)}, u32[]{:S(2)}) async-start(f32[8,2,2]{1,2,0:T(2,128)} %copy.90), calls=%async_computation.1 | async-start | bytes 16384 | tf_op jit(solution)/shard_map/all_to_all | solution.py:279
  125.0 4.2 %all-to-all-done.1 = f32[8,2,2]{1,2,0:T(2,128)S(1)} async-done(((f32[8,2,2]{1,2,0:T(2,128)}), f32[8,2,2]{1,2,0:T(2,128)S(1)}, u32[]{:S(2)}, u32[]{:S(2)}) %all-to-all-start.1) | async-done | bytes 160 | tf_op jit(solution)/shard_map/all_to_all | solution.py:279
  129.2 4.8 %all-to-all-start.4 = ((bf16[32,2,512]{2,1,0:T(2,128)(2,1)}), bf16[32,2,512]{2,1,0:T(2,128)(2,1)S(1)}, u32[]{:S(2)}, u32[]{:S(2)}) async-start(bf16[32,2,512]{2,1,0:T(2,128)(2,1)} %reshape.340), calls=%async_computation.4 | async-start | bytes 131072 | tf_op jit(solution)/shard_map/all_to_all | solution.py:284
  134.1 9.8 %all-to-all-done.4 = bf16[32,2,512]{2,1,0:T(2,128)(2,1)S(1)} async-done(((bf16[32,2,512]{2,1,0:T(2,128)(2,1)}), bf16[32,2,512]{2,1,0:T(2,128)(2,1)S(1)}, u32[]{:S(2)}, u32[]{:S(2)}) %all-to-all-start.4) | async-done | bytes 65568 | tf_op jit(solution)/shard_map/all_to_all | solution.py:284
  143.9 1.0 broadcast_in_dim.48
  145.0 3.9 %all-to-all-start.3 = ((f32[32,1,3692]{2,1,0:T(1,128)}), f32[32,1,3692]{2,1,0:T(1,128)S(1)}, u32[]{:S(2)}, u32[]{:S(2)}) async-start(f32[32,1,3692]{2,1,0:T(1,128)} %broadcast_in_dim.48), calls=%async_computation.3 | async-start | bytes 950272 | tf_op jit(solution)/shard_map/all_to_all | solution.py:78
  151.6 14.2 %all-to-all-done.3 = f32[32,1,3692]{2,1,0:T(1,128)S(1)} async-done(((f32[32,1,3692]{2,1,0:T(1,128)}), f32[32,1,3692]{2,1,0:T(1,128)S(1)}, u32[]{:S(2)}, u32[]{:S(2)}) %all-to-all-start.3) | async-done | bytes 472608 | tf_op jit(solution)/shard_map/all_to_all | solution.py:78
  169.7 0.9 copy.99
  170.6 2.1 %broadcast_in_dim_reshape_reshape.3 = f32[1,27,64,64]{3,2,1,0:T(8,128)} reshape(f32[32,3456]{1,0:T(8,128)} %slice.230) | data formatting | bytes 884736 | tf_op jit(solution)/shard_map/broadcast_in_dim;reshape;reshape | solution.py:308
  173.6 1.8 copy.96
  176.0 1.9 %fusion.15 = f32[1,64,2048]{2,1,0:T(8,128)} fusion(f32[64,2048]{1,0:T(8,128)S(1)} %get-tuple-element.110, f32[64]{0:T(128)S(1)} %add_sqrt_fusion, bf16[1,2048,2048]{2,1,0:T(8,128)(2,1)} %param.23, s32[]{:T(128)S(6)} %select_n.37), kind=kLoop, calls=%fused_computation.32 | loop fusion | flops 524288 | bytes 1310980 | tf_op jit(solution)/shard_map/broadcast_in_dim | solution.py:294
  (146 shorter events, 31.9 us)
Async XLA Ops:
  7.9 25.8 %collective-permute-start.2 = (f32[3,1,16,128]{3,2,1,0:T(8,128)S(1)}, f32[3,1,16,128]{3,2,1,0:T(8,128)S(1)}, u32[]{:S(2)}, u32[]{:S(2)}) collective-permute-start(f32[3,1,16,128]{3,2,1,0:T(8,128)S(1)} %get-tuple-element.102), channel_id=1, source_target_pairs={{0,32},{32,64},{64,96},{96,128},{128,160},{160,192},{192,224},{224... | collective-permute-start | bytes 73736 | tf_op jit(solution)/shard_map/ppermute | solution.py:34
  9.4 24.3 %collective-permute-start.3 = (f32[3,1,16,128]{3,2,1,0:T(8,128)S(1)}, f32[3,1,16,128]{3,2,1,0:T(8,128)S(1)}, u32[]{:S(2)}, u32[]{:S(2)}) collective-permute-start(f32[3,1,16,128]{3,2,1,0:T(8,128)S(1)} %get-tuple-element.101), channel_id=1, source_target_pairs={{32,0},{64,32},{96,64},{128,96},{160,128},{192,160},{224,192},{0,2... | collective-permute-start | bytes 73736 | tf_op jit(solution)/shard_map/ppermute | solution.py:35
  11.2 22.2 %collective-permute-start = (f32[3,8,1,128]{3,2,1,0:T(1,128)S(1)}, f32[3,8,1,128]{3,2,1,0:T(1,128)S(1)}, u32[]{:S(2)}, u32[]{:S(2)}) collective-permute-start(f32[3,8,1,128]{3,2,1,0:T(1,128)S(1)} %get-tuple-element.100), channel_id=1, source_target_pairs={{0,1},{1,2},{2,3},{3,4},{4,5},{5,6},{6,7},{7,8},{8,9},{9,10},{10,1... | collective-permute-start | bytes 36872 | tf_op jit(solution)/shard_map/ppermute | solution.py:34
  11.3 22.2 %collective-permute-start.1 = (f32[3,8,1,128]{3,2,1,0:T(1,128)S(1)}, f32[3,8,1,128]{3,2,1,0:T(1,128)S(1)}, u32[]{:S(2)}, u32[]{:S(2)}) collective-permute-start(f32[3,8,1,128]{3,2,1,0:T(1,128)S(1)} %get-tuple-element.99), channel_id=1, source_target_pairs={{1,0},{2,1},{3,2},{4,3},{5,4},{6,5},{7,6},{8,7},{9,8},{10,9},{11,1... | collective-permute-start | bytes 36872 | tf_op jit(solution)/shard_map/ppermute | solution.py:35
  19.8 12.0 %copy-start.19 = (pred[8]{0:T(512)(128)(4,1)}, pred[8]{0:T(512)(128)(4,1)S(1)}, u32[]{:S(2)}) copy-start(pred[8]{0:T(512)(128)(4,1)S(1)} %compare_and_fusion) | copy-start | bytes 28
  23.7 7.5 %copy-start.12 = (s32[1024]{0:T(1024)}, s32[1024]{0:T(1024)S(1)}, u32[]{:S(2)}) copy-start(s32[1024]{0:T(1024)S(1)} %pad_clamp_fusion) | copy-start | bytes 12292
  26.0 6.7 %copy-start.17 = (s32[8]{0:T(128)}, s32[8]{0:T(128)S(1)}, u32[]{:S(2)}) copy-start(s32[8]{0:T(128)S(1)} %multiply_add_fusion) | copy-start | bytes 100
  33.7 0.7 copy-start.2
  33.7 0.7 copy-start.1
  35.1 5.5 %copy-start = (f32[3,8,16,128]{3,2,1,0:T(8,128)S(1)}, f32[3,8,16,128]{3,2,1,0:T(8,128)}, u32[]{:S(2)}) copy-start(f32[3,8,16,128]{3,2,1,0:T(8,128)} %param.18) | copy-start | bytes 589828
  37.3 13.3 %copy-start.9 = (bf16[1,54,64]{2,1,0:T(8,128)(2,1)S(1)}, bf16[1,54,64]{2,1,0:T(8,128)(2,1)}, u32[]{:S(2)}) copy-start(bf16[1,54,64]{2,1,0:T(8,128)(2,1)} %param.21) | copy-start | bytes 20740
  44.6 10.7 %all-to-all-start = ((bf16[8,2,259]{2,1,0:T(2,128)(2,1)}), bf16[8,2,259]{2,1,0:T(2,128)(2,1)S(1)}, u32[]{:S(2)}, u32[]{:S(2)}) async-start(bf16[8,2,259]{2,1,0:T(2,128)(2,1)} %pad_maximum_fusion.5), calls=%async_computation | async-start | bytes 24576 | tf_op jit(solution)/shard_map/all_to_all | solution.py:51
  50.5 98.4 %all-gather.6.cloned.1.call-start = ((), (), s32[]{:S(2)}) async-start(), calls=%async_computation.5 | async-start | bytes 1179648 | tf_op jit(solution)/shard_map/all_gather | solution.py:65
  55.4 4.9 %copy-start.8 = (bf16[16,259]{1,0:T(8,128)(2,1)}, bf16[16,259]{1,0:T(8,128)(2,1)S(1)}, u32[]{:S(2)}) copy-start(bf16[16,259]{1,0:T(8,128)(2,1)S(1)} %all_to_all.39) | copy-start | bytes 24868
  56.2 4.1 %copy-start.5 = (bf16[16,256]{0,1:T(8,128)(2,1)}, bf16[16,256]{0,1:T(8,128)(2,1)S(1)}, u32[]{:S(2)}) copy-start(bf16[16,256]{0,1:T(8,128)(2,1)S(1)} %copy.86) | copy-start | bytes 24580
  60.3 0.7 slice-start
  61.0 4.6 %copy-start.10 = (bf16[1,2048,2]{1,2,0:T(2,128)(2,1)S(1)}, bf16[1,2048,2]{1,2,0:T(2,128)(2,1)}, u32[]{:S(2)}) copy-start(bf16[1,2048,2]{1,2,0:T(2,128)(2,1)} %param.24) | copy-start | bytes 24580
  61.0 4.8 %copy-start.15 = (f32[16]{0:T(128)S(1)}, f32[16]{0:T(128)}, u32[]{:S(2)}) copy-start(f32[16]{0:T(128)} %convert_reduce_fusion) | copy-start | bytes 196
  65.8 15.8 %copy-start.13 = (f32[16,2]{0,1:T(2,128)}, f32[16,2]{0,1:T(2,128)S(1)}, u32[]{:S(2)}) copy-start(f32[16,2]{0,1:T(2,128)S(1)} %convolution_multiply_fusion.7) | copy-start | bytes 388
  72.5 0.8 copy-start.3
  73.3 2.7 %copy-start.6 = (bf16[16,256]{0,1:T(8,128)(2,1)S(1)}, bf16[16,256]{0,1:T(8,128)(2,1)}, u32[]{:S(2)}) copy-start(bf16[16,256]{0,1:T(8,128)(2,1)} %copy-done.5) | copy-start | bytes 24580
  73.3 2.7 %copy-start.16 = (bf16[1,27,64,64]{3,2,1,0:T(8,128)(2,1)S(1)}, bf16[1,27,64,64]{3,2,1,0:T(8,128)(2,1)}, u32[]{:S(2)}) copy-start(bf16[1,27,64,64]{3,2,1,0:T(8,128)(2,1)} %param.22) | copy-start | bytes 663556
  89.0 9.1 %copy-start.14 = (f32[16,2]{0,1:T(2,128)S(1)}, f32[16,2]{0,1:T(2,128)}, u32[]{:S(2)}) copy-start(f32[16,2]{0,1:T(2,128)} %copy-done.13) | copy-start | bytes 388
  90.8 29.2 %all-to-all-start.2 = ((f32[32,1,3692]{2,1,0:T(1,128)}), f32[32,1,3692]{2,1,0:T(1,128)S(1)}, u32[]{:S(2)}, u32[]{:S(2)}) async-start(f32[32,1,3692]{2,1,0:T(1,128)} %all_to_all.43), calls=%async_computation.2 | async-start | bytes 950272 | tf_op jit(solution)/shard_map/all_to_all | solution.py:86
  98.1 51.5 %copy-start.11 = (bf16[1,2048,2]{1,2,0:T(2,128)(2,1)S(1)}, bf16[1,2048,2]{1,2,0:T(2,128)(2,1)}, u32[]{:S(2)}) copy-start(bf16[1,2048,2]{1,2,0:T(2,128)(2,1)} %param.24) | copy-start | bytes 24580
  98.2 51.8 %copy-start.18 = (s32[8]{0:T(128)S(1)}, s32[8]{0:T(128)}, u32[]{:S(2)}) copy-start(s32[8]{0:T(128)} %copy-done.17) | copy-start | bytes 100
  120.0 9.2 %all-to-all-start.1 = ((f32[8,2,2]{1,2,0:T(2,128)}), f32[8,2,2]{1,2,0:T(2,128)S(1)}, u32[]{:S(2)}, u32[]{:S(2)}) async-start(f32[8,2,2]{1,2,0:T(2,128)} %copy.90), calls=%async_computation.1 | async-start | bytes 16384 | tf_op jit(solution)/shard_map/all_to_all | solution.py:279
  129.2 14.8 %all-to-all-start.4 = ((bf16[32,2,512]{2,1,0:T(2,128)(2,1)}), bf16[32,2,512]{2,1,0:T(2,128)(2,1)S(1)}, u32[]{:S(2)}, u32[]{:S(2)}) async-start(bf16[32,2,512]{2,1,0:T(2,128)(2,1)} %reshape.340), calls=%async_computation.4 | async-start | bytes 131072 | tf_op jit(solution)/shard_map/all_to_all | solution.py:284
  145.0 20.9 %all-to-all-start.3 = ((f32[32,1,3692]{2,1,0:T(1,128)}), f32[32,1,3692]{2,1,0:T(1,128)S(1)}, u32[]{:S(2)}, u32[]{:S(2)}) async-start(f32[32,1,3692]{2,1,0:T(1,128)} %broadcast_in_dim.48), calls=%async_computation.3 | async-start | bytes 950272 | tf_op jit(solution)/shard_map/all_to_all | solution.py:78
  148.9 24.8 %all-gather.8.cloned.1.call-start = ((), (), s32[]{:S(2)}) async-start(), calls=%async_computation.6 | async-start | bytes 3145728 | tf_op jit(solution)/shard_map/all_gather | solution.py:65
  169.7 3.1 %copy-start.7 = (f32[118,64]{1,0:T(8,128)S(1)}, f32[118,64]{1,0:T(8,128)}, u32[]{:S(2)}) copy-start(f32[118,64]{1,0:T(8,128)} %slice.205) | copy-start | bytes 90628
  173.6 1.8 copy-start.4
Sparse Core Ops, SparseCore 0:
  89.8 40.5 all-gather.5
  151.5 16.1 all-gather.7

commit v4 on v3

--- a/solution.py
+++ b/solution.py
@@ -53,39 +53,23 @@
     return tuple((b.reshape(*whole.shape[:along], *a.shape[along:]) for a, b in zip(arrays, tiles)))
 
 
-def joined_along(tiles, dim):
-    lengths = list(tiles.shape[1:])
-    lengths[dim] *= tiles.shape[0]
-    return jnp.moveaxis(tiles, 0, dim).reshape(lengths)
-
-
-def gather_in_order(shard, axes, order):
-    tiles = shard
-    for k in order:
-        tiles = lax.all_gather(tiles, axes[k])
-    done = order[::-1]
-    back = [done.index(k) for k in range(len(axes))]
-    tiles = tiles.transpose(*back, *range(len(axes), tiles.ndim))
-    return tiles.reshape(-1, *shard.shape)
-
-
-def gathered_by_axis(shard, axes, order, dim):
-    return joined_along(gather_in_order(shard, axes, order), dim)
-
-
 def from_everyone(shard, axis):
     copies = jnp.broadcast_to(shard, (lax.axis_size(axis), *shard.shape))
     return lax.all_to_all(copies, axis, split_axis=0, concat_axis=0, tiled=True)
 
 
-def owner_sums(rows, small, axis):
+def owner_sums(rows, small, tiles, axis):
     count = lax.axis_size(axis)
     spare = -small.size % count
     small = jnp.pad(small, (0, spare))
-    both = jnp.concatenate([rows.reshape(count, -1), small.reshape(count, -1)], axis=1)
-    arrived = lax.all_to_all(both, axis, split_axis=0, concat_axis=0, tiled=True).sum(axis=0)
+    summed = [rows.reshape(count, -1), small.reshape(count, -1)]
+    width = sum(part.shape[1] for part in summed)
+    both = jnp.concatenate(summed + [tiles.reshape(count, -1).astype(jnp.float32)], axis=1)
+    arrived = lax.all_to_all(both, axis, split_axis=0, concat_axis=0, tiled=True)
+    total = arrived[:, :width].sum(axis=0)
     part = rows.size // count
-    return arrived[:part].reshape(-1, rows.shape[-1]), arrived[part:]
+    moved = arrived[:, width:].astype(tiles.dtype).reshape(-1, *tiles.shape[2:])
+    return total[:part].reshape(-1, rows.shape[-1]), total[part:], moved
 
 
 def shared_back(rows, chunk, axis):
@@ -281,19 +265,19 @@
     stress = stress_local.T[:, None, :]
     share_rows = FEATS // flow_count
     dense_scale = 1.0 / math.sqrt(1.0 * FEATS)
-    columns_here = lax.all_to_all(features, STREAM, split_axis=1, concat_axis=0, tiled=True)
+    small = jnp.concatenate([grad_one.ravel(), grad_out.ravel()])
+    tiles = features.reshape(features.shape[0], flow_count, -1).transpose(1, 0, 2)
+    grad_share, small_part, columns_here = owner_sums(grad_two.reshape(-1, CH), small, tiles, STREAM)
     grad_hidden = (
         jnp.dot(
             columns_here.T,
-            gathered_by_axis(delta_three, STREAM, (1, 0, 2), 0),
+            lax.all_gather(delta_three, STREAM, axis=0, tiled=True),
             preferred_element_type=jnp.float32,
         )
         * dense_scale
     )
     own_rows = lax.dynamic_slice_in_dim(w_hidden[0], flow_place * share_rows, share_rows, 0)
     new_w_hidden = row_update(own_rows, grad_hidden)[None]
-    small = jnp.concatenate([grad_one.ravel(), grad_out.ravel()])
-    grad_share, small_part = owner_sums(grad_two.reshape(-1, CH), small, STREAM)
     share_count = grad_share.shape[0]
     kernel_own = lax.dynamic_slice_in_dim(
         k_second[0].reshape(-1, CH), flow_place * share_count, share_count, 0

time: 187 us -> 197 us (1.053)
  waiting for transfers between devices: 54.2 us -> 66.4 us
  blocking collectives: 6.55 us -> 0 us
  other arithmetic: 13.8 us -> 18.7 us
  starting transfers between devices: 35.8 us -> 32 us
  matrix products: 30.6 us -> 33.2 us
    all_gather x2 -> x1, waiting for transfers between devices: 0.02 us -> 24.1 us  [body(): lax.all_gather(delta_three, STREAM, axis=0, tiled=True)]
    all_to_all x1 -> x0, waiting for transfers between devices: 9.8 us -> none  [body(): lax.all_to_all(features, STREAM, split_axis=1, concat_axis=0, tiled=True)]
    all_gather x1 -> x0, blocking collectives: 6.55 us -> none  [gather_in_order(): tiles = lax.all_gather(tiles, axes[k])]
    all_to_all x1 -> x0, starting transfers between devices: 4.75 us -> none  [body(): lax.all_to_all(features, STREAM, split_axis=1, concat_axis=0, tiled=True)]
    all_to_all x1, waiting for transfers between devices: 20.4 us -> 18.4 us  [owner_sums(): lax.all_to_all(both, axis, split_axis=0, concat_axis=0, tiled=True)]
    unnamed x47 -> x34, local copies, waits for them, and re-layouts: 5.1 us -> 4.23 us
  transfers between devices with their start and end apart: 11 -> 9, of which waited for: 5 -> 5; matrix products, arithmetic and copies ran while one was open for 15% -> 17% of each run, Pallas kernels for 0% -> 0%
where the time goes in v4:
time: 197 us; the launch traced here: 194 us
  waiting for transfers between devices  66.4 us (34%)
  matrix products  33.2 us (17%)
  starting transfers between devices  32 us (16%)
  local copies, waits for them, and re-layouts  28.5 us (14%)
  other arithmetic  18.7 us (9%)
  between operations  15.3 us (8%)
    all_gather x1, waiting for transfers between devices, body(): lax.all_gather(delta_three, STREAM, axis=0, tiled=True)  24.1 us
    all_to_all x1, waiting for transfers between devices, owner_sums(): lax.all_to_all(both, axis, split_axis=0, concat_axis=0, tiled=True)  18.4 us
    all_to_all x1, waiting for transfers between devices, from_everyone(): return lax.all_to_all(copies, axis, split_axis=0, concat_axis=0, tiled=True)  14.9 us
    transpose x2, matrix products, conv_filter(): return jnp.moveaxis(taps, 0, 3)  9.21 us
    ppermute x2, starting transfers between devices, extended(): lax.ppermute(first, axis, [(b, a) for a, b in up])  7.9 us
    all_to_all x1, starting transfers between devices, owner_sums(): lax.all_to_all(both, axis, split_axis=0, concat_axis=0, tiled=True)  7.37 us
    all_to_all x1, starting transfers between devices, in_one_piece(): lax.all_to_all(both, axis, split_axis=split_dim, concat_axis=concat_dim,...  5.88 us
    dot_general x1, matrix products, forward_back(): jnp.dot(delta_three, w_hidden.T, preferred_element_type=jnp.float32)  5.67 us
  transfers between devices with their start and end apart: 9, of which 5 were waited for; matrix products, arithmetic and copies ran while one was open for 17% of the time, Pallas kernels for 0%

profile of v4, /device:TPU:2, one launch (start us, length us, event | category | flops | bytes accessed | tf_op | source)
XLA Modules:
  0.0 194.2 jit_solution(9005336837468079802)
XLA Ops:
  7.2 1.4 fusion.46
  8.6 1.5 collective-permute-start.2
  10.9 1.6 fusion.45
  12.4 7.1 %collective-permute-start.1 = (f32[3,8,1,128]{3,2,1,0:T(1,128)}, f32[3,8,1,128]{3,2,1,0:T(1,128)}, u32[]{:S(2)}, u32[]{:S(2)}) collective-permute-start(f32[3,8,1,128]{3,2,1,0:T(1,128)} %get-tuple-element.99), channel_id=1, source_target_pairs={{1,0},{2,1},{3,2},{4,3},{5,4},{6,5},{7,6},{8,7},{9,8},{10,9},{11,1... | collective-permute-start | bytes 36872 | tf_op jit(solution)/shard_map/ppermute | solution.py:35
  20.9 1.6 slice_bitcast_fusion.2
  22.4 0.9 fusion.44
  23.3 1.5 fusion.22
  27.1 1.4 convolution_bitcast_fusion.1
  28.5 1.5 convolution_bitcast_fusion
  30.0 1.2 reshape.310
  39.0 2.1 %reshape.313 = f32[2,2,4,4,4,16,8]{6,5,4,3,2,1,0:T(8,128)S(1)} reshape(f32[2,8,16,128]{3,2,1,0:T(8,128)} %pad_maximum_fusion.1) | data formatting | bytes 262144 | tf_op jit(solution)/shard_map/reshape | solution.py:237
  44.4 1.8 fusion.19
  48.5 5.9 %all-to-all-start = ((bf16[8,2,259]{2,1,0:T(2,128)(2,1)}), bf16[8,2,259]{2,1,0:T(2,128)(2,1)S(1)}, u32[]{:S(2)}, u32[]{:S(2)}) async-start(bf16[8,2,259]{2,1,0:T(2,128)(2,1)} %pad_maximum_fusion.4), calls=%async_computation | async-start | bytes 24576 | tf_op jit(solution)/shard_map/all_to_all | solution.py:51
  54.4 4.8 %all-to-all-done = bf16[8,2,259]{2,1,0:T(2,128)(2,1)S(1)} async-done(((bf16[8,2,259]{2,1,0:T(2,128)(2,1)}), bf16[8,2,259]{2,1,0:T(2,128)(2,1)S(1)}, u32[]{:S(2)}, u32[]{:S(2)}) %all-to-all-start) | async-done | bytes 8320 | tf_op jit(solution)/shard_map/all_to_all | solution.py:51
  61.5 3.1 %fusion.14 = (f32[16,4,4,8,64]{4,0,3,2,1:T(8,128)S(1)}, f32[16,4,4,8,64]{4,0,3,2,1:T(8,128)S(1)}) fusion(bf16[3,3,3,64,64]{4,3,2,1,0:T(8,128)(2,1)} %bitcast.141, f32[16,4,4,8,64]{4,0,3,2,1:T(8,128)S(1)} %convolution_multiply_fusion.4), kind=kOutput, calls=%fused_computation.28 | convolution fusion | flops 289669120 | bytes 1794048 | tf_op jit(solution)/shard_map/conv_general_dilated | solution.py:136
  65.8 4.6 %multiply_convert_fusion.3 = (bf16[16,2048]{1,0:T(8,128)(2,1)S(1)}, f32[16,2048]{1,0:T(8,128)S(1)}) fusion(bf16[16,2048]{1,0:T(8,128)(2,1)S(1)} %convert_element_type.112, bf16[1,2048,2048]{2,1,0:T(8,128)(2,1)} %param.23), kind=kOutput, calls=%fused_computation.54 | convolution fusion | flops 134414336 | bytes 8650752 | tf_op jit(solution)/shard_map/dot_general | solution.py:165
  71.0 5.7 %fusion.8 = f32[16,2048]{1,0:T(8,128)S(1)} fusion(bf16[16,2048]{1,0:T(8,128)(2,1)S(1)} %fusion.11, bf16[1,2048,2048]{2,1,0:T(8,128)(2,1)} %param.23), kind=kOutput, calls=%fused_computation.9 | convolution fusion | flops 134250496 | bytes 8585216 | tf_op jit(solution)/shard_map/dot_general | solution.py:173
  78.3 5.2 %convolution_multiply_fusion.6 = f32[3,3,3,2,64]{4,3,2,1,0:T(2,128)S(1)} fusion(bf16[16,2,4,4,8]{0,4,3,2,1:T(8,128)(2,1)S(1)} %bitcast.136, bf16[16,4,4,8,64]{4,0,3,2,1:T(8,128)(2,1)S(1)} %multiply_convert_fusion, bf16[3,3,3,64,64]{4,3,2,1,0:T(8,128)(2,1)} %bitcast.142, f32[16,4,4,8,64]{4,0,3,2,1:T(8,128)S(1)} %convolution_multiply_fusion.4), kind=kOutput, calls=%fused_computation.20 | convolution fusion | flops 298683776 | bytes 1029632 | tf_op jit(solution)/shard_map/transpose | solution.py:147
  83.6 4.0 %convolution_multiply_fusion.5 = f32[3,3,3,64,64]{4,3,2,1,0:T(8,128)S(1)} fusion(bf16[16,4,4,8,64]{4,0,3,2,1:T(8,128)(2,1)} %copy-done.3, f32[16,4,4,8,64]{4,0,3,2,1:T(8,128)S(1)} %convolution_multiply_fusion.4), kind=kOutput, calls=%fused_computation.16 | convolution fusion | flops 289124352 | bytes 1228800 | tf_op jit(solution)/shard_map/transpose | solution.py:147
  89.2 1.2 all_to_all.33
  90.4 7.4 %all-to-all-start.2 = ((f32[32,1,4716]{2,1,0:T(1,128)}), f32[32,1,4716]{2,1,0:T(1,128)S(1)}, u32[]{:S(2)}, u32[]{:S(2)}) async-start(f32[32,1,4716]{2,1,0:T(1,128)} %all_to_all.33), calls=%async_computation.2 | async-start | bytes 1212416 | tf_op jit(solution)/shard_map/all_to_all | solution.py:68
  99.2 18.4 %all-to-all-done.2 = f32[32,1,4716]{2,1,0:T(1,128)S(1)} async-done(((f32[32,1,4716]{2,1,0:T(1,128)}), f32[32,1,4716]{2,1,0:T(1,128)S(1)}, u32[]{:S(2)}, u32[]{:S(2)}) %all-to-all-start.2) | async-done | bytes 603680 | tf_op jit(solution)/shard_map/all_to_all | solution.py:68
  117.6 4.7 %all-to-all-start.1 = ((f32[8,2,2]{1,2,0:T(2,128)}), f32[8,2,2]{1,2,0:T(2,128)S(1)}, u32[]{:S(2)}, u32[]{:S(2)}) async-start(f32[8,2,2]{1,2,0:T(2,128)} %copy.89), calls=%async_computation.1 | async-start | bytes 16384 | tf_op jit(solution)/shard_map/all_to_all | solution.py:263
  123.5 3.5 %all-to-all-done.1 = f32[8,2,2]{1,2,0:T(2,128)S(1)} async-done(((f32[8,2,2]{1,2,0:T(2,128)}), f32[8,2,2]{1,2,0:T(2,128)S(1)}, u32[]{:S(2)}, u32[]{:S(2)}) %all-to-all-start.1) | async-done | bytes 160 | tf_op jit(solution)/shard_map/all_to_all | solution.py:263
  127.0 1.0 broadcast_in_dim.48
  128.0 4.7 %all-to-all-start.3 = ((f32[32,1,3692]{2,1,0:T(1,128)}), f32[32,1,3692]{2,1,0:T(1,128)S(1)}, u32[]{:S(2)}, u32[]{:S(2)}) async-start(f32[32,1,3692]{2,1,0:T(1,128)} %broadcast_in_dim.48), calls=%async_computation.3 | async-start | bytes 950272 | tf_op jit(solution)/shard_map/all_to_all | solution.py:58
  134.8 14.9 %all-to-all-done.3 = f32[32,1,3692]{2,1,0:T(1,128)S(1)} async-done(((f32[32,1,3692]{2,1,0:T(1,128)}), f32[32,1,3692]{2,1,0:T(1,128)S(1)}, u32[]{:S(2)}, u32[]{:S(2)}) %all-to-all-start.3) | async-done | bytes 472608 | tf_op jit(solution)/shard_map/all_to_all | solution.py:58
  153.6 0.9 copy.97
  154.5 2.1 %broadcast_in_dim_reshape_reshape.3 = f32[1,27,64,64]{3,2,1,0:T(8,128)} reshape(f32[32,3456]{1,0:T(8,128)} %slice.240) | data formatting | bytes 884736 | tf_op jit(solution)/shard_map/broadcast_in_dim;reshape;reshape | solution.py:292
  159.0 24.1 %all-gather.2.cloned.1.call-done = bf16[512,2048]{1,0:T(8,128)(2,1)} async-done(((bf16[16,2048]{1,0:T(8,128)(2,1)}), bf16[512,2048]{1,0:T(8,128)(2,1)}) %all-gather.2.cloned.1.call-update) | async-done | bytes 2097168 | tf_op jit(solution)/shard_map/all_gather | solution.py:274
  183.1 2.3 %multiply_reduce_fusion.1 = (f32[64]{0:T(128)S(1)}, f32[64,2048]{1,0:T(8,128)S(1)}) fusion(bf16[512,64]{1,0:T(8,128)(2,1)} %reshape.320, bf16[512,2048]{1,0:T(8,128)(2,1)} %all-gather.2.cloned.1.call-done), kind=kOutput, calls=%fused_computation.34 | convolution fusion | flops 134610880 | bytes 2687232 | tf_op jit(solution)/shard_map/dot_general | solution.py:272
  185.4 1.9 fusion.15
  (129 shorter events, 34.9 us)
Async XLA Ops:
  7.2 37.2 %copy-start = (f32[3,8,16,128]{3,2,1,0:T(8,128)S(1)}, f32[3,8,16,128]{3,2,1,0:T(8,128)}, u32[]{:S(2)}) copy-start(f32[3,8,16,128]{3,2,1,0:T(8,128)} %param.18) | copy-start | bytes 589828
  7.2 47.2 %copy-start.7 = (bf16[1,54,64]{2,1,0:T(8,128)(2,1)S(1)}, bf16[1,54,64]{2,1,0:T(8,128)(2,1)}, u32[]{:S(2)}) copy-start(bf16[1,54,64]{2,1,0:T(8,128)(2,1)} %param.21) | copy-start | bytes 20740
  8.6 27.6 %collective-permute-start.2 = (f32[3,1,16,128]{3,2,1,0:T(8,128)}, f32[3,1,16,128]{3,2,1,0:T(8,128)}, u32[]{:S(2)}, u32[]{:S(2)}) collective-permute-start(f32[3,1,16,128]{3,2,1,0:T(8,128)} %get-tuple-element.102), channel_id=1, source_target_pairs={{0,32},{32,64},{64,96},{96,128},{128,160},{160,192},{192,224},{224... | collective-permute-start | bytes 73736 | tf_op jit(solution)/shard_map/ppermute | solution.py:34
  10.1 26.9 %collective-permute-start.3 = (f32[3,1,16,128]{3,2,1,0:T(8,128)}, f32[3,1,16,128]{3,2,1,0:T(8,128)}, u32[]{:S(2)}, u32[]{:S(2)}) collective-permute-start(f32[3,1,16,128]{3,2,1,0:T(8,128)} %get-tuple-element.101), channel_id=1, source_target_pairs={{32,0},{64,32},{96,64},{128,96},{160,128},{192,160},{224,192},{0,2... | collective-permute-start | bytes 73736 | tf_op jit(solution)/shard_map/ppermute | solution.py:35
  12.4 22.1 %collective-permute-start = (f32[3,8,1,128]{3,2,1,0:T(1,128)}, f32[3,8,1,128]{3,2,1,0:T(1,128)}, u32[]{:S(2)}, u32[]{:S(2)}) collective-permute-start(f32[3,8,1,128]{3,2,1,0:T(1,128)} %get-tuple-element.100), channel_id=1, source_target_pairs={{0,1},{1,2},{2,3},{3,4},{4,5},{5,6},{6,7},{7,8},{8,9},{9,10},{10,1... | collective-permute-start | bytes 36872 | tf_op jit(solution)/shard_map/ppermute | solution.py:34
  12.4 22.9 %collective-permute-start.1 = (f32[3,8,1,128]{3,2,1,0:T(1,128)}, f32[3,8,1,128]{3,2,1,0:T(1,128)}, u32[]{:S(2)}, u32[]{:S(2)}) collective-permute-start(f32[3,8,1,128]{3,2,1,0:T(1,128)} %get-tuple-element.99), channel_id=1, source_target_pairs={{1,0},{2,1},{3,2},{4,3},{5,4},{6,5},{7,6},{8,7},{9,8},{10,9},{11,1... | collective-permute-start | bytes 36872 | tf_op jit(solution)/shard_map/ppermute | solution.py:35
  20.9 13.4 %copy-start.13 = (pred[8]{0:T(512)(128)(4,1)}, pred[8]{0:T(512)(128)(4,1)S(1)}, u32[]{:S(2)}) copy-start(pred[8]{0:T(512)(128)(4,1)S(1)} %compare_and_fusion) | copy-start | bytes 28
  24.8 9.5 %copy-start.9 = (s32[1024]{0:T(1024)}, s32[1024]{0:T(1024)S(1)}, u32[]{:S(2)}) copy-start(s32[1024]{0:T(1024)S(1)} %pad_clamp_fusion) | copy-start | bytes 12292
  27.1 7.2 %copy-start.11 = (s32[8]{0:T(128)}, s32[8]{0:T(128)S(1)}, u32[]{:S(2)}) copy-start(s32[8]{0:T(128)S(1)} %multiply_add_fusion) | copy-start | bytes 100
  36.1 1.6 copy-start.2
  37.7 0.7 copy-start.1
  48.5 10.7 %all-to-all-start = ((bf16[8,2,259]{2,1,0:T(2,128)(2,1)}), bf16[8,2,259]{2,1,0:T(2,128)(2,1)S(1)}, u32[]{:S(2)}, u32[]{:S(2)}) async-start(bf16[8,2,259]{2,1,0:T(2,128)(2,1)} %pad_maximum_fusion.4), calls=%async_computation | async-start | bytes 24576 | tf_op jit(solution)/shard_map/all_to_all | solution.py:51
  60.6 4.0 %copy-start.5 = (bf16[16,256]{0,1:T(8,128)(2,1)}, bf16[16,256]{0,1:T(8,128)(2,1)S(1)}, u32[]{:S(2)}) copy-start(bf16[16,256]{0,1:T(8,128)(2,1)S(1)} %copy.85) | copy-start | bytes 24580
  64.8 5.7 %copy-start.8 = (bf16[1,2048,2]{1,2,0:T(2,128)(2,1)S(1)}, bf16[1,2048,2]{1,2,0:T(2,128)(2,1)}, u32[]{:S(2)}) copy-start(bf16[1,2048,2]{1,2,0:T(2,128)(2,1)} %param.24) | copy-start | bytes 24580
  64.8 5.8 %copy-start.10 = (f32[16]{0:T(128)S(1)}, f32[16]{0:T(128)}, u32[]{:S(2)}) copy-start(f32[16]{0:T(128)} %convert_reduce_fusion) | copy-start | bytes 196
  70.4 7.9 %copy-start.6 = (bf16[16,256]{0,1:T(8,128)(2,1)S(1)}, bf16[16,256]{0,1:T(8,128)(2,1)}, u32[]{:S(2)}) copy-start(bf16[16,256]{0,1:T(8,128)(2,1)} %copy-done.5) | copy-start | bytes 24580
  71.0 12.5 %copy-start.4 = (bf16[16,2048]{1,0:T(8,128)(2,1)}, bf16[16,2048]{1,0:T(8,128)(2,1)S(1)}, u32[]{:S(2)}) copy-start(bf16[16,2048]{1,0:T(8,128)(2,1)S(1)} %fusion.11) | copy-start | bytes 196612
  77.5 0.8 copy-start.3
  87.5 45.6 %copy-start.12 = (s32[8]{0:T(128)S(1)}, s32[8]{0:T(128)}, u32[]{:S(2)}) copy-start(s32[8]{0:T(128)} %copy-done.11) | copy-start | bytes 100
  90.4 27.2 %all-to-all-start.2 = ((f32[32,1,4716]{2,1,0:T(1,128)}), f32[32,1,4716]{2,1,0:T(1,128)S(1)}, u32[]{:S(2)}, u32[]{:S(2)}) async-start(f32[32,1,4716]{2,1,0:T(1,128)} %all_to_all.33), calls=%async_computation.2 | async-start | bytes 1212416 | tf_op jit(solution)/shard_map/all_to_all | solution.py:68
  97.8 85.3 %all-gather.2.cloned.1.call-start = ((), (), s32[]{:S(2)}) async-start(), calls=%async_computation.4 | async-start | bytes 2162688 | tf_op jit(solution)/shard_map/all_gather | solution.py:274
  117.6 9.4 %all-to-all-start.1 = ((f32[8,2,2]{1,2,0:T(2,128)}), f32[8,2,2]{1,2,0:T(2,128)S(1)}, u32[]{:S(2)}, u32[]{:S(2)}) async-start(f32[8,2,2]{1,2,0:T(2,128)} %copy.89), calls=%async_computation.1 | async-start | bytes 16384 | tf_op jit(solution)/shard_map/all_to_all | solution.py:263
  128.0 21.7 %all-to-all-start.3 = ((f32[32,1,3692]{2,1,0:T(1,128)}), f32[32,1,3692]{2,1,0:T(1,128)S(1)}, u32[]{:S(2)}, u32[]{:S(2)}) async-start(f32[32,1,3692]{2,1,0:T(1,128)} %broadcast_in_dim.48), calls=%async_computation.3 | async-start | bytes 950272 | tf_op jit(solution)/shard_map/all_to_all | solution.py:58
Sparse Core Ops, SparseCore 0:
  101.4 81.6 all-gather.1

commit v5 on v4

--- a/solution.py
+++ b/solution.py
@@ -51,6 +51,26 @@
     whole = lax.all_to_all(both, axis, split_axis=split_dim, concat_axis=concat_dim, tiled=True)
     tiles = jnp.split(whole, [sum(widths[:k]) for k in range(1, len(widths))], axis=along)
     return tuple((b.reshape(*whole.shape[:along], *a.shape[along:]) for a, b in zip(arrays, tiles)))
+
+
+def joined_along(tiles, dim):
+    lengths = list(tiles.shape[1:])
+    lengths[dim] *= tiles.shape[0]
+    return jnp.moveaxis(tiles, 0, dim).reshape(lengths)
+
+
+def gather_in_order(shard, axes, order):
+    tiles = shard
+    for k in order:
+        tiles = lax.all_gather(tiles, axes[k])
+    done = order[::-1]
+    back = [done.index(k) for k in range(len(axes))]
+    tiles = tiles.transpose(*back, *range(len(axes), tiles.ndim))
+    return tiles.reshape(-1, *shard.shape)
+
+
+def gathered_by_axis(shard, axes, order, dim):
+    return joined_along(gather_in_order(shard, axes, order), dim)
 
 
 def from_everyone(shard, axis):
@@ -271,7 +291,7 @@
     grad_hidden = (
         jnp.dot(
             columns_here.T,
-            lax.all_gather(delta_three, STREAM, axis=0, tiled=True),
+            gathered_by_axis(delta_three, STREAM, (1, 0, 2), 0),
             preferred_element_type=jnp.float32,
         )
         * dense_scale

time: 197 us -> 171 us (0.87)
  waiting for transfers between devices: 66.4 us -> 41.9 us
  blocking collectives: 0 us -> 7.62 us
  other arithmetic: 18.7 us -> 13.8 us
  matrix products: 33.2 us -> 30.5 us
    all_to_all x1, waiting for transfers between devices: 14.9 us -> 1.08 us  [from_everyone(): return lax.all_to_all(copies, axis, split_axis=0, concat_axis=0, tiled=True)]
    all_gather x0 -> x1, blocking collectives: none -> 7.62 us  [gather_in_order(): tiles = lax.all_gather(tiles, axes[k])]
    all_to_all x1, waiting for transfers between devices: 18.4 us -> 11.4 us  [owner_sums(): lax.all_to_all(both, axis, split_axis=0, concat_axis=0, tiled=True)]
    all_gather x1 -> x2, waiting for transfers between devices: 24.1 us -> 21.1 us  [gather_in_order(): tiles = lax.all_gather(tiles, axes[k])]
    unnamed x34 -> x30, local copies, waits for them, and re-layouts: 4.23 us -> 2.75 us
  transfers between devices with their start and end apart: 9 -> 10, of which waited for: 5 -> 6; matrix products, arithmetic and copies ran while one was open for 17% -> 17% of each run, Pallas kernels for 0% -> 0%
where the time goes in v5:
time: 171 us; the launch traced here: 169 us
  waiting for transfers between devices  41.9 us (25%)
  starting transfers between devices  32.1 us (19%)
  matrix products  30.5 us (18%)
  local copies, waits for them, and re-layouts  27.3 us (16%)
  between operations  15.3 us (9%)
  other arithmetic  13.8 us (8%)
  blocking collectives  7.62 us (4%)
    all_gather x2, waiting for transfers between devices, gather_in_order(): tiles = lax.all_gather(tiles, axes[k])  21.1 us
    all_to_all x1, waiting for transfers between devices, owner_sums(): lax.all_to_all(both, axis, split_axis=0, concat_axis=0, tiled=True)  11.4 us
    transpose x2, matrix products, conv_filter(): return jnp.moveaxis(taps, 0, 3)  8.18 us
    ppermute x2, starting transfers between devices, extended(): lax.ppermute(first, axis, [(b, a) for a, b in up])  7.98 us
    all_gather x1, blocking collectives, gather_in_order(): tiles = lax.all_gather(tiles, axes[k])  7.62 us
    all_to_all x1, starting transfers between devices, owner_sums(): lax.all_to_all(both, axis, split_axis=0, concat_axis=0, tiled=True)  7.28 us
    all_to_all x1, starting transfers between devices, in_one_piece(): lax.all_to_all(both, axis, split_axis=split_dim, concat_axis=concat_dim,...  5.89 us
    dot_general x1, matrix products, forward_back(): jnp.dot(delta_three, w_hidden.T, preferred_element_type=jnp.float32)  5.65 us
  transfers between devices with their start and end apart: 10, of which 6 were waited for; matrix products, arithmetic and copies ran while one was open for 17% of the time, Pallas kernels for 0%

profile of v5, /device:TPU:2, one launch (start us, length us, event | category | flops | bytes accessed | tf_op | source)
XLA Modules:
  0.0 168.6 jit_solution(950964300961894074)
XLA Ops:
  7.9 1.5 collective-permute-start.2
  10.3 1.0 fusion.45
  11.3 7.1 %collective-permute-start.1 = (f32[3,8,1,128]{3,2,1,0:T(1,128)S(1)}, f32[3,8,1,128]{3,2,1,0:T(1,128)S(1)}, u32[]{:S(2)}, u32[]{:S(2)}) collective-permute-start(f32[3,8,1,128]{3,2,1,0:T(1,128)S(1)} %get-tuple-element.99), channel_id=1, source_target_pairs={{1,0},{2,1},{3,2},{4,3},{5,4},{6,5},{7,6},{8,7},{9,8},{10,9},{11,1... | collective-permute-start | bytes 36872 | tf_op jit(solution)/shard_map/ppermute | solution.py:35
  19.8 1.6 slice_bitcast_fusion.2
  22.2 1.5 fusion.22
  26.0 1.4 convolution_bitcast_fusion.1
  27.4 1.5 convolution_bitcast_fusion
  28.9 1.2 reshape.310
  35.1 2.2 %reshape.313 = f32[2,2,4,4,4,16,8]{6,5,4,3,2,1,0:T(8,128)S(1)} reshape(f32[2,8,16,128]{3,2,1,0:T(8,128)} %pad_maximum_fusion.1) | data formatting | bytes 262144 | tf_op jit(solution)/shard_map/reshape | solution.py:257
  40.5 1.8 %fusion.19 = f32[3,8,16,128]{3,2,1,0:T(8,128)} fusion(f32[3,8,16,128]{3,2,1,0:T(8,128)S(1)} %copy-done, f32[3,8,16,256]{3,2,1,0:T(8,128)S(1)} %convolution_bitcast_fusion, f32[3,16,16,128]{3,2,1,0:T(8,128)S(1)} %bitcast.141, f32[3,8,32,128]{3,2,1,0:T(8,128)S(1)} %convolution_bitcast_fusion.1, f32[3,8,16,128]{3,2,1,0:T(8,128)} %copy-done.1, ...), kind=kLoop, calls=%fused_computation.44 | loop fusion | flops 589824 | bytes 1769472 | tf_op jit(solution)/shard_map/add | solution.py:253
  44.6 5.9 %all-to-all-start = ((bf16[8,2,259]{2,1,0:T(2,128)(2,1)}), bf16[8,2,259]{2,1,0:T(2,128)(2,1)S(1)}, u32[]{:S(2)}, u32[]{:S(2)}) async-start(bf16[8,2,259]{2,1,0:T(2,128)(2,1)} %pad_maximum_fusion.4), calls=%async_computation | async-start | bytes 24576 | tf_op jit(solution)/shard_map/all_to_all | solution.py:51
  50.5 4.8 %all-to-all-done = bf16[8,2,259]{2,1,0:T(2,128)(2,1)S(1)} async-done(((bf16[8,2,259]{2,1,0:T(2,128)(2,1)}), bf16[8,2,259]{2,1,0:T(2,128)(2,1)S(1)}, u32[]{:S(2)}, u32[]{:S(2)}) %all-to-all-start) | async-done | bytes 8320 | tf_op jit(solution)/shard_map/all_to_all | solution.py:51
  56.5 3.1 %fusion.14 = (f32[16,4,4,8,64]{4,0,3,2,1:T(8,128)S(1)}, f32[16,4,4,8,64]{4,0,3,2,1:T(8,128)S(1)}) fusion(bf16[3,3,3,64,64]{4,3,2,1,0:T(8,128)(2,1)} %bitcast.151, f32[16,4,4,8,64]{4,0,3,2,1:T(8,128)S(1)} %convolution_multiply_fusion.4), kind=kOutput, calls=%fused_computation.28 | convolution fusion | flops 289669120 | bytes 1794048 | tf_op jit(solution)/shard_map/conv_general_dilated | solution.py:156
  60.5 4.6 %multiply_convert_fusion.3 = (bf16[16,2048]{1,0:T(8,128)(2,1)S(1)}, f32[16,2048]{1,0:T(8,128)S(1)}) fusion(bf16[16,2048]{1,0:T(8,128)(2,1)S(1)} %convert_element_type.112, bf16[1,2048,2048]{2,1,0:T(8,128)(2,1)} %param.23), kind=kOutput, calls=%fused_computation.54 | convolution fusion | flops 134414336 | bytes 8650752 | tf_op jit(solution)/shard_map/dot_general | solution.py:185
  65.7 5.6 %fusion.8 = f32[16,2048]{1,0:T(8,128)S(1)} fusion(bf16[16,2048]{1,0:T(8,128)(2,1)S(1)} %fusion.11, bf16[1,2048,2048]{2,1,0:T(8,128)(2,1)} %param.23), kind=kOutput, calls=%fused_computation.9 | convolution fusion | flops 134250496 | bytes 8585216 | tf_op jit(solution)/shard_map/dot_general | solution.py:193
  72.1 5.2 %convolution_multiply_fusion.6 = f32[3,3,3,2,64]{4,3,2,1,0:T(2,128)S(1)} fusion(bf16[16,2,4,4,8]{0,4,3,2,1:T(8,128)(2,1)S(1)} %bitcast.146, bf16[16,4,4,8,64]{4,0,3,2,1:T(8,128)(2,1)S(1)} %multiply_convert_fusion, bf16[3,3,3,64,64]{4,3,2,1,0:T(8,128)(2,1)} %bitcast.152, f32[16,4,4,8,64]{4,0,3,2,1:T(8,128)S(1)} %convolution_multiply_fusion.4), kind=kOutput, calls=%fused_computation.20 | convolution fusion | flops 298683776 | bytes 1029632 | tf_op jit(solution)/shard_map/transpose | solution.py:167
  77.4 2.9 %convolution_multiply_fusion.5 = f32[3,3,3,64,64]{4,3,2,1,0:T(8,128)S(1)} fusion(bf16[16,4,4,8,64]{4,0,3,2,1:T(8,128)(2,1)S(1)} %multiply_convert_fusion, f32[16,4,4,8,64]{4,0,3,2,1:T(8,128)S(1)} %convolution_multiply_fusion.4), kind=kOutput, calls=%fused_computation.16 | convolution fusion | flops 289124352 | bytes 1228800 | tf_op jit(solution)/shard_map/transpose | solution.py:167
  81.9 1.2 all_to_all.33
  83.1 7.3 %all-to-all-start.2 = ((f32[32,1,4716]{2,1,0:T(1,128)}), f32[32,1,4716]{2,1,0:T(1,128)S(1)}, u32[]{:S(2)}, u32[]{:S(2)}) async-start(f32[32,1,4716]{2,1,0:T(1,128)} %all_to_all.33), calls=%async_computation.2 | async-start | bytes 1212416 | tf_op jit(solution)/shard_map/all_to_all | solution.py:88
  90.5 7.6 %all-gather = bf16[32,2048]{1,0:T(8,128)(2,1)} all-gather(bf16[16,2048]{1,0:T(8,128)(2,1)S(1)} %fusion.11), channel_id=2, replica_groups=mesh['wall'=8,'stream_0'=8,'stream_1'=2,'stream_2'=2] {'stream_1'}, dimensions={0}, use_global_device_ids=true | all-gather | bytes 196608 | tf_op jit(solution)/shard_map/all_gather | solution.py:65
  98.8 11.4 %all-to-all-done.2 = f32[32,1,4716]{2,1,0:T(1,128)S(1)} async-done(((f32[32,1,4716]{2,1,0:T(1,128)}), f32[32,1,4716]{2,1,0:T(1,128)S(1)}, u32[]{:S(2)}, u32[]{:S(2)}) %all-to-all-start.2) | async-done | bytes 603680 | tf_op jit(solution)/shard_map/all_to_all | solution.py:88
  110.2 4.7 %all-to-all-start.1 = ((f32[8,2,2]{1,2,0:T(2,128)}), f32[8,2,2]{1,2,0:T(2,128)S(1)}, u32[]{:S(2)}, u32[]{:S(2)}) async-start(f32[8,2,2]{1,2,0:T(2,128)} %copy.91), calls=%async_computation.1 | async-start | bytes 16384 | tf_op jit(solution)/shard_map/all_to_all | solution.py:283
  116.2 3.5 %all-to-all-done.1 = f32[8,2,2]{1,2,0:T(2,128)S(1)} async-done(((f32[8,2,2]{1,2,0:T(2,128)}), f32[8,2,2]{1,2,0:T(2,128)S(1)}, u32[]{:S(2)}, u32[]{:S(2)}) %all-to-all-start.1) | async-done | bytes 160 | tf_op jit(solution)/shard_map/all_to_all | solution.py:283
  119.7 1.0 broadcast_in_dim.48
  120.7 4.7 %all-to-all-start.3 = ((f32[32,1,3692]{2,1,0:T(1,128)}), f32[32,1,3692]{2,1,0:T(1,128)S(1)}, u32[]{:S(2)}, u32[]{:S(2)}) async-start(f32[32,1,3692]{2,1,0:T(1,128)} %broadcast_in_dim.48), calls=%async_computation.3 | async-start | bytes 950272 | tf_op jit(solution)/shard_map/all_to_all | solution.py:78
  125.4 15.1 %all-gather.6.cloned.1.call-done = bf16[16,16,2048]{2,1,0:T(8,128)(2,1)} async-done(((bf16[2,16,2048]{2,1,0:T(8,128)(2,1)}), bf16[16,16,2048]{2,1,0:T(8,128)(2,1)}) %all-gather.6.cloned.1.call-update) | async-done | bytes 1048592 | tf_op jit(solution)/shard_map/all_gather | solution.py:65
  142.5 1.1 all-to-all-done.3
  147.5 0.9 copy.100
  148.4 2.1 %broadcast_in_dim_reshape_reshape.3 = f32[1,27,64,64]{3,2,1,0:T(8,128)} reshape(f32[32,3456]{1,0:T(8,128)} %slice.240) | data formatting | bytes 884736 | tf_op jit(solution)/shard_map/broadcast_in_dim;reshape;reshape | solution.py:312
  151.4 6.0 %all-gather.8.cloned.1.call-done = bf16[16,2,16,2048]{3,2,1,0:T(8,128)(2,1)} async-done(((bf16[8,2,16,2048]{3,2,1,0:T(8,128)(2,1)}), bf16[16,2,16,2048]{3,2,1,0:T(8,128)(2,1)}) %all-gather.8.cloned.1.call-update) | async-done | bytes 2097168 | tf_op jit(solution)/shard_map/all_gather | solution.py:65
  157.4 1.8 %copy.97 = bf16[8,2,2,16,2048]{4,3,2,1,0:T(8,128)(2,1)S(1)} copy(bf16[8,2,2,16,2048]{4,3,1,0,2:T(8,128)(2,1)} %bitcast.136) | data formatting | bytes 4194304 | tf_op jit(solution)/shard_map/transpose | solution.py:68
  159.8 1.9 %fusion.15 = f32[1,64,2048]{2,1,0:T(8,128)} fusion(f32[64,2048]{1,0:T(8,128)S(1)} %get-tuple-element.110, f32[64]{0:T(128)S(1)} %add_sqrt_fusion, bf16[1,2048,2048]{2,1,0:T(8,128)(2,1)} %param.23, s32[]{:T(128)S(6)} %select_n.37), kind=kLoop, calls=%fused_computation.33 | loop fusion | flops 524288 | bytes 1310980 | tf_op jit(solution)/shard_map/broadcast_in_dim | solution.py:300
  (131 shorter events, 30.0 us)
Async XLA Ops:
  7.9 25.7 %collective-permute-start.2 = (f32[3,1,16,128]{3,2,1,0:T(8,128)S(1)}, f32[3,1,16,128]{3,2,1,0:T(8,128)S(1)}, u32[]{:S(2)}, u32[]{:S(2)}) collective-permute-start(f32[3,1,16,128]{3,2,1,0:T(8,128)S(1)} %get-tuple-element.102), channel_id=1, source_target_pairs={{0,32},{32,64},{64,96},{96,128},{128,160},{160,192},{192,224},{224... | collective-permute-start | bytes 73736 | tf_op jit(solution)/shard_map/ppermute | solution.py:34
  9.4 24.3 %collective-permute-start.3 = (f32[3,1,16,128]{3,2,1,0:T(8,128)S(1)}, f32[3,1,16,128]{3,2,1,0:T(8,128)S(1)}, u32[]{:S(2)}, u32[]{:S(2)}) collective-permute-start(f32[3,1,16,128]{3,2,1,0:T(8,128)S(1)} %get-tuple-element.101), channel_id=1, source_target_pairs={{32,0},{64,32},{96,64},{128,96},{160,128},{192,160},{224,192},{0,2... | collective-permute-start | bytes 73736 | tf_op jit(solution)/shard_map/ppermute | solution.py:35
  11.2 22.2 %collective-permute-start = (f32[3,8,1,128]{3,2,1,0:T(1,128)S(1)}, f32[3,8,1,128]{3,2,1,0:T(1,128)S(1)}, u32[]{:S(2)}, u32[]{:S(2)}) collective-permute-start(f32[3,8,1,128]{3,2,1,0:T(1,128)S(1)} %get-tuple-element.100), channel_id=1, source_target_pairs={{0,1},{1,2},{2,3},{3,4},{4,5},{5,6},{6,7},{7,8},{8,9},{9,10},{10,1... | collective-permute-start | bytes 36872 | tf_op jit(solution)/shard_map/ppermute | solution.py:34
  11.3 22.2 %collective-permute-start.1 = (f32[3,8,1,128]{3,2,1,0:T(1,128)S(1)}, f32[3,8,1,128]{3,2,1,0:T(1,128)S(1)}, u32[]{:S(2)}, u32[]{:S(2)}) collective-permute-start(f32[3,8,1,128]{3,2,1,0:T(1,128)S(1)} %get-tuple-element.99), channel_id=1, source_target_pairs={{1,0},{2,1},{3,2},{4,3},{5,4},{6,5},{7,6},{8,7},{9,8},{10,9},{11,1... | collective-permute-start | bytes 36872 | tf_op jit(solution)/shard_map/ppermute | solution.py:35
  19.8 12.0 %copy-start.11 = (pred[8]{0:T(512)(128)(4,1)}, pred[8]{0:T(512)(128)(4,1)S(1)}, u32[]{:S(2)}) copy-start(pred[8]{0:T(512)(128)(4,1)S(1)} %compare_and_fusion) | copy-start | bytes 28
  23.7 7.5 %copy-start.8 = (s32[1024]{0:T(1024)}, s32[1024]{0:T(1024)S(1)}, u32[]{:S(2)}) copy-start(s32[1024]{0:T(1024)S(1)} %pad_clamp_fusion) | copy-start | bytes 12292
  26.0 6.7 %copy-start.9 = (s32[8]{0:T(128)}, s32[8]{0:T(128)S(1)}, u32[]{:S(2)}) copy-start(s32[8]{0:T(128)S(1)} %multiply_add_fusion) | copy-start | bytes 100
  33.7 0.7 copy-start.2
  33.7 0.7 copy-start.1
  35.1 5.4 %copy-start = (f32[3,8,16,128]{3,2,1,0:T(8,128)S(1)}, f32[3,8,16,128]{3,2,1,0:T(8,128)}, u32[]{:S(2)}) copy-start(f32[3,8,16,128]{3,2,1,0:T(8,128)} %param.18) | copy-start | bytes 589828
  37.2 13.2 %copy-start.6 = (bf16[1,54,64]{2,1,0:T(8,128)(2,1)S(1)}, bf16[1,54,64]{2,1,0:T(8,128)(2,1)}, u32[]{:S(2)}) copy-start(bf16[1,54,64]{2,1,0:T(8,128)(2,1)} %param.21) | copy-start | bytes 20740
  44.6 10.7 %all-to-all-start = ((bf16[8,2,259]{2,1,0:T(2,128)(2,1)}), bf16[8,2,259]{2,1,0:T(2,128)(2,1)S(1)}, u32[]{:S(2)}, u32[]{:S(2)}) async-start(bf16[8,2,259]{2,1,0:T(2,128)(2,1)} %pad_maximum_fusion.4), calls=%async_computation | async-start | bytes 24576 | tf_op jit(solution)/shard_map/all_to_all | solution.py:51
  55.3 4.4 %copy-start.5 = (bf16[16,259]{1,0:T(8,128)(2,1)}, bf16[16,259]{1,0:T(8,128)(2,1)S(1)}, u32[]{:S(2)}) copy-start(bf16[16,259]{1,0:T(8,128)(2,1)S(1)} %all_to_all.29) | copy-start | bytes 24868
  59.7 0.7 slice-start
  60.5 4.6 %copy-start.7 = (bf16[1,2048,2]{1,2,0:T(2,128)(2,1)S(1)}, bf16[1,2048,2]{1,2,0:T(2,128)(2,1)}, u32[]{:S(2)}) copy-start(bf16[1,2048,2]{1,2,0:T(2,128)(2,1)} %param.24) | copy-start | bytes 24580
  83.1 27.1 %all-to-all-start.2 = ((f32[32,1,4716]{2,1,0:T(1,128)}), f32[32,1,4716]{2,1,0:T(1,128)S(1)}, u32[]{:S(2)}, u32[]{:S(2)}) async-start(f32[32,1,4716]{2,1,0:T(1,128)} %all_to_all.33), calls=%async_computation.2 | async-start | bytes 1212416 | tf_op jit(solution)/shard_map/all_to_all | solution.py:88
  90.4 50.0 %all-gather.6.cloned.1.call-start = ((), (), s32[]{:S(2)}) async-start(), calls=%async_computation.4 | async-start | bytes 1179648 | tf_op jit(solution)/shard_map/all_gather | solution.py:65
  110.2 9.5 %all-to-all-start.1 = ((f32[8,2,2]{1,2,0:T(2,128)}), f32[8,2,2]{1,2,0:T(2,128)S(1)}, u32[]{:S(2)}, u32[]{:S(2)}) async-start(f32[8,2,2]{1,2,0:T(2,128)} %copy.91), calls=%async_computation.1 | async-start | bytes 16384 | tf_op jit(solution)/shard_map/all_to_all | solution.py:283
  114.9 26.0 %copy-start.10 = (s32[8]{0:T(128)S(1)}, s32[8]{0:T(128)}, u32[]{:S(2)}) copy-start(s32[8]{0:T(128)} %copy-done.9) | copy-start | bytes 100
  120.7 22.9 %all-to-all-start.3 = ((f32[32,1,3692]{2,1,0:T(1,128)}), f32[32,1,3692]{2,1,0:T(1,128)S(1)}, u32[]{:S(2)}, u32[]{:S(2)}) async-start(f32[32,1,3692]{2,1,0:T(1,128)} %broadcast_in_dim.48), calls=%async_computation.3 | async-start | bytes 950272 | tf_op jit(solution)/shard_map/all_to_all | solution.py:78
  125.3 32.1 %all-gather.8.cloned.1.call-start = ((), (), s32[]{:S(2)}) async-start(), calls=%async_computation.5 | async-start | bytes 3145728 | tf_op jit(solution)/shard_map/all_gather | solution.py:65
  147.5 3.1 %copy-start.4 = (f32[118,64]{1,0:T(8,128)S(1)}, f32[118,64]{1,0:T(8,128)}, u32[]{:S(2)}) copy-start(f32[118,64]{1,0:T(8,128)} %slice.213) | copy-start | bytes 90628
  157.4 1.8 %copy-start.3 = (bf16[512,64]{1,0:T(8,128)(2,1)S(1)}, bf16[512,64]{1,0:T(8,128)(2,1)}, u32[]{:S(2)}) copy-start(bf16[512,64]{1,0:T(8,128)(2,1)} %reshape.320) | copy-start | bytes 196612
Sparse Core Ops, SparseCore 0:
  98.2 42.1 all-gather.5
  142.3 15.1 all-gather.7

commit v6 on v5

--- a/solution.py
+++ b/solution.py
@@ -59,9 +59,9 @@
     return jnp.moveaxis(tiles, 0, dim).reshape(lengths)
 
 
-def gather_in_order(shard, axes, order):
-    tiles = shard
-    for k in order:
+def gather_in_order(shard, axes, order, started=None, stages=0):
+    tiles = shard if started is None else started
+    for k in order[stages:]:
         tiles = lax.all_gather(tiles, axes[k])
     done = order[::-1]
     back = [done.index(k) for k in range(len(axes))]
@@ -69,8 +69,8 @@
     return tiles.reshape(-1, *shard.shape)
 
 
-def gathered_by_axis(shard, axes, order, dim):
-    return joined_along(gather_in_order(shard, axes, order), dim)
+def gathered_by_axis(shard, axes, order, dim, started=None, stages=0):
+    return joined_along(gather_in_order(shard, axes, order, started, stages), dim)
 
 
 def from_everyone(shard, axis):
@@ -167,7 +167,7 @@
     return jnp.moveaxis(taps, 0, 3)
 
 
-def forward_back(patches, aim_rows, valid, k_first, k_second, w_hidden, w_out):
+def forward_back(patches, aim_rows, valid, k_first, k_second, w_hidden, w_out, early):
     batch = patches.shape[0]
     channels = k_second.shape[-1]
     inputs = patches.reshape(batch, 2, PY, PX, PZ).transpose(0, 2, 3, 4, 1)
@@ -190,6 +190,7 @@
     delta_three = (
         jnp.dot(error, w_out.astype(jnp.float32).T, precision=highest) * scale_four * silu_slope(pre_three)
     ).astype(jnp.bfloat16)
+    delta_three, started = lax.optimization_barrier((delta_three, early(delta_three)))
     back_feat = jnp.dot(delta_three, w_hidden.T, preferred_element_type=jnp.float32) * scale_three
     back_grid = back_feat.reshape(batch, PY // 2, 1, PX // 2, 1, PZ, channels)
     spread_back = jnp.broadcast_to(back_grid, (batch, PY // 2, 2, PX // 2, 2, PZ, channels)).reshape(pre_two.shape) * 0.25
@@ -199,7 +200,7 @@
     back_one = conv_taps(delta_two, mirrored)
     delta_one = (back_one * scale_two * silu_slope(pre_one)).astype(jnp.bfloat16)
     grad_one = (conv_filter(inputs, delta_one) * scale_one).reshape(54, channels)
-    return (pred, grad_one, grad_two, grad_out, features, delta_three)
+    return (pred, grad_one, grad_two, grad_out, features, delta_three, started)
 
 
 def row_update(weight, grad):
@@ -277,8 +278,10 @@
     recv_rows, recv_aims, recv_valid = in_one_piece(
         (send_rows, send_aims, send_valid), "wall", 0, 0, 1
     )
-    pred, grad_one, grad_two, grad_out, features, delta_three = forward_back(
-        recv_rows, recv_aims, recv_valid, k_first[0], k_second[0], w_hidden[0], w_out[0]
+    gather_order = (1, 0, 2)
+    pred, grad_one, grad_two, grad_out, features, delta_three, started = forward_back(
+        recv_rows, recv_aims, recv_valid, k_first[0], k_second[0], w_hidden[0], w_out[0],
+        lambda delta: lax.all_gather(delta, STREAM[gather_order[0]]),
     )
     back = lax.all_to_all(pred, "wall", split_axis=0, concat_axis=0, tiled=True)
     stress_local = jnp.dot(select.T, back, precision=highest)
@@ -287,11 +290,13 @@
     dense_scale = 1.0 / math.sqrt(1.0 * FEATS)
     small = jnp.concatenate([grad_one.ravel(), grad_out.ravel()])
     tiles = features.reshape(features.shape[0], flow_count, -1).transpose(1, 0, 2)
+    started = lax.all_gather(started, STREAM[gather_order[1]])
+    started, grad_two, small, tiles = lax.optimization_barrier((started, grad_two, small, tiles))
     grad_share, small_part, columns_here = owner_sums(grad_two.reshape(-1, CH), small, tiles, STREAM)
     grad_hidden = (
         jnp.dot(
             columns_here.T,
-            gathered_by_axis(delta_three, STREAM, (1, 0, 2), 0),
+            gathered_by_axis(delta_three, STREAM, gather_order, 0, started, 2),
             preferred_element_type=jnp.float32,
         )
         * dense_scale

time: 171 us -> 191 us (1.12)
  waiting for transfers between devices: 41.9 us -> 63.8 us
    all_gather x0 -> x1, waiting for transfers between devices: none -> 21.7 us  [body(): started = lax.all_gather(started, STREAM[gather_order[1]])]
    all_gather x2 -> x1, waiting for transfers between devices: 21.1 us -> 0.01 us  [gather_in_order(): tiles = lax.all_gather(tiles, axes[k])]
    all_to_all x1, waiting for transfers between devices: 1.08 us -> 14.1 us  [from_everyone(): return lax.all_to_all(copies, axis, split_axis=0, concat_axis=0, tiled=True)]
    all_to_all x1, waiting for transfers between devices: 11.4 us -> 19.1 us  [owner_sums(): lax.all_to_all(both, axis, split_axis=0, concat_axis=0, tiled=True)]
  transfers between devices with their start and end apart: 10 -> 10, of which waited for: 6 -> 5; matrix products, arithmetic and copies ran while one was open for 17% -> 21% of each run, Pallas kernels for 0% -> 0%
where the time goes in v6:
time: 191 us; the launch traced here: 189 us
  waiting for transfers between devices  63.8 us (33%)
  starting transfers between devices  32.3 us (17%)
  matrix products  29.1 us (15%)
  local copies, waits for them, and re-layouts  26.7 us (14%)
  between operations  15.4 us (8%)
  other arithmetic  14.7 us (8%)
  blocking collectives  6.55 us (3%)
    all_gather x1, waiting for transfers between devices, body(): started = lax.all_gather(started, STREAM[gather_order[1]])  21.7 us
    all_to_all x1, waiting for transfers between devices, owner_sums(): lax.all_to_all(both, axis, split_axis=0, concat_axis=0, tiled=True)  19.1 us
    all_to_all x1, waiting for transfers between devices, from_everyone(): return lax.all_to_all(copies, axis, split_axis=0, concat_axis=0, tiled=True)  14.1 us
    ppermute x2, starting transfers between devices, extended(): lax.ppermute(first, axis, [(b, a) for a, b in up])  7.9 us
    all_to_all x1, starting transfers between devices, owner_sums(): lax.all_to_all(both, axis, split_axis=0, concat_axis=0, tiled=True)  7.04 us
    transpose x2, matrix products, conv_filter(): return jnp.moveaxis(taps, 0, 3)  6.93 us
    all_gather x1, blocking collectives, body(): lax.all_gather(delta, STREAM[gather_order[0]])  6.55 us
    all_to_all x1, starting transfers between devices, in_one_piece(): lax.all_to_all(both, axis, split_axis=split_dim, concat_axis=concat_dim,...  5.88 us
  transfers between devices with their start and end apart: 10, of which 5 were waited for; matrix products, arithmetic and copies ran while one was open for 21% of the time, Pallas kernels for 0%

profile of v6, /device:TPU:2, one launch (start us, length us, event | category | flops | bytes accessed | tf_op | source)
XLA Modules:
  0.0 188.6 jit_solution(14176507087532092567)
XLA Ops:
  7.2 1.4 fusion.46
  8.6 1.5 collective-permute-start.2
  10.9 1.6 fusion.45
  12.4 7.1 %collective-permute-start.1 = (f32[3,8,1,128]{3,2,1,0:T(1,128)S(1)}, f32[3,8,1,128]{3,2,1,0:T(1,128)}, u32[]{:S(2)}, u32[]{:S(2)}) collective-permute-start(f32[3,8,1,128]{3,2,1,0:T(1,128)S(1)} %get-tuple-element.111), channel_id=1, source_target_pairs={{1,0},{2,1},{3,2},{4,3},{5,4},{6,5},{7,6},{8,7},{9,8},{10,9},{11,1... | collective-permute-start | bytes 36872 | tf_op jit(solution)/shard_map/ppermute | solution.py:35
  19.6 1.6 slice_bitcast_fusion.2
  23.3 1.5 convolution_bitcast_fusion
  24.8 1.5 fusion.22
  26.3 1.2 convolution_bitcast_fusion.1
  27.5 1.2 reshape.311
  36.9 2.1 %reshape.314 = f32[2,2,4,4,4,16,8]{6,5,4,3,2,1,0:T(8,128)S(1)} reshape(f32[2,8,16,128]{3,2,1,0:T(8,128)} %pad_maximum_fusion.1) | data formatting | bytes 262144 | tf_op jit(solution)/shard_map/reshape | solution.py:258
  41.4 0.9 convolution_convert_fusion.1
  42.3 1.8 fusion.19
  46.4 5.9 %all-to-all-start = ((bf16[8,2,259]{2,1,0:T(2,128)(2,1)}), bf16[8,2,259]{2,1,0:T(2,128)(2,1)S(1)}, u32[]{:S(2)}, u32[]{:S(2)}) async-start(bf16[8,2,259]{2,1,0:T(2,128)(2,1)} %pad_maximum_fusion.4), calls=%async_computation | async-start | bytes 24576 | tf_op jit(solution)/shard_map/all_to_all | solution.py:51
  52.3 4.8 %all-to-all-done = bf16[8,2,259]{2,1,0:T(2,128)(2,1)S(1)} async-done(((bf16[8,2,259]{2,1,0:T(2,128)(2,1)}), bf16[8,2,259]{2,1,0:T(2,128)(2,1)S(1)}, u32[]{:S(2)}, u32[]{:S(2)}) %all-to-all-start) | async-done | bytes 8320 | tf_op jit(solution)/shard_map/all_to_all | solution.py:51
  58.4 3.1 %fusion.14 = (f32[16,4,4,8,64]{4,0,3,2,1:T(8,128)S(1)}, f32[16,4,4,8,64]{4,0,3,2,1:T(8,128)S(1)}) fusion(bf16[3,3,3,64,64]{4,3,2,1,0:T(8,128)(2,1)} %bitcast.150, f32[16,4,4,8,64]{4,0,3,2,1:T(8,128)S(1)} %convolution_multiply_fusion.4), kind=kOutput, calls=%fused_computation.28 | convolution fusion | flops 289669120 | bytes 1794048 | tf_op jit(solution)/shard_map/conv_general_dilated | solution.py:156
  62.3 4.6 %multiply_convert_fusion.3 = (bf16[16,2048]{1,0:T(8,128)(2,1)S(1)}, f32[16,2048]{1,0:T(8,128)S(1)}) fusion(bf16[16,2048]{1,0:T(8,128)(2,1)S(1)} %convert_element_type.108, bf16[1,2048,2048]{2,1,0:T(8,128)(2,1)} %param.23), kind=kOutput, calls=%fused_computation.53 | convolution fusion | flops 134414336 | bytes 8650752 | tf_op jit(solution)/shard_map/dot_general | solution.py:185
  67.4 6.6 %all-gather = bf16[32,2048]{1,0:T(8,128)(2,1)} all-gather(bf16[16,2048]{1,0:T(8,128)(2,1)S(1)} %fusion.11), channel_id=2, replica_groups=mesh['wall'=8,'stream_0'=8,'stream_1'=2,'stream_2'=2] {'stream_1'}, dimensions={0}, use_global_device_ids=true | all-gather | bytes 196608 | tf_op jit(solution)/shard_map/all_gather | solution.py:284
  73.9 5.7 %fusion.8 = f32[16,2048]{1,0:T(8,128)S(1)} fusion(bf16[16,2048]{1,0:T(8,128)(2,1)S(1)} %fusion.11, bf16[1,2048,2048]{2,1,0:T(8,128)(2,1)} %param.23), kind=kOutput, calls=%fused_computation.9 | convolution fusion | flops 134250496 | bytes 8585216 | tf_op jit(solution)/shard_map/dot_general | solution.py:194
  82.0 4.2 %convolution_multiply_fusion.6 = f32[3,3,3,2,64]{4,3,2,1,0:T(2,128)S(1)} fusion(bf16[16,2,4,4,8]{0,4,3,2,1:T(8,128)(2,1)S(1)} %bitcast.145, bf16[16,4,4,8,64]{4,0,3,2,1:T(8,128)(2,1)S(1)} %multiply_convert_fusion, bf16[3,3,3,64,64]{4,3,2,1,0:T(8,128)(2,1)S(1)} %bitcast.152, f32[16,4,4,8,64]{4,0,3,2,1:T(8,128)S(1)} %convolution_multiply_fusion.4), kind=kOutput, calls=%fused_computation.20 | convolution fusion | flops 298683776 | bytes 1029632 | tf_op jit(solution)/shard_map/transpose | solution.py:167
  86.3 2.7 %convolution_multiply_fusion.5 = f32[3,3,3,64,64]{4,3,2,1,0:T(8,128)S(1)} fusion(bf16[16,4,4,8,64]{4,0,3,2,1:T(8,128)(2,1)S(1)} %multiply_convert_fusion, f32[16,4,4,8,64]{4,0,3,2,1:T(8,128)S(1)} %convolution_multiply_fusion.4), kind=kOutput, calls=%fused_computation.16 | convolution fusion | flops 289124352 | bytes 1228800 | tf_op jit(solution)/shard_map/transpose | solution.py:167
  89.0 21.7 %all-gather.6.cloned.1.call-done = bf16[16,16,2048]{2,1,0:T(8,128)(2,1)} async-done(((bf16[2,16,2048]{2,1,0:T(8,128)(2,1)}), bf16[16,16,2048]{2,1,0:T(8,128)(2,1)}) %all-gather.6.cloned.1.call-update) | async-done | bytes 1048592 | tf_op jit(solution)/shard_map/all_gather | solution.py:293
  111.3 1.2 all_to_all.33
  112.6 7.0 %all-to-all-start.2 = ((f32[32,1,4716]{2,1,0:T(1,128)}), f32[32,1,4716]{2,1,0:T(1,128)S(1)}, u32[]{:S(2)}, u32[]{:S(2)}) async-start(f32[32,1,4716]{2,1,0:T(1,128)} %all_to_all.33), calls=%async_computation.2 | async-start | bytes 1212416 | tf_op jit(solution)/shard_map/all_to_all | solution.py:88
  120.3 19.1 %all-to-all-done.2 = f32[32,1,4716]{2,1,0:T(1,128)S(1)} async-done(((f32[32,1,4716]{2,1,0:T(1,128)}), f32[32,1,4716]{2,1,0:T(1,128)S(1)}, u32[]{:S(2)}, u32[]{:S(2)}) %all-to-all-start.2) | async-done | bytes 603680 | tf_op jit(solution)/shard_map/all_to_all | solution.py:88
  139.4 4.8 %all-to-all-start.1 = ((f32[8,2,2]{1,2,0:T(2,128)}), f32[8,2,2]{1,2,0:T(2,128)S(1)}, u32[]{:S(2)}, u32[]{:S(2)}) async-start(f32[8,2,2]{1,2,0:T(2,128)} %copy.91), calls=%async_computation.1 | async-start | bytes 16384 | tf_op jit(solution)/shard_map/all_to_all | solution.py:286
  145.5 3.4 %all-to-all-done.1 = f32[8,2,2]{1,2,0:T(2,128)S(1)} async-done(((f32[8,2,2]{1,2,0:T(2,128)}), f32[8,2,2]{1,2,0:T(2,128)S(1)}, u32[]{:S(2)}, u32[]{:S(2)}) %all-to-all-start.1) | async-done | bytes 160 | tf_op jit(solution)/shard_map/all_to_all | solution.py:286
  149.0 1.0 broadcast_in_dim.48
  150.0 5.1 %all-to-all-start.3 = ((f32[32,1,3692]{2,1,0:T(1,128)}), f32[32,1,3692]{2,1,0:T(1,128)S(1)}, u32[]{:S(2)}, u32[]{:S(2)}) async-start(f32[32,1,3692]{2,1,0:T(1,128)} %broadcast_in_dim.48), calls=%async_computation.3 | async-start | bytes 950272 | tf_op jit(solution)/shard_map/all_to_all | solution.py:78
  158.0 14.1 %all-to-all-done.3 = f32[32,1,3692]{2,1,0:T(1,128)S(1)} async-done(((f32[32,1,3692]{2,1,0:T(1,128)}), f32[32,1,3692]{2,1,0:T(1,128)S(1)}, u32[]{:S(2)}, u32[]{:S(2)}) %all-to-all-start.3) | async-done | bytes 472608 | tf_op jit(solution)/shard_map/all_to_all | solution.py:78
  173.7 1.1 broadcast_in_dim_reshape_reshape.3
  177.5 1.8 copy.97
  179.9 1.9 %fusion.15 = f32[1,64,2048]{2,1,0:T(8,128)} fusion(f32[64,2048]{1,0:T(8,128)S(1)} %get-tuple-element.122, f32[64]{0:T(128)S(1)} %add_sqrt_fusion, bf16[1,2048,2048]{2,1,0:T(8,128)(2,1)} %param.23, s32[]{:T(128)S(6)} %select_n.37), kind=kLoop, calls=%fused_computation.33 | loop fusion | flops 524288 | bytes 1310980 | tf_op jit(solution)/shard_map/broadcast_in_dim | solution.py:305
  (148 shorter events, 29.9 us)
Async XLA Ops:
  7.2 19.1 %copy-start = (f32[3,8,16,128]{3,2,1,0:T(8,128)S(1)}, f32[3,8,16,128]{3,2,1,0:T(8,128)}, u32[]{:S(2)}) copy-start(f32[3,8,16,128]{3,2,1,0:T(8,128)} %param.18) | copy-start | bytes 589828
  8.6 25.4 %collective-permute-start.2 = (f32[3,1,16,128]{3,2,1,0:T(8,128)}, f32[3,1,16,128]{3,2,1,0:T(8,128)}, u32[]{:S(2)}, u32[]{:S(2)}) collective-permute-start(f32[3,1,16,128]{3,2,1,0:T(8,128)} %get-tuple-element.114), channel_id=1, source_target_pairs={{0,32},{32,64},{64,96},{96,128},{128,160},{160,192},{192,224},{224... | collective-permute-start | bytes 73736 | tf_op jit(solution)/shard_map/ppermute | solution.py:34
  10.1 24.7 %collective-permute-start.3 = (f32[3,1,16,128]{3,2,1,0:T(8,128)}, f32[3,1,16,128]{3,2,1,0:T(8,128)}, u32[]{:S(2)}, u32[]{:S(2)}) collective-permute-start(f32[3,1,16,128]{3,2,1,0:T(8,128)} %get-tuple-element.113), channel_id=1, source_target_pairs={{32,0},{64,32},{96,64},{128,96},{160,128},{192,160},{224,192},{0,2... | collective-permute-start | bytes 73736 | tf_op jit(solution)/shard_map/ppermute | solution.py:35
  12.4 19.9 %collective-permute-start = (f32[3,8,1,128]{3,2,1,0:T(1,128)}, f32[3,8,1,128]{3,2,1,0:T(1,128)}, u32[]{:S(2)}, u32[]{:S(2)}) collective-permute-start(f32[3,8,1,128]{3,2,1,0:T(1,128)} %get-tuple-element.112), channel_id=1, source_target_pairs={{0,1},{1,2},{2,3},{3,4},{4,5},{5,6},{6,7},{7,8},{8,9},{9,10},{10,1... | collective-permute-start | bytes 36872 | tf_op jit(solution)/shard_map/ppermute | solution.py:34
  12.4 20.7 %collective-permute-start.1 = (f32[3,8,1,128]{3,2,1,0:T(1,128)S(1)}, f32[3,8,1,128]{3,2,1,0:T(1,128)}, u32[]{:S(2)}, u32[]{:S(2)}) collective-permute-start(f32[3,8,1,128]{3,2,1,0:T(1,128)S(1)} %get-tuple-element.111), channel_id=1, source_target_pairs={{1,0},{2,1},{3,2},{4,3},{5,4},{6,5},{7,6},{8,7},{9,8},{10,9},{11,1... | collective-permute-start | bytes 36872 | tf_op jit(solution)/shard_map/ppermute | solution.py:35
  23.3 7.4 %copy-start.20 = (pred[8]{0:T(512)(128)(4,1)}, pred[8]{0:T(512)(128)(4,1)S(1)}, u32[]{:S(2)}) copy-start(pred[8]{0:T(512)(128)(4,1)S(1)} %compare_and_fusion) | copy-start | bytes 28
  26.3 3.5 %copy-start.16 = (s32[1,8,1]{1,2,0:T(1,128)S(1)}, s32[1,8,1]{1,2,0:T(1,128)}, u32[]{:S(2)}) copy-start(s32[1,8,1]{1,2,0:T(1,128)} %param.20) | copy-start | bytes 100
  29.8 5.8 %copy-start.11 = (s32[1024]{0:T(1024)}, s32[1024]{0:T(1024)S(1)}, u32[]{:S(2)}) copy-start(s32[1024]{0:T(1024)S(1)} %pad_clamp_fusion) | copy-start | bytes 12292
  30.1 5.5 %copy-start.18 = (s32[8]{0:T(128)}, s32[8]{0:T(128)S(1)}, u32[]{:S(2)}) copy-start(s32[8]{0:T(128)S(1)} %multiply_add_fusion) | copy-start | bytes 100
  34.0 1.6 copy-start.2
  35.5 0.7 copy-start.1
  39.0 13.3 %copy-start.7 = (bf16[1,54,64]{2,1,0:T(8,128)(2,1)S(1)}, bf16[1,54,64]{2,1,0:T(8,128)(2,1)}, u32[]{:S(2)}) copy-start(bf16[1,54,64]{2,1,0:T(8,128)(2,1)} %param.21) | copy-start | bytes 20740
  46.4 10.7 %all-to-all-start = ((bf16[8,2,259]{2,1,0:T(2,128)(2,1)}), bf16[8,2,259]{2,1,0:T(2,128)(2,1)S(1)}, u32[]{:S(2)}, u32[]{:S(2)}) async-start(bf16[8,2,259]{2,1,0:T(2,128)(2,1)} %pad_maximum_fusion.4), calls=%async_computation | async-start | bytes 24576 | tf_op jit(solution)/shard_map/all_to_all | solution.py:51
  52.3 58.4 %all-gather.6.cloned.1.call-start = ((), (), s32[]{:S(2)}) async-start(), calls=%async_computation.4 | async-start | bytes 1179648 | tf_op jit(solution)/shard_map/all_gather | solution.py:293
  57.1 4.4 %copy-start.6 = (bf16[16,259]{1,0:T(8,128)(2,1)}, bf16[16,259]{1,0:T(8,128)(2,1)S(1)}, u32[]{:S(2)}) copy-start(bf16[16,259]{1,0:T(8,128)(2,1)S(1)} %all_to_all.29) | copy-start | bytes 24868
  57.3 9.7 %copy-start.14 = (f32[16]{0:T(128)}, f32[16]{0:T(128)S(1)}, u32[]{:S(2)}) copy-start(f32[16]{0:T(128)S(1)} %convert_reduce_fusion) | copy-start | bytes 196
  57.5 4.1 %copy-start.4 = (bf16[16,256]{0,1:T(8,128)(2,1)}, bf16[16,256]{0,1:T(8,128)(2,1)S(1)}, u32[]{:S(2)}) copy-start(bf16[16,256]{0,1:T(8,128)(2,1)S(1)} %copy.87) | copy-start | bytes 24580
  61.5 0.7 slice-start
  62.3 4.6 %copy-start.9 = (bf16[1,2048,2]{1,2,0:T(2,128)(2,1)S(1)}, bf16[1,2048,2]{1,2,0:T(2,128)(2,1)}, u32[]{:S(2)}) copy-start(bf16[1,2048,2]{1,2,0:T(2,128)(2,1)} %param.24) | copy-start | bytes 24580
  67.1 12.8 %copy-start.12 = (f32[16,2]{0,1:T(2,128)}, f32[16,2]{0,1:T(2,128)S(1)}, u32[]{:S(2)}) copy-start(f32[16,2]{0,1:T(2,128)S(1)} %convolution_multiply_fusion.7) | copy-start | bytes 388
  73.9 6.0 %copy-start.15 = (f32[16]{0:T(128)S(1)}, f32[16]{0:T(128)}, u32[]{:S(2)}) copy-start(f32[16]{0:T(128)} %copy-done.14) | copy-start | bytes 196
  80.9 0.8 copy-start.5
  80.9 1.0 copy-start.17
  110.9 8.7 %copy-start.13 = (f32[16,2]{0,1:T(2,128)S(1)}, f32[16,2]{0,1:T(2,128)}, u32[]{:S(2)}) copy-start(f32[16,2]{0,1:T(2,128)} %copy-done.12) | copy-start | bytes 388
  112.6 26.8 %all-to-all-start.2 = ((f32[32,1,4716]{2,1,0:T(1,128)}), f32[32,1,4716]{2,1,0:T(1,128)S(1)}, u32[]{:S(2)}, u32[]{:S(2)}) async-start(f32[32,1,4716]{2,1,0:T(1,128)} %all_to_all.33), calls=%async_computation.2 | async-start | bytes 1212416 | tf_op jit(solution)/shard_map/all_to_all | solution.py:88
  139.4 9.6 %all-to-all-start.1 = ((f32[8,2,2]{1,2,0:T(2,128)}), f32[8,2,2]{1,2,0:T(2,128)S(1)}, u32[]{:S(2)}, u32[]{:S(2)}) async-start(f32[8,2,2]{1,2,0:T(2,128)} %copy.91), calls=%async_computation.1 | async-start | bytes 16384 | tf_op jit(solution)/shard_map/all_to_all | solution.py:286
  144.2 11.7 %copy-start.10 = (bf16[1,2048,2]{1,2,0:T(2,128)(2,1)S(1)}, bf16[1,2048,2]{1,2,0:T(2,128)(2,1)}, u32[]{:S(2)}) copy-start(bf16[1,2048,2]{1,2,0:T(2,128)(2,1)} %param.24) | copy-start | bytes 24580
  144.3 12.0 %copy-start.19 = (s32[8]{0:T(128)S(1)}, s32[8]{0:T(128)}, u32[]{:S(2)}) copy-start(s32[8]{0:T(128)} %copy-done.18) | copy-start | bytes 100
  150.0 22.1 %all-to-all-start.3 = ((f32[32,1,3692]{2,1,0:T(1,128)}), f32[32,1,3692]{2,1,0:T(1,128)S(1)}, u32[]{:S(2)}, u32[]{:S(2)}) async-start(f32[32,1,3692]{2,1,0:T(1,128)} %broadcast_in_dim.48), calls=%async_computation.3 | async-start | bytes 950272 | tf_op jit(solution)/shard_map/all_to_all | solution.py:78
  155.1 22.4 %all-gather.8.cloned.1.call-start = ((), (), s32[]{:S(2)}) async-start(), calls=%async_computation.5 | async-start | bytes 3145728 | tf_op jit(solution)/shard_map/all_gather | solution.py:65
  157.1 15.9 %copy-start.8 = (bf16[1,54,64]{2,1,0:T(8,128)(2,1)S(1)}, bf16[1,54,64]{2,1,0:T(8,128)(2,1)}, u32[]{:S(2)}) copy-start(bf16[1,54,64]{2,1,0:T(8,128)(2,1)} %param.21) | copy-start | bytes 20740
  177.5 1.8 copy-start.3
Sparse Core Ops, SparseCore 0:
  74.1 36.5 all-gather.5
  157.8 16.1 all-gather.7

commit v7 on v5

--- a/solution.py
+++ b/solution.py
@@ -237,20 +237,6 @@
         .add(lift_half * above)
     )
     high_y = along_y[:, size_y:]
-    along_x = jnp.einsum("cyxz,wx->cywz", velocity, pair_x, precision=highest)
-    grad_x = (
-        along_x[:, :, :size_x]
-        .at[:, :, 0]
-        .add(-lift_half * left_face)
-        .at[:, :, size_x - 1]
-        .add(lift_half * right_face)
-    )
-    high_x = along_x[:, :, size_x:]
-    along_z = jnp.einsum("cyxz,wz->cyxw", velocity, pair_z, precision=highest)
-    grad_z = along_z[..., :size_z]
-    high_z = along_z[..., size_z:]
-    advect = velocity[0][None] * grad_x + velocity[1][None] * grad_y + velocity[2][None] * grad_z
-    new_field = velocity + time_step * (-advect - relax_rate * (high_x + high_y + high_z))
     rows_y, rows_x, rows_z = (size_y // PY, size_x // PX, size_z // PZ)
     tangent = jnp.stack([velocity[0], velocity[2]]).reshape(2, rows_y, PY, rows_x, PX, rows_z, PZ)
     blocks = tangent.transpose(1, 3, 5, 0, 2, 4, 6).reshape(-1, 2 * PY * PX * PZ)
@@ -271,9 +257,23 @@
         jnp.bfloat16
     )
     send_valid = jnp.sum(select, axis=1).astype(jnp.bfloat16)
-    new_field, send_rows, send_aims, send_valid = lax.optimization_barrier(
-        (new_field, send_rows, send_aims, send_valid)
-    )
+    left_face, right_face, send_rows, send_aims, send_valid = lax.optimization_barrier(
+        (left_face, right_face, send_rows, send_aims, send_valid)
+    )
+    along_x = jnp.einsum("cyxz,wx->cywz", velocity, pair_x, precision=highest)
+    grad_x = (
+        along_x[:, :, :size_x]
+        .at[:, :, 0]
+        .add(-lift_half * left_face)
+        .at[:, :, size_x - 1]
+        .add(lift_half * right_face)
+    )
+    high_x = along_x[:, :, size_x:]
+    along_z = jnp.einsum("cyxz,wz->cyxw", velocity, pair_z, precision=highest)
+    grad_z = along_z[..., :size_z]
+    high_z = along_z[..., size_z:]
+    advect = velocity[0][None] * grad_x + velocity[1][None] * grad_y + velocity[2][None] * grad_z
+    new_field = velocity + time_step * (-advect - relax_rate * (high_x + high_y + high_z))
     recv_rows, recv_aims, recv_valid = in_one_piece(
         (send_rows, send_aims, send_valid), "wall", 0, 0, 1
     )

time: 171 us -> 171 us (level)
  starting transfers between devices: 32.1 us -> 35.2 us
  matrix products: 30.5 us -> 28.3 us
    all_to_all x1, waiting for transfers between devices: 1.08 us -> 7.98 us  [from_everyone(): return lax.all_to_all(copies, axis, split_axis=0, concat_axis=0, tiled=True)]
    all_to_all x1, waiting for transfers between devices: 3.49 us -> 0.01 us  [body(): back = lax.all_to_all(pred, 'wall', split_axis=0, concat_axis=0, tiled=True)]
    scatter-add x2, local copies, waits for them, and re-layouts: 0.16 us -> 3.17 us  [body(): grad_x = along_x[:, :, :size_x].at[:, :, 0].add(-lift_half * left_face).a...]
    all_to_all x1, waiting for transfers between devices: 11.4 us -> 8.65 us  [owner_sums(): lax.all_to_all(both, axis, split_axis=0, concat_axis=0, tiled=True)]
    all_to_all x1, starting transfers between devices: 4.66 us -> 7.03 us  [from_everyone(): return lax.all_to_all(copies, axis, split_axis=0, concat_axis=0, tiled=True)]
  transfers between devices with their start and end apart: 10 -> 10, of which waited for: 6 -> 4; matrix products, arithmetic and copies ran while one was open for 17% -> 20% of each run, Pallas kernels for 0% -> 0%
where the time goes in v7:
time: 171 us; the launch traced here: 170 us
  waiting for transfers between devices  42.1 us (25%)
  starting transfers between devices  35.2 us (21%)
  matrix products  28.3 us (17%)
  local copies, waits for them, and re-layouts  27.9 us (16%)
  between operations  15.4 us (9%)
  other arithmetic  13.4 us (8%)
  blocking collectives  7.68 us (4%)
    all_gather x2, waiting for transfers between devices, gather_in_order(): tiles = lax.all_gather(tiles, axes[k])  20.6 us
    all_to_all x1, waiting for transfers between devices, owner_sums(): lax.all_to_all(both, axis, split_axis=0, concat_axis=0, tiled=True)  8.65 us
    transpose x2, matrix products, conv_filter(): return jnp.moveaxis(taps, 0, 3)  8.17 us
    all_to_all x1, waiting for transfers between devices, from_everyone(): return lax.all_to_all(copies, axis, split_axis=0, concat_axis=0, tiled=True)  7.98 us
    ppermute x2, starting transfers between devices, extended(): lax.ppermute(first, axis, [(b, a) for a, b in up])  7.98 us
    all_gather x1, blocking collectives, gather_in_order(): tiles = lax.all_gather(tiles, axes[k])  7.68 us
    all_to_all x1, starting transfers between devices, owner_sums(): lax.all_to_all(both, axis, split_axis=0, concat_axis=0, tiled=True)  7.42 us
    all_to_all x1, starting transfers between devices, from_everyone(): return lax.all_to_all(copies, axis, split_axis=0, concat_axis=0, tiled=True)  7.03 us
  transfers between devices with their start and end apart: 10, of which 4 were waited for; matrix products, arithmetic and copies ran while one was open for 20% of the time, Pallas kernels for 0%

profile of v7, /device:TPU:2, one launch (start us, length us, event | category | flops | bytes accessed | tf_op | source)
XLA Modules:
  0.0 169.9 jit_solution(10689999702392000829)
XLA Ops:
  7.9 1.5 collective-permute-start.2
  10.3 1.0 fusion.45
  11.3 7.1 %collective-permute-start.1 = (f32[3,8,1,128]{3,1,0,2:T(8,128)S(1)}, f32[3,8,1,128]{3,1,0,2:T(8,128)S(1)}, u32[]{:S(2)}, u32[]{:S(2)}) collective-permute-start(f32[3,8,1,128]{3,1,0,2:T(8,128)S(1)} %bitcast.159), channel_id=1, source_target_pairs={{1,0},{2,1},{3,2},{4,3},{5,4},{6,5},{7,6},{8,7},{9,8},{10,9},{11,1... | collective-permute-start | bytes 36872 | tf_op jit(solution)/shard_map/ppermute | solution.py:35
  19.8 0.9 fusion.44
  20.7 1.5 fusion.22
  24.4 1.2 reshape.314
  27.8 1.1 reshape.317
  31.1 5.9 %all-to-all-start = ((bf16[8,2,259]{2,1,0:T(2,128)(2,1)}), bf16[8,2,259]{2,1,0:T(2,128)(2,1)S(1)}, u32[]{:S(2)}, u32[]{:S(2)}) async-start(bf16[8,2,259]{2,1,0:T(2,128)(2,1)} %pad_maximum_fusion.4), calls=%async_computation | async-start | bytes 24576 | tf_op jit(solution)/shard_map/all_to_all | solution.py:51
  37.0 4.8 %all-to-all-done = bf16[8,2,259]{2,1,0:T(2,128)(2,1)S(1)} async-done(((bf16[8,2,259]{2,1,0:T(2,128)(2,1)}), bf16[8,2,259]{2,1,0:T(2,128)(2,1)S(1)}, u32[]{:S(2)}, u32[]{:S(2)}) %all-to-all-start) | async-done | bytes 8320 | tf_op jit(solution)/shard_map/all_to_all | solution.py:51
  42.2 0.9 convolution_multiply_fusion.4
  43.1 4.1 %fusion.14 = (f32[16,4,4,8,64]{4,0,3,2,1:T(8,128)S(1)}, f32[16,4,4,8,64]{4,0,3,2,1:T(8,128)}) fusion(bf16[3,3,3,64,64]{4,3,2,1,0:T(8,128)(2,1)} %bitcast.163, f32[16,4,4,8,64]{4,0,3,2,1:T(8,128)S(1)} %convolution_multiply_fusion.4), kind=kOutput, calls=%fused_computation.28 | convolution fusion | flops 289669120 | bytes 1794048 | tf_op jit(solution)/shard_map/conv_general_dilated | solution.py:156
  48.0 4.6 %multiply_convert_fusion.3 = (bf16[16,2048]{1,0:T(8,128)(2,1)S(1)}, f32[16,2048]{1,0:T(8,128)S(1)}) fusion(bf16[16,2048]{1,0:T(8,128)(2,1)S(1)} %convert_element_type.112, bf16[1,2048,2048]{2,1,0:T(8,128)(2,1)} %param.23), kind=kOutput, calls=%fused_computation.54 | convolution fusion | flops 134414336 | bytes 8650752 | tf_op jit(solution)/shard_map/dot_general | solution.py:185
  53.2 5.6 %fusion.8 = f32[16,2048]{1,0:T(8,128)S(1)} fusion(bf16[16,2048]{1,0:T(8,128)(2,1)S(1)} %fusion.11, bf16[1,2048,2048]{2,1,0:T(8,128)(2,1)} %param.23), kind=kOutput, calls=%fused_computation.9 | convolution fusion | flops 134250496 | bytes 8585216 | tf_op jit(solution)/shard_map/dot_general | solution.py:193
  60.5 5.2 %convolution_multiply_fusion.6 = f32[3,3,3,2,64]{4,3,2,1,0:T(2,128)S(1)} fusion(bf16[16,2,4,4,8]{0,4,3,2,1:T(8,128)(2,1)S(1)} %bitcast.152, bf16[16,4,4,8,64]{4,0,3,2,1:T(8,128)(2,1)S(1)} %multiply_convert_fusion, bf16[3,3,3,64,64]{4,3,2,1,0:T(8,128)(2,1)} %bitcast.164, f32[16,4,4,8,64]{4,0,3,2,1:T(8,128)S(1)} %convolution_multiply_fusion.4), kind=kOutput, calls=%fused_computation.20 | convolution fusion | flops 298683776 | bytes 1029632 | tf_op jit(solution)/shard_map/transpose | solution.py:167
  65.7 2.9 %convolution_multiply_fusion.5 = f32[3,3,3,64,64]{4,3,2,1,0:T(8,128)S(1)} fusion(bf16[16,4,4,8,64]{4,0,3,2,1:T(8,128)(2,1)S(1)} %multiply_convert_fusion, f32[16,4,4,8,64]{4,0,3,2,1:T(8,128)S(1)} %convolution_multiply_fusion.4), kind=kOutput, calls=%fused_computation.16 | convolution fusion | flops 289124352 | bytes 1228800 | tf_op jit(solution)/shard_map/transpose | solution.py:167
  70.3 1.2 all_to_all.33
  71.6 7.4 %all-to-all-start.2 = ((f32[32,1,4716]{2,1,0:T(1,128)}), f32[32,1,4716]{2,1,0:T(1,128)S(1)}, u32[]{:S(2)}, u32[]{:S(2)}) async-start(f32[32,1,4716]{2,1,0:T(1,128)} %all_to_all.33), calls=%async_computation.2 | async-start | bytes 1212416 | tf_op jit(solution)/shard_map/all_to_all | solution.py:88
  79.4 7.7 %all-gather = bf16[32,2048]{1,0:T(8,128)(2,1)} all-gather(bf16[16,2048]{1,0:T(8,128)(2,1)S(1)} %fusion.11), channel_id=2, replica_groups=mesh['wall'=8,'stream_0'=8,'stream_1'=2,'stream_2'=2] {'stream_1'}, dimensions={0}, use_global_device_ids=true | all-gather | bytes 196608 | tf_op jit(solution)/shard_map/all_gather | solution.py:65
  90.1 8.6 %all-to-all-done.2 = f32[32,1,4716]{2,1,0:T(1,128)S(1)} async-done(((f32[32,1,4716]{2,1,0:T(1,128)}), f32[32,1,4716]{2,1,0:T(1,128)S(1)}, u32[]{:S(2)}, u32[]{:S(2)}) %all-to-all-start.2) | async-done | bytes 603680 | tf_op jit(solution)/shard_map/all_to_all | solution.py:88
  98.8 5.2 %all-to-all-start.1 = ((f32[8,2,2]{1,2,0:T(2,128)}), f32[8,2,2]{1,2,0:T(2,128)}, u32[]{:S(2)}, u32[]{:S(2)}) async-start(f32[8,2,2]{1,2,0:T(2,128)} %copy.101), calls=%async_computation.1 | async-start | bytes 16384 | tf_op jit(solution)/shard_map/all_to_all | solution.py:283
  105.3 20.6 %all-gather.6.cloned.1.call-done = bf16[16,16,2048]{2,1,0:T(8,128)(2,1)} async-done(((bf16[2,16,2048]{2,1,0:T(8,128)(2,1)}), bf16[16,16,2048]{2,1,0:T(8,128)(2,1)}) %all-gather.6.cloned.1.call-update) | async-done | bytes 1048592 | tf_op jit(solution)/shard_map/all_gather | solution.py:65
  126.0 1.0 broadcast_in_dim.48
  127.0 7.0 %all-to-all-start.3 = ((f32[32,1,3692]{2,1,0:T(1,128)}), f32[32,1,3692]{2,1,0:T(1,128)S(1)}, u32[]{:S(2)}, u32[]{:S(2)}) async-start(f32[32,1,3692]{2,1,0:T(1,128)} %broadcast_in_dim.48), calls=%async_computation.3 | async-start | bytes 950272 | tf_op jit(solution)/shard_map/all_to_all | solution.py:78
  134.8 1.6 scatter-add.16
  136.3 0.9 slice_add_fusion.4
  137.3 1.6 scatter-add.19
  138.8 1.7 %fusion.19 = f32[3,8,16,128]{3,2,1,0:T(8,128)} fusion(f32[3,8,16,128]{3,2,1,0:T(8,128)S(1)} %copy-done, f32[3,8,16,256]{3,2,1,0:T(8,128)S(1)} %convolution_bitcast_fusion, f32[3,16,16,128]{3,2,1,0:T(8,128)S(1)} %bitcast.147, f32[3,8,32,128]{3,2,1,0:T(8,128)S(1)} %convolution_bitcast_fusion.1, f32[3,8,16,128]{3,2,1,0:T(8,128)S(1)} %fusion.27, ...), kind=kLoop, calls=%fused_computation.44 | loop fusion | flops 589824 | bytes 1769472 | tf_op jit(solution)/shard_map/add | solution.py:276
  143.0 8.0 %all-to-all-done.3 = f32[32,1,3692]{2,1,0:T(1,128)S(1)} async-done(((f32[32,1,3692]{2,1,0:T(1,128)}), f32[32,1,3692]{2,1,0:T(1,128)S(1)}, u32[]{:S(2)}, u32[]{:S(2)}) %all-to-all-start.3) | async-done | bytes 472608 | tf_op jit(solution)/shard_map/all_to_all | solution.py:78
  154.9 0.9 copy.110
  155.8 2.1 %broadcast_in_dim_reshape_reshape.3 = f32[1,27,64,64]{3,2,1,0:T(8,128)} reshape(f32[32,3456]{1,0:T(8,128)} %slice.240) | data formatting | bytes 884736 | tf_op jit(solution)/shard_map/broadcast_in_dim;reshape;reshape | solution.py:312
  158.8 1.8 %copy.107 = bf16[8,2,2,16,2048]{4,3,2,1,0:T(8,128)(2,1)S(1)} copy(bf16[8,2,2,16,2048]{4,3,1,0,2:T(8,128)(2,1)} %bitcast.142) | data formatting | bytes 4194304 | tf_op jit(solution)/shard_map/transpose | solution.py:68
  161.2 1.9 %fusion.15 = f32[1,64,2048]{2,1,0:T(8,128)} fusion(f32[64,2048]{1,0:T(8,128)S(1)} %get-tuple-element.112, f32[64]{0:T(128)S(1)} %add_sqrt_fusion, bf16[1,2048,2048]{2,1,0:T(8,128)(2,1)} %param.23, s32[]{:T(128)S(6)} %select_n.37), kind=kLoop, calls=%fused_computation.33 | loop fusion | flops 524288 | bytes 1310980 | tf_op jit(solution)/shard_map/broadcast_in_dim | solution.py:300
  (150 shorter events, 26.8 us)
Async XLA Ops:
  7.9 19.8 %collective-permute-start.2 = (f32[3,1,16,128]{3,2,1,0:T(8,128)S(1)}, f32[3,1,16,128]{3,2,1,0:T(8,128)S(1)}, u32[]{:S(2)}, u32[]{:S(2)}) collective-permute-start(f32[3,1,16,128]{3,2,1,0:T(8,128)S(1)} %get-tuple-element.104), channel_id=1, source_target_pairs={{0,32},{32,64},{64,96},{96,128},{128,160},{160,192},{192,224},{224... | collective-permute-start | bytes 73736 | tf_op jit(solution)/shard_map/ppermute | solution.py:34
  9.4 18.3 %collective-permute-start.3 = (f32[3,1,16,128]{3,2,1,0:T(8,128)S(1)}, f32[3,1,16,128]{3,2,1,0:T(8,128)S(1)}, u32[]{:S(2)}, u32[]{:S(2)}) collective-permute-start(f32[3,1,16,128]{3,2,1,0:T(8,128)S(1)} %get-tuple-element.103), channel_id=1, source_target_pairs={{32,0},{64,32},{96,64},{128,96},{160,128},{192,160},{224,192},{0,2... | collective-permute-start | bytes 73736 | tf_op jit(solution)/shard_map/ppermute | solution.py:35
  11.2 19.0 %collective-permute-start = (f32[3,8,1,128]{3,1,0,2:T(8,128)S(1)}, f32[3,8,1,128]{3,1,0,2:T(8,128)S(1)}, u32[]{:S(2)}, u32[]{:S(2)}) collective-permute-start(f32[3,8,1,128]{3,1,0,2:T(8,128)S(1)} %bitcast.160), channel_id=1, source_target_pairs={{0,1},{1,2},{2,3},{3,4},{4,5},{5,6},{6,7},{7,8},{8,9},{9,10},{10,1... | collective-permute-start | bytes 36872 | tf_op jit(solution)/shard_map/ppermute | solution.py:34
  11.3 18.9 %collective-permute-start.1 = (f32[3,8,1,128]{3,1,0,2:T(8,128)S(1)}, f32[3,8,1,128]{3,1,0,2:T(8,128)S(1)}, u32[]{:S(2)}, u32[]{:S(2)}) collective-permute-start(f32[3,8,1,128]{3,1,0,2:T(8,128)S(1)} %bitcast.159), channel_id=1, source_target_pairs={{1,0},{2,1},{3,2},{4,3},{5,4},{6,5},{7,6},{8,7},{9,8},{10,9},{11,1... | collective-permute-start | bytes 36872 | tf_op jit(solution)/shard_map/ppermute | solution.py:35
  24.4 5.5 %copy-start.19 = (s32[8]{0:T(128)}, s32[8]{0:T(128)S(1)}, u32[]{:S(2)}) copy-start(s32[8]{0:T(128)S(1)} %multiply_add_fusion) | copy-start | bytes 100
  27.8 9.2 %copy-start.8 = (bf16[1,54,64]{2,1,0:T(8,128)(2,1)S(1)}, bf16[1,54,64]{2,1,0:T(8,128)(2,1)}, u32[]{:S(2)}) copy-start(bf16[1,54,64]{2,1,0:T(8,128)(2,1)} %param.21) | copy-start | bytes 20740
  30.2 17.0 %copy-start.10 = (f32[3,8,1,128]{3,1,0,2:T(8,128)}, f32[3,8,1,128]{3,1,0,2:T(8,128)S(1)}, u32[]{:S(2)}) copy-start(f32[3,8,1,128]{3,1,0,2:T(8,128)S(1)} %collective-permute-done) | copy-start | bytes 36868
  30.2 17.0 %copy-start.12 = (f32[3,8,1,128]{3,1,0,2:T(8,128)}, f32[3,8,1,128]{3,1,0,2:T(8,128)S(1)}, u32[]{:S(2)}) copy-start(f32[3,8,1,128]{3,1,0,2:T(8,128)S(1)} %collective-permute-done.1) | copy-start | bytes 36868
  31.1 10.7 %all-to-all-start = ((bf16[8,2,259]{2,1,0:T(2,128)(2,1)}), bf16[8,2,259]{2,1,0:T(2,128)(2,1)S(1)}, u32[]{:S(2)}, u32[]{:S(2)}) async-start(bf16[8,2,259]{2,1,0:T(2,128)(2,1)} %pad_maximum_fusion.4), calls=%async_computation | async-start | bytes 24576 | tf_op jit(solution)/shard_map/all_to_all | solution.py:51
  41.8 5.3 %copy-start.7 = (bf16[16,259]{1,0:T(8,128)(2,1)}, bf16[16,259]{1,0:T(8,128)(2,1)S(1)}, u32[]{:S(2)}) copy-start(bf16[16,259]{1,0:T(8,128)(2,1)S(1)} %all_to_all.29) | copy-start | bytes 24868
  42.2 5.0 %copy-start.3 = (bf16[16,256]{0,1:T(8,128)(2,1)}, bf16[16,256]{0,1:T(8,128)(2,1)S(1)}, u32[]{:S(2)}) copy-start(bf16[16,256]{0,1:T(8,128)(2,1)S(1)} %copy.97) | copy-start | bytes 24580
  47.2 0.7 slice-start
  48.0 4.6 %copy-start.14 = (bf16[1,2048,2]{1,2,0:T(2,128)(2,1)S(1)}, bf16[1,2048,2]{1,2,0:T(2,128)(2,1)}, u32[]{:S(2)}) copy-start(bf16[1,2048,2]{1,2,0:T(2,128)(2,1)} %param.24) | copy-start | bytes 24580
  52.7 6.1 %copy-start.17 = (f32[16,2]{0,1:T(2,128)}, f32[16,2]{0,1:T(2,128)S(1)}, u32[]{:S(2)}) copy-start(f32[16,2]{0,1:T(2,128)S(1)} %convolution_multiply_fusion.7) | copy-start | bytes 388
  58.8 1.2 copy-start.1
  59.1 1.4 copy-start.4
  70.0 9.0 %copy-start.15 = (bf16[1,2048,2]{1,2,0:T(2,128)(2,1)S(1)}, bf16[1,2048,2]{1,2,0:T(2,128)(2,1)}, u32[]{:S(2)}) copy-start(bf16[1,2048,2]{1,2,0:T(2,128)(2,1)} %param.24) | copy-start | bytes 24580
  70.2 16.9 %copy-start = (f32[3,8,16,128]{3,2,1,0:T(8,128)S(1)}, f32[3,8,16,128]{3,2,1,0:T(8,128)}, u32[]{:S(2)}) copy-start(f32[3,8,16,128]{3,2,1,0:T(8,128)} %param.18) | copy-start | bytes 589828
  70.2 16.9 %copy-start.16 = (f32[32,16,1,1]{0,1,3,2:T(8,128)S(1)}, f32[32,16,1,1]{0,1,3,2:T(8,128)}, u32[]{:S(2)}) copy-start(f32[32,16,1,1]{0,1,3,2:T(8,128)} %constant.249) | copy-start | bytes 6148
  70.3 18.0 %copy-start.6 = (f32[256,128,1,1]{1,0,3,2:T(8,128)S(1)}, f32[256,128,1,1]{1,0,3,2:T(8,128)}, u32[]{:S(2)}) copy-start(f32[256,128,1,1]{1,0,3,2:T(8,128)} %constant.251) | copy-start | bytes 393220
  71.6 17.3 %copy-start.11 = (f32[3,8,1,128]{3,1,0,2:T(8,128)S(1)}, f32[3,8,1,128]{3,1,0,2:T(8,128)}, u32[]{:S(2)}) copy-start(f32[3,8,1,128]{3,1,0,2:T(8,128)} %copy-done.10) | copy-start | bytes 36868
  71.6 17.3 %copy-start.13 = (f32[3,8,1,128]{3,1,0,2:T(8,128)S(1)}, f32[3,8,1,128]{3,1,0,2:T(8,128)}, u32[]{:S(2)}) copy-start(f32[3,8,1,128]{3,1,0,2:T(8,128)} %copy-done.12) | copy-start | bytes 36868
  71.6 17.9 %copy-start.18 = (f32[16,2]{0,1:T(2,128)S(1)}, f32[16,2]{0,1:T(2,128)}, u32[]{:S(2)}) copy-start(f32[16,2]{0,1:T(2,128)} %copy-done.17) | copy-start | bytes 388
  71.6 27.2 %all-to-all-start.2 = ((f32[32,1,4716]{2,1,0:T(1,128)}), f32[32,1,4716]{2,1,0:T(1,128)S(1)}, u32[]{:S(2)}, u32[]{:S(2)}) async-start(f32[32,1,4716]{2,1,0:T(1,128)} %all_to_all.33), calls=%async_computation.2 | async-start | bytes 1212416 | tf_op jit(solution)/shard_map/all_to_all | solution.py:88
  79.0 46.9 %all-gather.6.cloned.1.call-start = ((), (), s32[]{:S(2)}) async-start(), calls=%async_computation.4 | async-start | bytes 1179648 | tf_op jit(solution)/shard_map/all_gather | solution.py:65
  98.8 27.2 %all-to-all-start.1 = ((f32[8,2,2]{1,2,0:T(2,128)}), f32[8,2,2]{1,2,0:T(2,128)}, u32[]{:S(2)}, u32[]{:S(2)}) async-start(f32[8,2,2]{1,2,0:T(2,128)} %copy.101), calls=%async_computation.1 | async-start | bytes 16384 | tf_op jit(solution)/shard_map/all_to_all | solution.py:283
  104.0 54.8 %all-gather.8.cloned.1.call-start = ((), (), s32[]{:S(2)}) async-start(), calls=%async_computation.5 | async-start | bytes 3145728 | tf_op jit(solution)/shard_map/all_gather | solution.py:65
  125.9 15.4 %copy-start.20 = (s32[8]{0:T(128)S(1)}, s32[8]{0:T(128)}, u32[]{:S(2)}) copy-start(s32[8]{0:T(128)} %copy-done.19) | copy-start | bytes 100
  127.0 24.0 %all-to-all-start.3 = ((f32[32,1,3692]{2,1,0:T(1,128)}), f32[32,1,3692]{2,1,0:T(1,128)S(1)}, u32[]{:S(2)}, u32[]{:S(2)}) async-start(f32[32,1,3692]{2,1,0:T(1,128)} %broadcast_in_dim.48), calls=%async_computation.3 | async-start | bytes 950272 | tf_op jit(solution)/shard_map/all_to_all | solution.py:78
  154.7 3.4 %copy-start.9 = (bf16[1,54,64]{2,1,0:T(8,128)(2,1)S(1)}, bf16[1,54,64]{2,1,0:T(8,128)(2,1)}, u32[]{:S(2)}) copy-start(bf16[1,54,64]{2,1,0:T(8,128)(2,1)} %param.21) | copy-start | bytes 20740
  154.9 3.1 %copy-start.5 = (f32[118,64]{1,0:T(8,128)S(1)}, f32[118,64]{1,0:T(8,128)}, u32[]{:S(2)}) copy-start(f32[118,64]{1,0:T(8,128)} %slice.213) | copy-start | bytes 90628
  158.8 1.8 %copy-start.2 = (bf16[512,64]{1,0:T(8,128)(2,1)S(1)}, bf16[512,64]{1,0:T(8,128)(2,1)}, u32[]{:S(2)}) copy-start(bf16[512,64]{1,0:T(8,128)(2,1)} %reshape.326) | copy-start | bytes 196612
Sparse Core Ops, SparseCore 0:
  87.2 38.6 all-gather.5
  127.7 14.3 all-gather.7

commit v8 on v7

--- a/solution.py
+++ b/solution.py
@@ -291,7 +291,7 @@
     grad_hidden = (
         jnp.dot(
             columns_here.T,
-            gathered_by_axis(delta_three, STREAM, (1, 0, 2), 0),
+            gathered_by_axis(delta_three, STREAM, (0, 1, 2), 0),
             preferred_element_type=jnp.float32,
         )
         * dense_scale

time: 171 us -> 203 us (1.19)
  blocking collectives: 7.68 us -> 38.5 us
    all_gather x1, blocking collectives: 7.68 us -> 38.5 us  [gather_in_order(): tiles = lax.all_gather(tiles, axes[k])]
    all_to_all x1, waiting for transfers between devices: 8.65 us -> 0.01 us  [owner_sums(): lax.all_to_all(both, axis, split_axis=0, concat_axis=0, tiled=True)]
    all_to_all x1, waiting for transfers between devices: 0.01 us -> 3.45 us  [body(): back = lax.all_to_all(pred, 'wall', split_axis=0, concat_axis=0, tiled=True)]
    all_gather x2, waiting for transfers between devices: 20.6 us -> 23.3 us  [gather_in_order(): tiles = lax.all_gather(tiles, axes[k])]
  transfers between devices with their start and end apart: 10 -> 10, of which waited for: 4 -> 4; matrix products, arithmetic and copies ran while one was open for 20% -> 16% of each run, Pallas kernels for 0% -> 0%
where the time goes in v8:
time: 203 us; the launch traced here: 201 us
  waiting for transfers between devices  41 us (20%)
  blocking collectives  38.5 us (19%)
  starting transfers between devices  36.8 us (18%)
  local copies, waits for them, and re-layouts  28.9 us (14%)
  matrix products  28.3 us (14%)
  between operations  15.4 us (8%)
  other arithmetic  12.1 us (6%)
    all_gather x1, blocking collectives, gather_in_order(): tiles = lax.all_gather(tiles, axes[k])  38.5 us
    all_gather x2, waiting for transfers between devices, gather_in_order(): tiles = lax.all_gather(tiles, axes[k])  23.3 us
    all_to_all x1, waiting for transfers between devices, from_everyone(): return lax.all_to_all(copies, axis, split_axis=0, concat_axis=0, tiled=True)  9.39 us
    all_to_all x1, starting transfers between devices, from_everyone(): return lax.all_to_all(copies, axis, split_axis=0, concat_axis=0, tiled=True)  8.86 us
    transpose x2, matrix products, conv_filter(): return jnp.moveaxis(taps, 0, 3)  8.17 us
    ppermute x2, starting transfers between devices, extended(): lax.ppermute(first, axis, [(b, a) for a, b in up])  7.98 us
    all_to_all x1, starting transfers between devices, owner_sums(): lax.all_to_all(both, axis, split_axis=0, concat_axis=0, tiled=True)  7.41 us
    all_to_all x1, starting transfers between devices, in_one_piece(): lax.all_to_all(both, axis, split_axis=split_dim, concat_axis=concat_dim,...  5.88 us
  transfers between devices with their start and end apart: 10, of which 4 were waited for; matrix products, arithmetic and copies ran while one was open for 16% of the time, Pallas kernels for 0%

profile of v8, /device:TPU:2, one launch (start us, length us, event | category | flops | bytes accessed | tf_op | source)
XLA Modules:
  0.0 200.9 jit_solution(13806253505400243977)
XLA Ops:
  7.9 1.5 collective-permute-start.2
  10.3 1.0 fusion.45
  11.3 7.1 %collective-permute-start.1 = (f32[3,8,1,128]{3,1,0,2:T(8,128)S(1)}, f32[3,8,1,128]{3,1,0,2:T(8,128)S(1)}, u32[]{:S(2)}, u32[]{:S(2)}) collective-permute-start(f32[3,8,1,128]{3,1,0,2:T(8,128)S(1)} %bitcast.159), channel_id=1, source_target_pairs={{1,0},{2,1},{3,2},{4,3},{5,4},{6,5},{7,6},{8,7},{9,8},{10,9},{11,1... | collective-permute-start | bytes 36872 | tf_op jit(solution)/shard_map/ppermute | solution.py:35
  19.8 0.9 fusion.44
  20.7 1.5 fusion.22
  24.4 1.2 reshape.314
  28.5 1.1 reshape.317
  31.8 5.9 %all-to-all-start = ((bf16[8,2,259]{2,1,0:T(2,128)(2,1)}), bf16[8,2,259]{2,1,0:T(2,128)(2,1)S(1)}, u32[]{:S(2)}, u32[]{:S(2)}) async-start(bf16[8,2,259]{2,1,0:T(2,128)(2,1)} %pad_maximum_fusion.4), calls=%async_computation | async-start | bytes 24576 | tf_op jit(solution)/shard_map/all_to_all | solution.py:51
  37.7 4.8 %all-to-all-done = bf16[8,2,259]{2,1,0:T(2,128)(2,1)S(1)} async-done(((bf16[8,2,259]{2,1,0:T(2,128)(2,1)}), bf16[8,2,259]{2,1,0:T(2,128)(2,1)S(1)}, u32[]{:S(2)}, u32[]{:S(2)}) %all-to-all-start) | async-done | bytes 8320 | tf_op jit(solution)/shard_map/all_to_all | solution.py:51
  42.8 0.9 convolution_multiply_fusion.4
  43.7 4.1 %fusion.14 = (f32[16,4,4,8,64]{4,0,3,2,1:T(8,128)S(1)}, f32[16,4,4,8,64]{4,0,3,2,1:T(8,128)}) fusion(bf16[3,3,3,64,64]{4,3,2,1,0:T(8,128)(2,1)} %bitcast.163, f32[16,4,4,8,64]{4,0,3,2,1:T(8,128)S(1)} %convolution_multiply_fusion.4), kind=kOutput, calls=%fused_computation.28 | convolution fusion | flops 289669120 | bytes 1794048 | tf_op jit(solution)/shard_map/conv_general_dilated | solution.py:156
  48.6 4.6 %multiply_convert_fusion.3 = (bf16[16,2048]{1,0:T(8,128)(2,1)S(1)}, f32[16,2048]{1,0:T(8,128)S(1)}) fusion(bf16[16,2048]{1,0:T(8,128)(2,1)S(1)} %convert_element_type.112, bf16[1,2048,2048]{2,1,0:T(8,128)(2,1)} %param.23), kind=kOutput, calls=%fused_computation.54 | convolution fusion | flops 134414336 | bytes 8650752 | tf_op jit(solution)/shard_map/dot_general | solution.py:185
  54.2 5.6 %fusion.8 = f32[16,2048]{1,0:T(8,128)S(1)} fusion(bf16[16,2048]{1,0:T(8,128)(2,1)S(1)} %fusion.11, bf16[1,2048,2048]{2,1,0:T(8,128)(2,1)} %param.23), kind=kOutput, calls=%fused_computation.9 | convolution fusion | flops 134250496 | bytes 8585216 | tf_op jit(solution)/shard_map/dot_general | solution.py:193
  61.5 5.2 %convolution_multiply_fusion.6 = f32[3,3,3,2,64]{4,3,2,1,0:T(2,128)S(1)} fusion(bf16[16,2,4,4,8]{0,4,3,2,1:T(8,128)(2,1)S(1)} %bitcast.152, bf16[16,4,4,8,64]{4,0,3,2,1:T(8,128)(2,1)S(1)} %multiply_convert_fusion, bf16[3,3,3,64,64]{4,3,2,1,0:T(8,128)(2,1)} %bitcast.164, f32[16,4,4,8,64]{4,0,3,2,1:T(8,128)S(1)} %convolution_multiply_fusion.4), kind=kOutput, calls=%fused_computation.20 | convolution fusion | flops 298683776 | bytes 1029632 | tf_op jit(solution)/shard_map/transpose | solution.py:167
  66.8 2.9 %convolution_multiply_fusion.5 = f32[3,3,3,64,64]{4,3,2,1,0:T(8,128)S(1)} fusion(bf16[16,4,4,8,64]{4,0,3,2,1:T(8,128)(2,1)S(1)} %multiply_convert_fusion, f32[16,4,4,8,64]{4,0,3,2,1:T(8,128)S(1)} %convolution_multiply_fusion.4), kind=kOutput, calls=%fused_computation.16 | convolution fusion | flops 289124352 | bytes 1228800 | tf_op jit(solution)/shard_map/transpose | solution.py:167
  71.3 1.2 all_to_all.33
  72.6 7.4 %all-to-all-start.2 = ((f32[32,1,4716]{2,1,0:T(1,128)}), f32[32,1,4716]{2,1,0:T(1,128)S(1)}, u32[]{:S(2)}, u32[]{:S(2)}) async-start(f32[32,1,4716]{2,1,0:T(1,128)} %all_to_all.33), calls=%async_computation.2 | async-start | bytes 1212416 | tf_op jit(solution)/shard_map/all_to_all | solution.py:88
  80.1 38.5 %all-gather = bf16[128,2048]{1,0:T(8,128)(2,1)} all-gather(bf16[16,2048]{1,0:T(8,128)(2,1)S(1)} %fusion.11), channel_id=2, replica_groups=mesh['wall'=8,'stream_0'=8,'stream_1'=2,'stream_2'=2] {'stream_0'}, dimensions={0}, use_global_device_ids=true | all-gather | bytes 589824 | tf_op jit(solution)/shard_map/all_gather | solution.py:65
  122.1 23.3 %all-gather.6.cloned.1.call-done = bf16[16,16,2048]{2,1,0:T(8,128)(2,1)} async-done(((bf16[8,16,2048]{2,1,0:T(8,128)(2,1)}), bf16[16,16,2048]{2,1,0:T(8,128)(2,1)}) %all-gather.6.cloned.1.call-update) | async-done | bytes 1048592 | tf_op jit(solution)/shard_map/all_gather | solution.py:65
  145.4 5.0 %all-to-all-start.1 = ((f32[8,2,2]{1,2,0:T(2,128)}), f32[8,2,2]{1,2,0:T(2,128)S(1)}, u32[]{:S(2)}, u32[]{:S(2)}) async-start(f32[8,2,2]{1,2,0:T(2,128)} %copy.101), calls=%async_computation.1 | async-start | bytes 16384 | tf_op jit(solution)/shard_map/all_to_all | solution.py:283
  151.7 3.5 %all-to-all-done.1 = f32[8,2,2]{1,2,0:T(2,128)S(1)} async-done(((f32[8,2,2]{1,2,0:T(2,128)}), f32[8,2,2]{1,2,0:T(2,128)S(1)}, u32[]{:S(2)}, u32[]{:S(2)}) %all-to-all-start.1) | async-done | bytes 160 | tf_op jit(solution)/shard_map/all_to_all | solution.py:283
  155.1 1.0 broadcast_in_dim.48
  156.1 8.9 %all-to-all-start.3 = ((f32[32,1,3692]{2,1,0:T(1,128)}), f32[32,1,3692]{2,1,0:T(1,128)S(1)}, u32[]{:S(2)}, u32[]{:S(2)}) async-start(f32[32,1,3692]{2,1,0:T(1,128)} %broadcast_in_dim.48), calls=%async_computation.3 | async-start | bytes 950272 | tf_op jit(solution)/shard_map/all_to_all | solution.py:78
  165.0 1.6 scatter-add.16
  166.6 0.9 slice_add_fusion.4
  167.5 1.6 scatter-add.19
  169.1 1.7 fusion.19
  172.6 9.4 %all-to-all-done.3 = f32[32,1,3692]{2,1,0:T(1,128)S(1)} async-done(((f32[32,1,3692]{2,1,0:T(1,128)}), f32[32,1,3692]{2,1,0:T(1,128)S(1)}, u32[]{:S(2)}, u32[]{:S(2)}) %all-to-all-start.3) | async-done | bytes 472608 | tf_op jit(solution)/shard_map/all_to_all | solution.py:78
  185.9 0.9 copy.110
  186.8 2.1 %broadcast_in_dim_reshape_reshape.3 = f32[1,27,64,64]{3,2,1,0:T(8,128)} reshape(f32[32,3456]{1,0:T(8,128)} %slice.240) | data formatting | bytes 884736 | tf_op jit(solution)/shard_map/broadcast_in_dim;reshape;reshape | solution.py:312
  189.8 1.8 copy.107
  192.2 1.9 fusion.15
  (150 shorter events, 26.5 us)
Async XLA Ops:
  7.9 19.8 %collective-permute-start.2 = (f32[3,1,16,128]{3,2,1,0:T(8,128)S(1)}, f32[3,1,16,128]{3,2,1,0:T(8,128)S(1)}, u32[]{:S(2)}, u32[]{:S(2)}) collective-permute-start(f32[3,1,16,128]{3,2,1,0:T(8,128)S(1)} %get-tuple-element.104), channel_id=1, source_target_pairs={{0,32},{32,64},{64,96},{96,128},{128,160},{160,192},{192,224},{224... | collective-permute-start | bytes 73736 | tf_op jit(solution)/shard_map/ppermute | solution.py:34
  9.4 18.3 %collective-permute-start.3 = (f32[3,1,16,128]{3,2,1,0:T(8,128)S(1)}, f32[3,1,16,128]{3,2,1,0:T(8,128)S(1)}, u32[]{:S(2)}, u32[]{:S(2)}) collective-permute-start(f32[3,1,16,128]{3,2,1,0:T(8,128)S(1)} %get-tuple-element.103), channel_id=1, source_target_pairs={{32,0},{64,32},{96,64},{128,96},{160,128},{192,160},{224,192},{0,2... | collective-permute-start | bytes 73736 | tf_op jit(solution)/shard_map/ppermute | solution.py:35
  11.2 19.6 %collective-permute-start = (f32[3,8,1,128]{3,1,0,2:T(8,128)S(1)}, f32[3,8,1,128]{3,1,0,2:T(8,128)S(1)}, u32[]{:S(2)}, u32[]{:S(2)}) collective-permute-start(f32[3,8,1,128]{3,1,0,2:T(8,128)S(1)} %bitcast.160), channel_id=1, source_target_pairs={{0,1},{1,2},{2,3},{3,4},{4,5},{5,6},{6,7},{7,8},{8,9},{9,10},{10,1... | collective-permute-start | bytes 36872 | tf_op jit(solution)/shard_map/ppermute | solution.py:34
  11.3 19.5 %collective-permute-start.1 = (f32[3,8,1,128]{3,1,0,2:T(8,128)S(1)}, f32[3,8,1,128]{3,1,0,2:T(8,128)S(1)}, u32[]{:S(2)}, u32[]{:S(2)}) collective-permute-start(f32[3,8,1,128]{3,1,0,2:T(8,128)S(1)} %bitcast.159), channel_id=1, source_target_pairs={{1,0},{2,1},{3,2},{4,3},{5,4},{6,5},{7,6},{8,7},{9,8},{10,9},{11,1... | collective-permute-start | bytes 36872 | tf_op jit(solution)/shard_map/ppermute | solution.py:35
  24.4 6.2 %copy-start.19 = (s32[8]{0:T(128)}, s32[8]{0:T(128)S(1)}, u32[]{:S(2)}) copy-start(s32[8]{0:T(128)S(1)} %multiply_add_fusion) | copy-start | bytes 100
  27.8 0.7 copy-start.1
  28.5 9.2 %copy-start.8 = (bf16[1,54,64]{2,1,0:T(8,128)(2,1)S(1)}, bf16[1,54,64]{2,1,0:T(8,128)(2,1)}, u32[]{:S(2)}) copy-start(bf16[1,54,64]{2,1,0:T(8,128)(2,1)} %param.21) | copy-start | bytes 20740
  30.8 12.9 %copy-start.10 = (f32[3,8,1,128]{3,1,0,2:T(8,128)}, f32[3,8,1,128]{3,1,0,2:T(8,128)S(1)}, u32[]{:S(2)}) copy-start(f32[3,8,1,128]{3,1,0,2:T(8,128)S(1)} %collective-permute-done) | copy-start | bytes 36868
  30.9 12.9 %copy-start.12 = (f32[3,8,1,128]{3,1,0,2:T(8,128)}, f32[3,8,1,128]{3,1,0,2:T(8,128)S(1)}, u32[]{:S(2)}) copy-start(f32[3,8,1,128]{3,1,0,2:T(8,128)S(1)} %collective-permute-done.1) | copy-start | bytes 36868
  31.8 10.7 %all-to-all-start = ((bf16[8,2,259]{2,1,0:T(2,128)(2,1)}), bf16[8,2,259]{2,1,0:T(2,128)(2,1)S(1)}, u32[]{:S(2)}, u32[]{:S(2)}) async-start(bf16[8,2,259]{2,1,0:T(2,128)(2,1)} %pad_maximum_fusion.4), calls=%async_computation | async-start | bytes 24576 | tf_op jit(solution)/shard_map/all_to_all | solution.py:51
  42.5 5.4 %copy-start.7 = (bf16[16,259]{1,0:T(8,128)(2,1)}, bf16[16,259]{1,0:T(8,128)(2,1)S(1)}, u32[]{:S(2)}) copy-start(bf16[16,259]{1,0:T(8,128)(2,1)S(1)} %all_to_all.29) | copy-start | bytes 24868
  47.8 0.7 slice-start
  48.6 4.6 %copy-start.14 = (bf16[1,2048,2]{1,2,0:T(2,128)(2,1)S(1)}, bf16[1,2048,2]{1,2,0:T(2,128)(2,1)}, u32[]{:S(2)}) copy-start(bf16[1,2048,2]{1,2,0:T(2,128)(2,1)} %param.24) | copy-start | bytes 24580
  53.4 0.6 copy-start.17
  59.9 1.2 copy-start.3
  71.2 47.5 %copy-start.15 = (bf16[1,2048,2]{1,2,0:T(2,128)(2,1)S(1)}, bf16[1,2048,2]{1,2,0:T(2,128)(2,1)}, u32[]{:S(2)}) copy-start(bf16[1,2048,2]{1,2,0:T(2,128)(2,1)} %param.24) | copy-start | bytes 24580
  71.3 47.7 %copy-start = (f32[3,8,16,128]{3,2,1,0:T(8,128)S(1)}, f32[3,8,16,128]{3,2,1,0:T(8,128)}, u32[]{:S(2)}) copy-start(f32[3,8,16,128]{3,2,1,0:T(8,128)} %param.18) | copy-start | bytes 589828
  71.3 47.7 %copy-start.16 = (f32[32,16,1,1]{0,1,3,2:T(8,128)S(1)}, f32[32,16,1,1]{0,1,3,2:T(8,128)}, u32[]{:S(2)}) copy-start(f32[32,16,1,1]{0,1,3,2:T(8,128)} %constant.249) | copy-start | bytes 6148
  72.6 48.3 %copy-start.6 = (f32[256,128,1,1]{1,0,3,2:T(8,128)S(1)}, f32[256,128,1,1]{1,0,3,2:T(8,128)}, u32[]{:S(2)}) copy-start(f32[256,128,1,1]{1,0,3,2:T(8,128)} %constant.251) | copy-start | bytes 393220
  72.6 72.8 %all-to-all-start.2 = ((f32[32,1,4716]{2,1,0:T(1,128)}), f32[32,1,4716]{2,1,0:T(1,128)S(1)}, u32[]{:S(2)}, u32[]{:S(2)}) async-start(f32[32,1,4716]{2,1,0:T(1,128)} %all_to_all.33), calls=%async_computation.2 | async-start | bytes 1212416 | tf_op jit(solution)/shard_map/all_to_all | solution.py:88
  80.0 41.3 %copy-start.11 = (f32[3,8,1,128]{3,1,0,2:T(8,128)S(1)}, f32[3,8,1,128]{3,1,0,2:T(8,128)}, u32[]{:S(2)}) copy-start(f32[3,8,1,128]{3,1,0,2:T(8,128)} %copy-done.10) | copy-start | bytes 36868
  80.0 41.3 %copy-start.13 = (f32[3,8,1,128]{3,1,0,2:T(8,128)S(1)}, f32[3,8,1,128]{3,1,0,2:T(8,128)}, u32[]{:S(2)}) copy-start(f32[3,8,1,128]{3,1,0,2:T(8,128)} %copy-done.12) | copy-start | bytes 36868
  80.0 41.4 %copy-start.18 = (f32[16,2]{0,1:T(2,128)S(1)}, f32[16,2]{0,1:T(2,128)}, u32[]{:S(2)}) copy-start(f32[16,2]{0,1:T(2,128)} %copy-done.17) | copy-start | bytes 388
  80.0 65.3 %all-gather.6.cloned.1.call-start = ((), (), s32[]{:S(2)}) async-start(), calls=%async_computation.4 | async-start | bytes 1572864 | tf_op jit(solution)/shard_map/all_gather | solution.py:65
  118.6 71.2 %all-gather.8.cloned.1.call-start = ((), (), s32[]{:S(2)}) async-start(), calls=%async_computation.5 | async-start | bytes 3145728 | tf_op jit(solution)/shard_map/all_gather | solution.py:65
  145.4 23.8 %copy-start.2 = (f32[3,8,16,128]{3,2,1,0:T(8,128)S(1)}, f32[3,8,16,128]{3,2,1,0:T(8,128)}, u32[]{:S(2)}) copy-start(f32[3,8,16,128]{3,2,1,0:T(8,128)} %copy-done.1) | copy-start | bytes 589828
  145.4 9.7 %all-to-all-start.1 = ((f32[8,2,2]{1,2,0:T(2,128)}), f32[8,2,2]{1,2,0:T(2,128)S(1)}, u32[]{:S(2)}, u32[]{:S(2)}) async-start(f32[8,2,2]{1,2,0:T(2,128)} %copy.101), calls=%async_computation.1 | async-start | bytes 16384 | tf_op jit(solution)/shard_map/all_to_all | solution.py:283
  150.4 20.5 %copy-start.20 = (s32[8]{0:T(128)S(1)}, s32[8]{0:T(128)}, u32[]{:S(2)}) copy-start(s32[8]{0:T(128)} %copy-done.19) | copy-start | bytes 100
  156.1 25.8 %all-to-all-start.3 = ((f32[32,1,3692]{2,1,0:T(1,128)}), f32[32,1,3692]{2,1,0:T(1,128)S(1)}, u32[]{:S(2)}, u32[]{:S(2)}) async-start(f32[32,1,3692]{2,1,0:T(1,128)} %broadcast_in_dim.48), calls=%async_computation.3 | async-start | bytes 950272 | tf_op jit(solution)/shard_map/all_to_all | solution.py:78
  185.7 3.4 %copy-start.9 = (bf16[1,54,64]{2,1,0:T(8,128)(2,1)S(1)}, bf16[1,54,64]{2,1,0:T(8,128)(2,1)}, u32[]{:S(2)}) copy-start(bf16[1,54,64]{2,1,0:T(8,128)(2,1)} %param.21) | copy-start | bytes 20740
  185.9 3.1 %copy-start.5 = (f32[118,64]{1,0:T(8,128)S(1)}, f32[118,64]{1,0:T(8,128)}, u32[]{:S(2)}) copy-start(f32[118,64]{1,0:T(8,128)} %slice.213) | copy-start | bytes 90628
  189.8 1.8 copy-start.4
Sparse Core Ops, SparseCore 0:
  118.7 26.5 all-gather.5
  147.2 15.3 all-gather.7

commit v9 on v7

--- a/solution.py
+++ b/solution.py
@@ -84,9 +84,10 @@
     small = jnp.pad(small, (0, spare))
     summed = [rows.reshape(count, -1), small.reshape(count, -1)]
     width = sum(part.shape[1] for part in summed)
-    both = jnp.concatenate(summed + [tiles.reshape(count, -1).astype(jnp.float32)], axis=1)
+    summed = [part.astype(tiles.dtype) for part in summed]
+    both = jnp.concatenate(summed + [tiles.reshape(count, -1)], axis=1)
     arrived = lax.all_to_all(both, axis, split_axis=0, concat_axis=0, tiled=True)
-    total = arrived[:, :width].sum(axis=0)
+    total = arrived[:, :width].astype(jnp.float32).sum(axis=0)
     part = rows.size // count
     moved = arrived[:, width:].astype(tiles.dtype).reshape(-1, *tiles.shape[2:])
     return total[:part].reshape(-1, rows.shape[-1]), total[part:], moved

time: 171 us -> 160 us (0.936)
  waiting for transfers between devices: 42.1 us -> 34.8 us
  local copies, waits for them, and re-layouts: 27.9 us -> 25.6 us
    all_gather x2, waiting for transfers between devices: 20.6 us -> 0.96 us  [gather_in_order(): tiles = lax.all_gather(tiles, axes[k])]
    all_to_all x1, waiting for transfers between devices: 8.65 us -> 14.7 us  [owner_sums(): lax.all_to_all(both, axis, split_axis=0, concat_axis=0, tiled=True)]
    all_to_all x1, waiting for transfers between devices: 7.98 us -> 13.9 us  [from_everyone(): return lax.all_to_all(copies, axis, split_axis=0, concat_axis=0, tiled=True)]
    scatter-add x2, local copies, waits for them, and re-layouts: 3.17 us -> 0.42 us  [body(): grad_x = along_x[:, :, :size_x].at[:, :, 0].add(-lift_half * left_face).a...]
    all_to_all x1, waiting for transfers between devices: 0.01 us -> 1.97 us  [body(): back = lax.all_to_all(pred, 'wall', split_axis=0, concat_axis=0, tiled=True)]
  transfers between devices with their start and end apart: 10 -> 10, of which waited for: 4 -> 5; matrix products, arithmetic and copies ran while one was open for 20% -> 22% of each run, Pallas kernels for 0% -> 0%
where the time goes in v9:
time: 160 us; the launch traced here: 159 us
  waiting for transfers between devices  34.8 us (22%)
  starting transfers between devices  34.4 us (22%)
  matrix products  28.9 us (18%)
  local copies, waits for them, and re-layouts  25.6 us (16%)
  between operations  15.4 us (10%)
  other arithmetic  13.5 us (8%)
  blocking collectives  6.78 us (4%)
    all_to_all x1, waiting for transfers between devices, owner_sums(): lax.all_to_all(both, axis, split_axis=0, concat_axis=0, tiled=True)  14.7 us
    all_to_all x1, waiting for transfers between devices, from_everyone(): return lax.all_to_all(copies, axis, split_axis=0, concat_axis=0, tiled=True)  13.9 us
    transpose x2, matrix products, conv_filter(): return jnp.moveaxis(taps, 0, 3)  9.39 us
    ppermute x2, starting transfers between devices, extended(): lax.ppermute(first, axis, [(b, a) for a, b in up])  7.98 us
    all_to_all x1, starting transfers between devices, owner_sums(): lax.all_to_all(both, axis, split_axis=0, concat_axis=0, tiled=True)  7.28 us
    all_gather x1, blocking collectives, gather_in_order(): tiles = lax.all_gather(tiles, axes[k])  6.78 us
    all_to_all x1, starting transfers between devices, from_everyone(): return lax.all_to_all(copies, axis, split_axis=0, concat_axis=0, tiled=True)  6.15 us
    all_to_all x1, starting transfers between devices, in_one_piece(): lax.all_to_all(both, axis, split_axis=split_dim, concat_axis=concat_dim,...  5.88 us
  transfers between devices with their start and end apart: 10, of which 5 were waited for; matrix products, arithmetic and copies ran while one was open for 22% of the time, Pallas kernels for 0%

profile of v9, /device:TPU:2, one launch (start us, length us, event | category | flops | bytes accessed | tf_op | source)
XLA Modules:
  0.0 159.3 jit_solution(6914719016052230719)
XLA Ops:
  7.9 1.5 collective-permute-start.2
  10.3 1.0 fusion.48
  11.3 7.1 %collective-permute-start.1 = (f32[3,8,1,128]{3,1,0,2:T(8,128)S(1)}, f32[3,8,1,128]{3,1,0,2:T(8,128)S(1)}, u32[]{:S(2)}, u32[]{:S(2)}) collective-permute-start(f32[3,8,1,128]{3,1,0,2:T(8,128)S(1)} %bitcast.160), channel_id=1, source_target_pairs={{1,0},{2,1},{3,2},{4,3},{5,4},{6,5},{7,6},{8,7},{9,8},{10,9},{11,1... | collective-permute-start | bytes 36872 | tf_op jit(solution)/shard_map/ppermute | solution.py:35
  19.8 0.9 fusion.47
  20.7 1.5 fusion.25
  24.4 1.2 reshape.313
  28.5 1.1 reshape.316
  31.8 5.9 %all-to-all-start = ((bf16[8,2,259]{2,1,0:T(2,128)(2,1)}), bf16[8,2,259]{2,1,0:T(2,128)(2,1)S(1)}, u32[]{:S(2)}, u32[]{:S(2)}) async-start(bf16[8,2,259]{2,1,0:T(2,128)(2,1)} %pad_maximum_fusion.4), calls=%async_computation | async-start | bytes 24576 | tf_op jit(solution)/shard_map/all_to_all | solution.py:51
  39.3 3.2 %all-to-all-done = bf16[8,2,259]{2,1,0:T(2,128)(2,1)S(1)} async-done(((bf16[8,2,259]{2,1,0:T(2,128)(2,1)}), bf16[8,2,259]{2,1,0:T(2,128)(2,1)S(1)}, u32[]{:S(2)}, u32[]{:S(2)}) %all-to-all-start) | async-done | bytes 8320 | tf_op jit(solution)/shard_map/all_to_all | solution.py:51
  42.8 0.9 convolution_multiply_fusion.4
  43.7 3.5 %fusion.17 = (f32[16,4,4,8,64]{4,0,3,2,1:T(8,128)}, f32[16,4,4,8,64]{4,0,3,2,1:T(8,128)}) fusion(bf16[3,3,3,64,64]{4,3,2,1,0:T(8,128)(2,1)S(1)} %bitcast.165, f32[16,4,4,8,64]{4,0,3,2,1:T(8,128)S(1)} %convolution_multiply_fusion.4), kind=kOutput, calls=%fused_computation.31 | convolution fusion | flops 289669120 | bytes 1794048 | tf_op jit(solution)/shard_map/conv_general_dilated | solution.py:157
  47.2 1.3 reduce_sum.84
  48.8 4.6 %multiply_convert_fusion.3 = (bf16[16,2048]{1,0:T(8,128)(2,1)S(1)}, f32[16,2048]{1,0:T(8,128)S(1)}) fusion(bf16[16,2048]{1,0:T(8,128)(2,1)S(1)} %convert_element_type.114, bf16[1,2048,2048]{2,1,0:T(8,128)(2,1)} %param.23), kind=kOutput, calls=%fused_computation.55 | convolution fusion | flops 134414336 | bytes 8650752 | tf_op jit(solution)/shard_map/dot_general | solution.py:186
  54.1 5.6 %fusion.8 = f32[16,2048]{1,0:T(8,128)S(1)} fusion(bf16[16,2048]{1,0:T(8,128)(2,1)S(1)} %fusion.11, bf16[1,2048,2048]{2,1,0:T(8,128)(2,1)} %param.23), kind=kOutput, calls=%fused_computation.9 | convolution fusion | flops 134250496 | bytes 8585216 | tf_op jit(solution)/shard_map/dot_general | solution.py:194
  59.7 6.8 %all-gather = bf16[32,2048]{1,0:T(8,128)(2,1)} all-gather(bf16[16,2048]{1,0:T(8,128)(2,1)S(1)} %fusion.11), channel_id=2, replica_groups=mesh['wall'=8,'stream_0'=8,'stream_1'=2,'stream_2'=2] {'stream_1'}, dimensions={0}, use_global_device_ids=true | all-gather | bytes 196608 | tf_op jit(solution)/shard_map/all_gather | solution.py:65
  66.9 1.6 %multiply_convert_fusion = bf16[16,4,4,8,64]{4,0,3,2,1:T(8,128)(2,1)S(1)} fusion(f32[16,4,4,8,64]{4,0,3,2,1:T(8,128)S(1)} %bitcast.137, f32[16,4,4,8,64]{4,0,3,2,1:T(8,128)} %get-tuple-element.114), kind=kLoop, calls=%fused_computation.29 | loop fusion | flops 1179648 | bytes 1310720 | tf_op jit(solution)/shard_map/convert_element_type | solution.py:197
  68.5 5.4 %fusion.16 = bf16[3,3,3,2,64]{4,3,2,1,0:T(2,128)(2,1)S(1)} fusion(bf16[16,2,4,4,8]{0,4,3,2,1:T(8,128)(2,1)S(1)} %bitcast.153, bf16[16,4,4,8,64]{4,0,3,2,1:T(8,128)(2,1)S(1)} %multiply_convert_fusion, bf16[3,3,3,64,64]{4,3,2,1,0:T(8,128)(2,1)S(1)} %bitcast.166, f32[16,4,4,8,64]{4,0,3,2,1:T(8,128)} %copy-done.3), kind=kOutput, calls=%fused_computation.23 | convolution fusion | flops 298687232 | bytes 1022720 | tf_op jit(solution)/shard_map/transpose | solution.py:168
  75.2 3.9 %fusion.15 = bf16[3,3,3,64,64]{4,3,2,1,0:T(8,128)(2,1)S(1)} fusion(bf16[16,4,4,8,64]{4,0,3,2,1:T(8,128)(2,1)S(1)} %multiply_convert_fusion, f32[16,4,4,8,64]{4,0,3,2,1:T(8,128)} %copy-done.3), kind=kOutput, calls=%fused_computation.19 | convolution fusion | flops 289234944 | bytes 1007616 | tf_op jit(solution)/shard_map/transpose | solution.py:168
  81.0 1.1 reshape.352
  82.0 7.3 %all-to-all-start.2 = ((bf16[32,2,2358]{2,1,0:T(2,128)(2,1)}), bf16[32,2,2358]{2,1,0:T(2,128)(2,1)S(1)}, u32[]{:S(2)}, u32[]{:S(2)}) async-start(bf16[32,2,2358]{2,1,0:T(2,128)(2,1)} %reshape.352), calls=%async_computation.2 | async-start | bytes 622592 | tf_op jit(solution)/shard_map/all_to_all | solution.py:89
  91.2 14.7 %all-to-all-done.2 = bf16[32,2,2358]{2,1,0:T(2,128)(2,1)S(1)} async-done(((bf16[32,2,2358]{2,1,0:T(2,128)(2,1)}), bf16[32,2,2358]{2,1,0:T(2,128)(2,1)S(1)}, u32[]{:S(2)}, u32[]{:S(2)}) %all-to-all-start.2) | async-done | bytes 301856 | tf_op jit(solution)/shard_map/all_to_all | solution.py:89
  105.9 5.6 %all-to-all-start.1 = ((f32[8,2,2]{1,2,0:T(2,128)}), f32[8,2,2]{1,2,0:T(2,128)S(1)}, u32[]{:S(2)}, u32[]{:S(2)}) async-start(f32[8,2,2]{1,2,0:T(2,128)} %copy.125), calls=%async_computation.1 | async-start | bytes 16384 | tf_op jit(solution)/shard_map/all_to_all | solution.py:284
  113.3 1.0 all-gather.6.cloned.1.call-done
  114.3 2.0 %all-to-all-done.1 = f32[8,2,2]{1,2,0:T(2,128)S(1)} async-done(((f32[8,2,2]{1,2,0:T(2,128)}), f32[8,2,2]{1,2,0:T(2,128)S(1)}, u32[]{:S(2)}, u32[]{:S(2)}) %all-to-all-start.1) | async-done | bytes 160 | tf_op jit(solution)/shard_map/all_to_all | solution.py:284
  116.2 1.0 broadcast_in_dim.48
  117.3 6.1 %all-to-all-start.3 = ((f32[32,1,3692]{2,1,0:T(1,128)}), f32[32,1,3692]{2,1,0:T(1,128)S(1)}, u32[]{:S(2)}, u32[]{:S(2)}) async-start(f32[32,1,3692]{2,1,0:T(1,128)} %broadcast_in_dim.48), calls=%async_computation.3 | async-start | bytes 950272 | tf_op jit(solution)/shard_map/all_to_all | solution.py:78
  126.5 13.9 %all-to-all-done.3 = f32[32,1,3692]{2,1,0:T(1,128)S(1)} async-done(((f32[32,1,3692]{2,1,0:T(1,128)}), f32[32,1,3692]{2,1,0:T(1,128)S(1)}, u32[]{:S(2)}, u32[]{:S(2)}) %all-to-all-start.3) | async-done | bytes 472608 | tf_op jit(solution)/shard_map/all_to_all | solution.py:78
  142.5 0.9 multiply_reduce_fusion
  144.3 0.9 copy.135
  145.2 2.1 %broadcast_in_dim_reshape_reshape.3 = f32[1,27,64,64]{3,2,1,0:T(8,128)} reshape(f32[32,3456]{1,0:T(8,128)} %slice.239) | data formatting | bytes 884736 | tf_op jit(solution)/shard_map/broadcast_in_dim;reshape;reshape | solution.py:313
  148.2 1.8 %copy.132 = bf16[8,2,2,16,2048]{4,3,2,1,0:T(8,128)(2,1)S(1)} copy(bf16[8,2,2,16,2048]{4,3,1,0,2:T(8,128)(2,1)} %bitcast.139) | data formatting | bytes 4194304 | tf_op jit(solution)/shard_map/transpose | solution.py:68
  150.6 1.9 %fusion.18 = f32[1,64,2048]{2,1,0:T(8,128)} fusion(f32[64,2048]{1,0:T(8,128)S(1)} %get-tuple-element.118, f32[64]{0:T(128)S(1)} %add_sqrt_fusion, bf16[1,2048,2048]{2,1,0:T(8,128)(2,1)} %param.23, s32[]{:T(128)S(6)} %select_n.37), kind=kLoop, calls=%fused_computation.35 | loop fusion | flops 524288 | bytes 1310980 | tf_op jit(solution)/shard_map/broadcast_in_dim | solution.py:301
  (150 shorter events, 26.7 us)
Async XLA Ops:
  7.9 19.8 %collective-permute-start.2 = (f32[3,1,16,128]{3,2,1,0:T(8,128)S(1)}, f32[3,1,16,128]{3,2,1,0:T(8,128)S(1)}, u32[]{:S(2)}, u32[]{:S(2)}) collective-permute-start(f32[3,1,16,128]{3,2,1,0:T(8,128)S(1)} %get-tuple-element.110), channel_id=1, source_target_pairs={{0,32},{32,64},{64,96},{96,128},{128,160},{160,192},{192,224},{224... | collective-permute-start | bytes 73736 | tf_op jit(solution)/shard_map/ppermute | solution.py:34
  9.4 18.4 %collective-permute-start.3 = (f32[3,1,16,128]{3,2,1,0:T(8,128)S(1)}, f32[3,1,16,128]{3,2,1,0:T(8,128)S(1)}, u32[]{:S(2)}, u32[]{:S(2)}) collective-permute-start(f32[3,1,16,128]{3,2,1,0:T(8,128)S(1)} %get-tuple-element.109), channel_id=1, source_target_pairs={{32,0},{64,32},{96,64},{128,96},{160,128},{192,160},{224,192},{0,2... | collective-permute-start | bytes 73736 | tf_op jit(solution)/shard_map/ppermute | solution.py:35
  11.2 19.6 %collective-permute-start = (f32[3,8,1,128]{3,1,0,2:T(8,128)S(1)}, f32[3,8,1,128]{3,1,0,2:T(8,128)S(1)}, u32[]{:S(2)}, u32[]{:S(2)}) collective-permute-start(f32[3,8,1,128]{3,1,0,2:T(8,128)S(1)} %bitcast.161), channel_id=1, source_target_pairs={{0,1},{1,2},{2,3},{3,4},{4,5},{5,6},{6,7},{7,8},{8,9},{9,10},{10,1... | collective-permute-start | bytes 36872 | tf_op jit(solution)/shard_map/ppermute | solution.py:34
  11.3 19.5 %collective-permute-start.1 = (f32[3,8,1,128]{3,1,0,2:T(8,128)S(1)}, f32[3,8,1,128]{3,1,0,2:T(8,128)S(1)}, u32[]{:S(2)}, u32[]{:S(2)}) collective-permute-start(f32[3,8,1,128]{3,1,0,2:T(8,128)S(1)} %bitcast.160), channel_id=1, source_target_pairs={{1,0},{2,1},{3,2},{4,3},{5,4},{6,5},{7,6},{8,7},{9,8},{10,9},{11,1... | collective-permute-start | bytes 36872 | tf_op jit(solution)/shard_map/ppermute | solution.py:35
  24.4 6.2 %copy-start.18 = (s32[8]{0:T(128)}, s32[8]{0:T(128)S(1)}, u32[]{:S(2)}) copy-start(s32[8]{0:T(128)S(1)} %multiply_add_fusion) | copy-start | bytes 100
  27.7 0.7 copy-start.1
  28.5 9.2 %copy-start = (f32[3,8,16,128]{3,2,1,0:T(8,128)S(1)}, f32[3,8,16,128]{3,2,1,0:T(8,128)}, u32[]{:S(2)}) copy-start(f32[3,8,16,128]{3,2,1,0:T(8,128)} %param.18) | copy-start | bytes 589828
  28.5 9.2 %copy-start.16 = (f32[32,16,1,1]{0,1,3,2:T(8,128)S(1)}, f32[32,16,1,1]{0,1,3,2:T(8,128)}, u32[]{:S(2)}) copy-start(f32[32,16,1,1]{0,1,3,2:T(8,128)} %constant.249) | copy-start | bytes 6148
  28.5 9.7 %copy-start.12 = (bf16[1,54,64]{2,1,0:T(8,128)(2,1)S(1)}, bf16[1,54,64]{2,1,0:T(8,128)(2,1)}, u32[]{:S(2)}) copy-start(bf16[1,54,64]{2,1,0:T(8,128)(2,1)} %param.21) | copy-start | bytes 20740
  29.6 8.6 %copy-start.15 = (bf16[1,2048,2]{1,2,0:T(2,128)(2,1)S(1)}, bf16[1,2048,2]{1,2,0:T(2,128)(2,1)}, u32[]{:S(2)}) copy-start(bf16[1,2048,2]{1,2,0:T(2,128)(2,1)} %param.24) | copy-start | bytes 24580
  29.9 13.8 %copy-start.17 = (bf16[1,27,64,64]{3,2,1,0:T(8,128)(2,1)S(1)}, bf16[1,27,64,64]{3,2,1,0:T(8,128)(2,1)}, u32[]{:S(2)}) copy-start(bf16[1,27,64,64]{3,2,1,0:T(8,128)(2,1)} %param.22) | copy-start | bytes 663556
  30.9 16.3 %copy-start.13 = (f32[3,8,1,128]{3,1,0,2:T(8,128)}, f32[3,8,1,128]{3,1,0,2:T(8,128)S(1)}, u32[]{:S(2)}) copy-start(f32[3,8,1,128]{3,1,0,2:T(8,128)S(1)} %collective-permute-done.1) | copy-start | bytes 36868
  31.8 10.7 %all-to-all-start = ((bf16[8,2,259]{2,1,0:T(2,128)(2,1)}), bf16[8,2,259]{2,1,0:T(2,128)(2,1)S(1)}, u32[]{:S(2)}, u32[]{:S(2)}) async-start(bf16[8,2,259]{2,1,0:T(2,128)(2,1)} %pad_maximum_fusion.4), calls=%async_computation | async-start | bytes 24576 | tf_op jit(solution)/shard_map/all_to_all | solution.py:51
  37.7 76.6 %all-gather.6.cloned.1.call-start = ((), (), s32[]{:S(2)}) async-start(), calls=%async_computation.4 | async-start | bytes 1179648 | tf_op jit(solution)/shard_map/all_gather | solution.py:65
  42.5 4.7 %copy-start.11 = (bf16[16,259]{1,0:T(8,128)(2,1)}, bf16[16,259]{1,0:T(8,128)(2,1)S(1)}, u32[]{:S(2)}) copy-start(bf16[16,259]{1,0:T(8,128)(2,1)S(1)} %all_to_all.29) | copy-start | bytes 24868
  43.7 3.5 %copy-start.3 = (f32[16,4,4,8,64]{4,0,3,2,1:T(8,128)}, f32[16,4,4,8,64]{4,0,3,2,1:T(8,128)S(1)}, u32[]{:S(2)}) copy-start(f32[16,4,4,8,64]{4,0,3,2,1:T(8,128)S(1)} %convolution_multiply_fusion.4) | copy-start | bytes 1572868
  48.8 4.8 %slice-start = ((bf16[16,259]{1,0:T(8,128)(2,1)}), bf16[16,2]{1,0:T(8,128)(2,1)S(1)}, s32[]{:S(2)}) async-start(bf16[16,259]{1,0:T(8,128)(2,1)} %copy-done.11), calls=%async_computation.6 | async-start | bytes 8192 | tf_op jit(solution)/shard_map/split | solution.py:52
  79.2 10.9 %copy-start.10 = (f32[256,128,1,1]{1,0,3,2:T(8,128)S(1)}, f32[256,128,1,1]{1,0,3,2:T(8,128)}, u32[]{:S(2)}) copy-start(f32[256,128,1,1]{1,0,3,2:T(8,128)} %constant.251) | copy-start | bytes 393220
  79.2 11.3 %copy-start.14 = (f32[3,8,1,128]{3,1,0,2:T(8,128)S(1)}, f32[3,8,1,128]{3,1,0,2:T(8,128)}, u32[]{:S(2)}) copy-start(f32[3,8,1,128]{3,1,0,2:T(8,128)} %copy-done.13) | copy-start | bytes 36868
  82.0 23.8 %all-to-all-start.2 = ((bf16[32,2,2358]{2,1,0:T(2,128)(2,1)}), bf16[32,2,2358]{2,1,0:T(2,128)(2,1)S(1)}, u32[]{:S(2)}, u32[]{:S(2)}) async-start(bf16[32,2,2358]{2,1,0:T(2,128)(2,1)} %reshape.352), calls=%async_computation.2 | async-start | bytes 622592 | tf_op jit(solution)/shard_map/all_to_all | solution.py:89
  105.9 10.4 %all-to-all-start.1 = ((f32[8,2,2]{1,2,0:T(2,128)}), f32[8,2,2]{1,2,0:T(2,128)S(1)}, u32[]{:S(2)}, u32[]{:S(2)}) async-start(f32[8,2,2]{1,2,0:T(2,128)} %copy.125), calls=%async_computation.1 | async-start | bytes 16384 | tf_op jit(solution)/shard_map/all_to_all | solution.py:284
  111.5 36.7 %all-gather.8.cloned.1.call-start = ((), (), s32[]{:S(2)}) async-start(), calls=%async_computation.5 | async-start | bytes 3145728 | tf_op jit(solution)/shard_map/all_gather | solution.py:65
  111.9 12.0 %copy-start.2 = (f32[16,3,16,128]{3,2,0,1:T(8,128)S(1)}, f32[16,3,16,128]{3,2,0,1:T(8,128)}, u32[]{:S(2)}) copy-start(f32[16,3,16,128]{3,2,0,1:T(8,128)} %copy-done.1) | copy-start | bytes 1179652
  112.0 11.5 %copy-start.4 = (f32[3,8,16,128]{3,2,1,0:T(8,128)S(1)}, f32[3,8,16,128]{3,2,1,0:T(8,128)}, u32[]{:S(2)}) copy-start(f32[3,8,16,128]{3,2,1,0:T(8,128)} %slice.222) | copy-start | bytes 589828
  112.0 11.9 %copy-start.6 = (f32[8,16,128]{2,1,0:T(8,128)S(1)}, f32[8,16,128]{2,1,0:T(8,128)}, u32[]{:S(2)}) copy-start(f32[8,16,128]{2,1,0:T(8,128)} %get-tuple-element.100) | copy-start | bytes 196612
  112.0 11.9 %copy-start.7 = (f32[8,16,128]{2,1,0:T(8,128)S(1)}, f32[8,16,128]{2,1,0:T(8,128)}, u32[]{:S(2)}) copy-start(f32[8,16,128]{2,1,0:T(8,128)} %get-tuple-element.101) | copy-start | bytes 196612
  112.0 11.9 %copy-start.8 = (f32[8,16,128]{2,1,0:T(8,128)S(1)}, f32[8,16,128]{2,1,0:T(8,128)}, u32[]{:S(2)}) copy-start(f32[8,16,128]{2,1,0:T(8,128)} %get-tuple-element.102) | copy-start | bytes 196612
  114.3 10.6 %copy-start.19 = (s32[8]{0:T(128)S(1)}, s32[8]{0:T(128)}, u32[]{:S(2)}) copy-start(s32[8]{0:T(128)} %copy-done.18) | copy-start | bytes 100
  117.3 23.1 %all-to-all-start.3 = ((f32[32,1,3692]{2,1,0:T(1,128)}), f32[32,1,3692]{2,1,0:T(1,128)S(1)}, u32[]{:S(2)}, u32[]{:S(2)}) async-start(f32[32,1,3692]{2,1,0:T(1,128)} %broadcast_in_dim.48), calls=%async_computation.3 | async-start | bytes 950272 | tf_op jit(solution)/shard_map/all_to_all | solution.py:78
  144.3 3.1 %copy-start.9 = (f32[118,64]{1,0:T(8,128)S(1)}, f32[118,64]{1,0:T(8,128)}, u32[]{:S(2)}) copy-start(f32[118,64]{1,0:T(8,128)} %slice.212) | copy-start | bytes 90628
  148.2 1.8 %copy-start.5 = (bf16[512,64]{1,0:T(8,128)(2,1)S(1)}, bf16[512,64]{1,0:T(8,128)(2,1)}, u32[]{:S(2)}) copy-start(bf16[512,64]{1,0:T(8,128)(2,1)} %reshape.325) | copy-start | bytes 196612
Sparse Core Ops, SparseCore 0:
  75.3 38.8 all-gather.5
  116.0 15.3 all-gather.7

commit v10 on v9

--- a/solution.py
+++ b/solution.py
@@ -299,13 +299,12 @@
     )
     own_rows = lax.dynamic_slice_in_dim(w_hidden[0], flow_place * share_rows, share_rows, 0)
     new_w_hidden = row_update(own_rows, grad_hidden)[None]
-    share_count = grad_share.shape[0]
-    kernel_own = lax.dynamic_slice_in_dim(
-        k_second[0].reshape(-1, CH), flow_place * share_count, share_count, 0
-    )
-    updated_rows = row_update(kernel_own, grad_share)
-    kernel_rows, small = shared_back(updated_rows, small_part, STREAM)
-    new_k_second = kernel_rows.reshape(k_second.shape[1:])
+    kernel_rows, small = shared_back(
+        grad_share.astype(jnp.bfloat16), small_part.astype(jnp.bfloat16), STREAM
+    )
+    kernel_grad = kernel_rows.astype(jnp.float32).reshape(k_second.shape[1:])
+    new_k_second = row_update(k_second[0], kernel_grad)
+    small = small.astype(jnp.float32)
     grad_one = small[: grad_one.size].reshape(grad_one.shape)
     grad_out = small[grad_one.size : grad_one.size + grad_out.size].reshape(grad_out.shape)
     new_k_first = row_update(k_first[0], grad_one)

time: 160 us -> 172 us (1.075); the launches traced: 159 us -> 169 us
  other arithmetic: 13.5 us -> 20 us
  matrix products: 28.9 us -> 33.6 us
  starting transfers between devices: 34.4 us -> 32.1 us
  waiting for transfers between devices: 34.8 us -> 36.7 us
    all_gather x2, waiting for transfers between devices: 0.96 us -> 6.11 us  [gather_in_order(): tiles = lax.all_gather(tiles, axes[k])]
    all_to_all x1, waiting for transfers between devices: 13.9 us -> 10.9 us  [from_everyone(): return lax.all_to_all(copies, axis, split_axis=0, concat_axis=0, tiled=True)]
    all_to_all x1, starting transfers between devices: 6.15 us -> 3.9 us  [from_everyone(): return lax.all_to_all(copies, axis, split_axis=0, concat_axis=0, tiled=True)]
    broadcast_in_dim x0 -> x1, other arithmetic: none -> 2.2 us  [from_everyone(): copies = jnp.broadcast_to(shard, (lax.axis_size(axis), *shard.shape))]
    another operation x2 -> x1, local copies, waits for them, and re-layouts: 2.44 us -> 0.31 us  [the longest x1 2.13 us: body(): new_k_second[None]]
    slice x4 -> x0, local copies, waits for them, and re-layouts: 2.1 us -> none  [the longest x1 0.79 us: shared_back(): whole_rows = everything[:, :rows.size].reshape(-1, rows.shape[-1])]
    unnamed x48 -> x60, local copies, waits for them, and re-layouts: 4.31 us -> 5.94 us
  transfers between devices with their start and end apart: 10 -> 10, of which waited for: 5 -> 5; matrix products, arithmetic and copies ran while one was open for 22% -> 25% of each run, Pallas kernels for 0% -> 0%
where the time goes in v10:
time: 172 us; the launch traced here: 169 us
  waiting for transfers between devices  36.7 us (21%)
  matrix products  33.6 us (20%)
  starting transfers between devices  32.1 us (19%)
  local copies, waits for them, and re-layouts  24.8 us (14%)
  other arithmetic  20 us (12%)
  between operations  15.5 us (9%)
  blocking collectives  6.78 us (4%)
    all_to_all x1, waiting for transfers between devices, owner_sums(): lax.all_to_all(both, axis, split_axis=0, concat_axis=0, tiled=True)  15.7 us
    all_to_all x1, waiting for transfers between devices, from_everyone(): return lax.all_to_all(copies, axis, split_axis=0, concat_axis=0, tiled=True)  10.9 us
    transpose x2, matrix products, conv_filter(): return jnp.moveaxis(taps, 0, 3)  9.64 us
    ppermute x2, starting transfers between devices, extended(): lax.ppermute(first, axis, [(b, a) for a, b in up])  7.98 us
    all_to_all x1, starting transfers between devices, owner_sums(): lax.all_to_all(both, axis, split_axis=0, concat_axis=0, tiled=True)  7.27 us
    all_gather x1, blocking collectives, gather_in_order(): tiles = lax.all_gather(tiles, axes[k])  6.78 us
    all_gather x2, waiting for transfers between devices, gather_in_order(): tiles = lax.all_gather(tiles, axes[k])  6.11 us
    unnamed x60, local copies, waits for them, and re-layouts  5.94 us
  transfers between devices with their start and end apart: 10, of which 5 were waited for; matrix products, arithmetic and copies ran while one was open for 25% of the time, Pallas kernels for 0%

profile of v10, /device:TPU:2, one launch (start us, length us, event | category | flops | bytes accessed | tf_op | source)
XLA Modules:
  0.0 169.4 jit_solution(2199525766164580513)
XLA Ops:
  8.0 1.5 collective-permute-start.2
  10.4 1.0 fusion.55
  11.4 7.1 %collective-permute-start.1 = (f32[3,8,1,128]{3,1,0,2:T(8,128)S(1)}, f32[3,8,1,128]{3,1,0,2:T(8,128)S(1)}, u32[]{:S(2)}, u32[]{:S(2)}) collective-permute-start(f32[3,8,1,128]{3,1,0,2:T(8,128)S(1)} %bitcast.161), channel_id=1, source_target_pairs={{1,0},{2,1},{3,2},{4,3},{5,4},{6,5},{7,6},{8,7},{9,8},{10,9},{11,1... | collective-permute-start | bytes 36872 | tf_op jit(solution)/shard_map/ppermute | solution.py:35
  20.7 1.5 fusion.29
  24.5 1.2 reshape.336
  26.8 1.4 convolution_bitcast_fusion.1
  28.2 1.5 convolution_bitcast_fusion
  33.3 2.1 %reshape.339 = f32[2,2,4,4,4,16,8]{6,5,4,3,2,1,0:T(8,128)S(1)} reshape(f32[2,8,16,128]{3,2,1,0:T(8,128)} %pad_maximum_fusion.1) | data formatting | bytes 262144 | tf_op jit(solution)/shard_map/reshape | solution.py:244
  36.5 0.9 convolution_convert_fusion.1
  39.7 5.9 %all-to-all-start = ((bf16[8,2,259]{2,1,0:T(2,128)(2,1)}), bf16[8,2,259]{2,1,0:T(2,128)(2,1)S(1)}, u32[]{:S(2)}, u32[]{:S(2)}) async-start(bf16[8,2,259]{2,1,0:T(2,128)(2,1)} %pad_maximum_fusion.3), calls=%async_computation | async-start | bytes 24576 | tf_op jit(solution)/shard_map/all_to_all | solution.py:51
  47.3 3.1 %all-to-all-done = bf16[8,2,259]{2,1,0:T(2,128)(2,1)S(1)} async-done(((bf16[8,2,259]{2,1,0:T(2,128)(2,1)}), bf16[8,2,259]{2,1,0:T(2,128)(2,1)S(1)}, u32[]{:S(2)}, u32[]{:S(2)}) %all-to-all-start) | async-done | bytes 8320 | tf_op jit(solution)/shard_map/all_to_all | solution.py:51
  52.2 4.8 %fusion.21 = (f32[16,4,4,8,64]{4,0,3,2,1:T(8,128)}, f32[16,4,4,8,64]{4,0,3,2,1:T(8,128)}) fusion(bf16[3,3,3,64,64]{4,3,2,1,0:T(8,128)(2,1)} %bitcast.151, f32[16,4,4,8,64]{4,0,3,2,1:T(8,128)S(1)} %convolution_multiply_fusion.4), kind=kOutput, calls=%fused_computation.35 | convolution fusion | flops 289669120 | bytes 1794048 | tf_op jit(solution)/shard_map/conv_general_dilated | solution.py:157
  57.0 1.3 reduce_sum.84
  58.6 4.6 %multiply_convert_fusion.3 = (bf16[16,2048]{1,0:T(8,128)(2,1)S(1)}, f32[16,2048]{1,0:T(8,128)S(1)}) fusion(bf16[16,2048]{1,0:T(8,128)(2,1)S(1)} %convert_element_type.140, bf16[1,2048,2048]{2,1,0:T(8,128)(2,1)} %param.23), kind=kOutput, calls=%fused_computation.62 | convolution fusion | flops 134414336 | bytes 8650752 | tf_op jit(solution)/shard_map/dot_general | solution.py:186
  64.2 5.6 %fusion.8 = f32[16,2048]{1,0:T(8,128)S(1)} fusion(bf16[16,2048]{1,0:T(8,128)(2,1)S(1)} %fusion.11, bf16[1,2048,2048]{2,1,0:T(8,128)(2,1)} %param.23), kind=kOutput, calls=%fused_computation.9 | convolution fusion | flops 134250496 | bytes 8585216 | tf_op jit(solution)/shard_map/dot_general | solution.py:194
  69.9 6.8 %all-gather = bf16[32,2048]{1,0:T(8,128)(2,1)} all-gather(bf16[16,2048]{1,0:T(8,128)(2,1)S(1)} %fusion.11), channel_id=2, replica_groups=mesh['wall'=8,'stream_0'=8,'stream_1'=2,'stream_2'=2] {'stream_1'}, dimensions={0}, use_global_device_ids=true | all-gather | bytes 196608 | tf_op jit(solution)/shard_map/all_gather | solution.py:65
  77.0 2.4 %multiply_convert_fusion = bf16[16,4,4,8,64]{4,0,3,2,1:T(8,128)(2,1)} fusion(f32[16,4,4,8,64]{4,0,3,2,1:T(8,128)S(1)} %bitcast.136, f32[16,4,4,8,64]{4,0,3,2,1:T(8,128)} %get-tuple-element.114), kind=kLoop, calls=%fused_computation.33 | loop fusion | flops 1179648 | bytes 1310720 | tf_op jit(solution)/shard_map/convert_element_type | solution.py:197
  79.4 5.4 %fusion.16 = bf16[3,3,3,2,64]{4,3,2,1,0:T(2,128)(2,1)S(1)} fusion(bf16[16,2,4,4,8]{0,4,3,2,1:T(8,128)(2,1)} %bitcast.154, bf16[16,4,4,8,64]{4,0,3,2,1:T(8,128)(2,1)} %multiply_convert_fusion, bf16[3,3,3,64,64]{4,3,2,1,0:T(8,128)(2,1)} %bitcast.152, f32[16,4,4,8,64]{4,0,3,2,1:T(8,128)S(1)} %convolution_multiply_fusion.4), kind=kOutput, calls=%fused_computation.25 | convolution fusion | flops 298687232 | bytes 1022720 | tf_op jit(solution)/shard_map/transpose | solution.py:168
  86.2 4.2 %fusion.15 = bf16[3,3,3,64,64]{4,3,2,1,0:T(8,128)(2,1)S(1)} fusion(bf16[16,4,4,8,64]{4,0,3,2,1:T(8,128)(2,1)} %multiply_convert_fusion, f32[16,4,4,8,64]{4,0,3,2,1:T(8,128)} %copy-done.3), kind=kOutput, calls=%fused_computation.21 | convolution fusion | flops 289234944 | bytes 1007616 | tf_op jit(solution)/shard_map/transpose | solution.py:168
  92.4 1.1 reshape.374
  93.4 7.3 %all-to-all-start.2 = ((bf16[32,2,2358]{2,1,0:T(2,128)(2,1)}), bf16[32,2,2358]{2,1,0:T(2,128)(2,1)S(1)}, u32[]{:S(2)}, u32[]{:S(2)}) async-start(bf16[32,2,2358]{2,1,0:T(2,128)(2,1)} %reshape.374), calls=%async_computation.2 | async-start | bytes 622592 | tf_op jit(solution)/shard_map/all_to_all | solution.py:89
  101.7 15.7 %all-to-all-done.2 = bf16[32,2,2358]{2,1,0:T(2,128)(2,1)S(1)} async-done(((bf16[32,2,2358]{2,1,0:T(2,128)(2,1)}), bf16[32,2,2358]{2,1,0:T(2,128)(2,1)S(1)}, u32[]{:S(2)}, u32[]{:S(2)}) %all-to-all-start.2) | async-done | bytes 301856 | tf_op jit(solution)/shard_map/all_to_all | solution.py:89
  117.4 5.4 %all-to-all-start.1 = ((f32[8,2,2]{1,2,0:T(2,128)}), f32[8,2,2]{1,2,0:T(2,128)S(1)}, u32[]{:S(2)}, u32[]{:S(2)}) async-start(f32[8,2,2]{1,2,0:T(2,128)} %copy.125), calls=%async_computation.1 | async-start | bytes 16384 | tf_op jit(solution)/shard_map/all_to_all | solution.py:284
  123.7 2.2 %reduce.13 = bf16[32,3692]{1,0:T(8,128)(2,1)S(1)} reduce(bf16[32,1,3692]{2,1,0:T(2,128)(2,1)S(1)} %broadcast_in_dim.49, bf16[]{:T(256)} %broadcast.241), dimensions={1}, to_apply=%broadcast_in_dim.49.reduce_sub_computation | reduce | bytes 472578 | tf_op jit(solution)/shard_map/broadcast_in_dim | solution.py:77
  125.9 0.9 reshape.376
  127.6 3.9 %all-to-all-start.3 = ((bf16[32,2,1846]{2,1,0:T(2,128)(2,1)}), bf16[32,2,1846]{2,1,0:T(2,128)(2,1)S(1)}, u32[]{:S(2)}, u32[]{:S(2)}) async-start(bf16[32,2,1846]{2,1,0:T(2,128)(2,1)} %reshape.376), calls=%async_computation.3 | async-start | bytes 491520 | tf_op jit(solution)/shard_map/all_to_all | solution.py:78
  133.5 10.9 %all-to-all-done.3 = bf16[32,2,1846]{2,1,0:T(2,128)(2,1)S(1)} async-done(((bf16[32,2,1846]{2,1,0:T(2,128)(2,1)}), bf16[32,2,1846]{2,1,0:T(2,128)(2,1)S(1)}, u32[]{:S(2)}, u32[]{:S(2)}) %all-to-all-start.3) | async-done | bytes 236320 | tf_op jit(solution)/shard_map/all_to_all | solution.py:78
  147.4 0.9 copy.135
  150.0 2.2 %divide_subtract_fusion = f32[1,27,64,64]{3,2,1,0:T(8,128)} fusion(f32[1,27,64,64]{3,2,1,0:T(8,128)S(1)} %mul.342, bf16[1,27,64,64]{3,2,1,0:T(8,128)(2,1)} %param.22, f32[27,64]{1,0:T(8,128)S(1)} %add_sqrt_fusion), kind=kLoop, calls=%fused_computation.38 | loop fusion | flops 331776 | bytes 1112832 | tf_op jit(solution)/shard_map/sub | solution.py:208
  152.2 6.1 %all-gather.8.cloned.1.call-done = bf16[16,2,16,2048]{3,2,1,0:T(8,128)(2,1)} async-done(((bf16[8,2,16,2048]{3,2,1,0:T(8,128)(2,1)}), bf16[16,2,16,2048]{3,2,1,0:T(8,128)(2,1)}) %all-gather.8.cloned.1.call-update) | async-done | bytes 2097168 | tf_op jit(solution)/shard_map/all_gather | solution.py:65
  158.3 1.7 %copy.132 = bf16[8,2,2,16,2048]{4,3,2,1,0:T(8,128)(2,1)S(1)} copy(bf16[8,2,2,16,2048]{4,3,1,0,2:T(8,128)(2,1)} %bitcast.138) | data formatting | bytes 4194304 | tf_op jit(solution)/shard_map/transpose | solution.py:68
  160.7 1.9 %fusion.22 = f32[1,64,2048]{2,1,0:T(8,128)} fusion(f32[64,2048]{1,0:T(8,128)S(1)} %get-tuple-element.118, f32[64]{0:T(128)S(1)} %add_sqrt_fusion.1, bf16[1,2048,2048]{2,1,0:T(8,128)(2,1)} %param.23, s32[]{:T(128)S(6)} %select_n.33), kind=kLoop, calls=%fused_computation.42 | loop fusion | flops 524288 | bytes 1310980 | tf_op jit(solution)/shard_map/broadcast_in_dim | solution.py:301
  (158 shorter events, 31.3 us)
Async XLA Ops:
  7.2 38.4 %copy-start = (f32[3,8,16,128]{3,2,1,0:T(8,128)S(1)}, f32[3,8,16,128]{3,2,1,0:T(8,128)}, u32[]{:S(2)}) copy-start(f32[3,8,16,128]{3,2,1,0:T(8,128)} %param.18) | copy-start | bytes 589828
  7.2 39.1 %copy-start.10 = (bf16[1,54,64]{2,1,0:T(8,128)(2,1)S(1)}, bf16[1,54,64]{2,1,0:T(8,128)(2,1)}, u32[]{:S(2)}) copy-start(bf16[1,54,64]{2,1,0:T(8,128)(2,1)} %param.21) | copy-start | bytes 20740
  7.2 39.1 %copy-start.16 = (bf16[1,2048,2]{1,2,0:T(2,128)(2,1)S(1)}, bf16[1,2048,2]{1,2,0:T(2,128)(2,1)}, u32[]{:S(2)}) copy-start(bf16[1,2048,2]{1,2,0:T(2,128)(2,1)} %param.24) | copy-start | bytes 24580
  8.0 23.9 %collective-permute-start.2 = (f32[3,1,16,128]{3,2,1,0:T(8,128)S(1)}, f32[3,1,16,128]{3,2,1,0:T(8,128)S(1)}, u32[]{:S(2)}, u32[]{:S(2)}) collective-permute-start(f32[3,1,16,128]{3,2,1,0:T(8,128)S(1)} %get-tuple-element.112), channel_id=1, source_target_pairs={{0,32},{32,64},{64,96},{96,128},{128,160},{160,192},{192,224},{224... | collective-permute-start | bytes 73736 | tf_op jit(solution)/shard_map/ppermute | solution.py:34
  9.5 22.4 %collective-permute-start.3 = (f32[3,1,16,128]{3,2,1,0:T(8,128)S(1)}, f32[3,1,16,128]{3,2,1,0:T(8,128)S(1)}, u32[]{:S(2)}, u32[]{:S(2)}) collective-permute-start(f32[3,1,16,128]{3,2,1,0:T(8,128)S(1)} %get-tuple-element.111), channel_id=1, source_target_pairs={{32,0},{64,32},{96,64},{128,96},{160,128},{192,160},{224,192},{0,2... | collective-permute-start | bytes 73736 | tf_op jit(solution)/shard_map/ppermute | solution.py:35
  11.3 26.1 %collective-permute-start = (f32[3,8,1,128]{3,1,0,2:T(8,128)S(1)}, f32[3,8,1,128]{3,1,0,2:T(8,128)S(1)}, u32[]{:S(2)}, u32[]{:S(2)}) collective-permute-start(f32[3,8,1,128]{3,1,0,2:T(8,128)S(1)} %bitcast.162), channel_id=1, source_target_pairs={{0,1},{1,2},{2,3},{3,4},{4,5},{5,6},{6,7},{7,8},{8,9},{9,10},{10,1... | collective-permute-start | bytes 36872 | tf_op jit(solution)/shard_map/ppermute | solution.py:34
  11.4 26.0 %collective-permute-start.1 = (f32[3,8,1,128]{3,1,0,2:T(8,128)S(1)}, f32[3,8,1,128]{3,1,0,2:T(8,128)S(1)}, u32[]{:S(2)}, u32[]{:S(2)}) collective-permute-start(f32[3,8,1,128]{3,1,0,2:T(8,128)S(1)} %bitcast.161), channel_id=1, source_target_pairs={{1,0},{2,1},{3,2},{4,3},{5,4},{6,5},{7,6},{8,7},{9,8},{10,9},{11,1... | collective-permute-start | bytes 36872 | tf_op jit(solution)/shard_map/ppermute | solution.py:35
  19.9 12.1 %copy-start.24 = (pred[8]{0:T(512)(128)(4,1)}, pred[8]{0:T(512)(128)(4,1)S(1)}, u32[]{:S(2)}) copy-start(pred[8]{0:T(512)(128)(4,1)S(1)} %compare_and_fusion) | copy-start | bytes 28
  22.2 11.0 %copy-start.18 = (s32[1024]{0:T(1024)}, s32[1024]{0:T(1024)S(1)}, u32[]{:S(2)}) copy-start(s32[1024]{0:T(1024)S(1)} %pad_clamp_fusion) | copy-start | bytes 12292
  24.5 7.5 %copy-start.22 = (s32[8]{0:T(128)}, s32[8]{0:T(128)S(1)}, u32[]{:S(2)}) copy-start(s32[8]{0:T(128)S(1)} %multiply_add_fusion) | copy-start | bytes 100
  39.7 10.7 %all-to-all-start = ((bf16[8,2,259]{2,1,0:T(2,128)(2,1)}), bf16[8,2,259]{2,1,0:T(2,128)(2,1)S(1)}, u32[]{:S(2)}, u32[]{:S(2)}) async-start(bf16[8,2,259]{2,1,0:T(2,128)(2,1)} %pad_maximum_fusion.3), calls=%async_computation | async-start | bytes 24576 | tf_op jit(solution)/shard_map/all_to_all | solution.py:51
  45.6 101.5 %all-gather.6.cloned.1.call-start = ((), (), s32[]{:S(2)}) async-start(), calls=%async_computation.4 | async-start | bytes 1179648 | tf_op jit(solution)/shard_map/all_gather | solution.py:65
  50.4 6.6 %copy-start.9 = (bf16[16,259]{1,0:T(8,128)(2,1)}, bf16[16,259]{1,0:T(8,128)(2,1)S(1)}, u32[]{:S(2)}) copy-start(bf16[16,259]{1,0:T(8,128)(2,1)S(1)} %all_to_all.29) | copy-start | bytes 24868
  51.3 5.7 %copy-start.8 = (bf16[16,256]{0,1:T(8,128)(2,1)}, bf16[16,256]{0,1:T(8,128)(2,1)S(1)}, u32[]{:S(2)}) copy-start(bf16[16,256]{0,1:T(8,128)(2,1)S(1)} %copy.121) | copy-start | bytes 24580
  52.2 27.2 %copy-start.3 = (f32[16,4,4,8,64]{4,0,3,2,1:T(8,128)}, f32[16,4,4,8,64]{4,0,3,2,1:T(8,128)S(1)}, u32[]{:S(2)}) copy-start(f32[16,4,4,8,64]{4,0,3,2,1:T(8,128)S(1)} %convolution_multiply_fusion.4) | copy-start | bytes 1572868
  58.3 4.9 %copy-start.17 = (bf16[1,2048,2]{1,2,0:T(2,128)(2,1)S(1)}, bf16[1,2048,2]{1,2,0:T(2,128)(2,1)}, u32[]{:S(2)}) copy-start(bf16[1,2048,2]{1,2,0:T(2,128)(2,1)} %param.24) | copy-start | bytes 24580
  58.4 5.0 %slice-start = ((bf16[16,259]{1,0:T(8,128)(2,1)}), bf16[16,2]{1,0:T(8,128)(2,1)S(1)}, s32[]{:S(2)}) async-start(bf16[16,259]{1,0:T(8,128)(2,1)} %copy-done.9), calls=%async_computation.6 | async-start | bytes 8192 | tf_op jit(solution)/shard_map/split | solution.py:52
  58.4 5.1 %copy-start.21 = (f32[16]{0:T(128)S(1)}, f32[16]{0:T(128)}, u32[]{:S(2)}) copy-start(f32[16]{0:T(128)} %convert_reduce_fusion) | copy-start | bytes 196
  86.1 14.6 %copy-start.13 = (f32[3,8,1,128]{3,1,0,2:T(8,128)S(1)}, f32[3,8,1,128]{3,1,0,2:T(8,128)}, u32[]{:S(2)}) copy-start(f32[3,8,1,128]{3,1,0,2:T(8,128)} %copy-done.12) | copy-start | bytes 36868
  86.1 14.6 %copy-start.15 = (f32[3,8,1,128]{3,1,0,2:T(8,128)S(1)}, f32[3,8,1,128]{3,1,0,2:T(8,128)}, u32[]{:S(2)}) copy-start(f32[3,8,1,128]{3,1,0,2:T(8,128)} %copy-done.14) | copy-start | bytes 36868
  86.1 14.6 %copy-start.4 = (f32[3,8,16,128]{3,2,1,0:T(8,128)S(1)}, f32[3,8,16,128]{3,2,1,0:T(8,128)}, u32[]{:S(2)}) copy-start(f32[3,8,16,128]{3,2,1,0:T(8,128)} %slice.227) | copy-start | bytes 589828
  86.1 14.8 %copy-start.20 = (f32[16,2]{0,1:T(2,128)S(1)}, f32[16,2]{0,1:T(2,128)}, u32[]{:S(2)}) copy-start(f32[16,2]{0,1:T(2,128)} %copy-done.19) | copy-start | bytes 388
  86.2 45.4 %copy-start.2 = (f32[3,8,16,128]{3,2,1,0:T(8,128)S(1)}, f32[3,8,16,128]{3,2,1,0:T(8,128)}, u32[]{:S(2)}) copy-start(f32[3,8,16,128]{3,2,1,0:T(8,128)} %copy-done.1) | copy-start | bytes 589828
  86.2 45.4 %copy-start.5 = (f32[8,16,128]{2,1,0:T(8,128)S(1)}, f32[8,16,128]{2,1,0:T(8,128)}, u32[]{:S(2)}) copy-start(f32[8,16,128]{2,1,0:T(8,128)} %get-tuple-element.102) | copy-start | bytes 196612
  86.2 45.4 %copy-start.6 = (f32[8,16,128]{2,1,0:T(8,128)S(1)}, f32[8,16,128]{2,1,0:T(8,128)}, u32[]{:S(2)}) copy-start(f32[8,16,128]{2,1,0:T(8,128)} %get-tuple-element.103) | copy-start | bytes 196612
  86.2 45.4 %copy-start.7 = (f32[8,16,128]{2,1,0:T(8,128)S(1)}, f32[8,16,128]{2,1,0:T(8,128)}, u32[]{:S(2)}) copy-start(f32[8,16,128]{2,1,0:T(8,128)} %get-tuple-element.104) | copy-start | bytes 196612
  86.2 46.3 %copy-start.23 = (s32[8]{0:T(128)S(1)}, s32[8]{0:T(128)}, u32[]{:S(2)}) copy-start(s32[8]{0:T(128)} %copy-done.22) | copy-start | bytes 100
  93.4 24.0 %all-to-all-start.2 = ((bf16[32,2,2358]{2,1,0:T(2,128)(2,1)}), bf16[32,2,2358]{2,1,0:T(2,128)(2,1)S(1)}, u32[]{:S(2)}, u32[]{:S(2)}) async-start(bf16[32,2,2358]{2,1,0:T(2,128)(2,1)} %reshape.374), calls=%async_computation.2 | async-start | bytes 622592 | tf_op jit(solution)/shard_map/all_to_all | solution.py:89
  117.4 10.2 %all-to-all-start.1 = ((f32[8,2,2]{1,2,0:T(2,128)}), f32[8,2,2]{1,2,0:T(2,128)S(1)}, u32[]{:S(2)}, u32[]{:S(2)}) async-start(f32[8,2,2]{1,2,0:T(2,128)} %copy.125), calls=%async_computation.1 | async-start | bytes 16384 | tf_op jit(solution)/shard_map/all_to_all | solution.py:284
  123.3 25.9 %copy-start.11 = (bf16[1,54,64]{2,1,0:T(8,128)(2,1)S(1)}, bf16[1,54,64]{2,1,0:T(8,128)(2,1)}, u32[]{:S(2)}) copy-start(bf16[1,54,64]{2,1,0:T(8,128)(2,1)} %param.21) | copy-start | bytes 20740
  127.6 16.8 %all-to-all-start.3 = ((bf16[32,2,1846]{2,1,0:T(2,128)(2,1)}), bf16[32,2,1846]{2,1,0:T(2,128)(2,1)S(1)}, u32[]{:S(2)}, u32[]{:S(2)}) async-start(bf16[32,2,1846]{2,1,0:T(2,128)(2,1)} %reshape.376), calls=%async_computation.3 | async-start | bytes 491520 | tf_op jit(solution)/shard_map/all_to_all | solution.py:78
  131.5 26.8 %all-gather.8.cloned.1.call-start = ((), (), s32[]{:S(2)}) async-start(), calls=%async_computation.5 | async-start | bytes 3145728 | tf_op jit(solution)/shard_map/all_gather | solution.py:65
  (4 other events, 5.8 us)
Sparse Core Ops, SparseCore 0:
  86.1 39.2 all-gather.5
  147.2 11.0 all-gather.7

commit v11 on v9

--- a/solution.py
+++ b/solution.py
@@ -51,26 +51,6 @@
     whole = lax.all_to_all(both, axis, split_axis=split_dim, concat_axis=concat_dim, tiled=True)
     tiles = jnp.split(whole, [sum(widths[:k]) for k in range(1, len(widths))], axis=along)
     return tuple((b.reshape(*whole.shape[:along], *a.shape[along:]) for a, b in zip(arrays, tiles)))
-
-
-def joined_along(tiles, dim):
-    lengths = list(tiles.shape[1:])
-    lengths[dim] *= tiles.shape[0]
-    return jnp.moveaxis(tiles, 0, dim).reshape(lengths)
-
-
-def gather_in_order(shard, axes, order):
-    tiles = shard
-    for k in order:
-        tiles = lax.all_gather(tiles, axes[k])
-    done = order[::-1]
-    back = [done.index(k) for k in range(len(axes))]
-    tiles = tiles.transpose(*back, *range(len(axes), tiles.ndim))
-    return tiles.reshape(-1, *shard.shape)
-
-
-def gathered_by_axis(shard, axes, order, dim):
-    return joined_along(gather_in_order(shard, axes, order), dim)
 
 
 def from_everyone(shard, axis):
@@ -289,10 +269,17 @@
     small = jnp.concatenate([grad_one.ravel(), grad_out.ravel()])
     tiles = features.reshape(features.shape[0], flow_count, -1).transpose(1, 0, 2)
     grad_share, small_part, columns_here = owner_sums(grad_two.reshape(-1, CH), small, tiles, STREAM)
+    gather_order = (1, 0, 2)
+    stacked = delta_three
+    for k in gather_order:
+        stacked = lax.all_gather(stacked, STREAM[k])
+    sizes = [lax.axis_size(name) for name in STREAM]
+    columns_here = columns_here.reshape(*sizes, delta_three.shape[0], -1)
+    columns_here = columns_here.transpose(*gather_order[::-1], 3, 4).reshape(stacked.size // FEATS, -1)
     grad_hidden = (
         jnp.dot(
             columns_here.T,
-            gathered_by_axis(delta_three, STREAM, (1, 0, 2), 0),
+            stacked.reshape(-1, FEATS),
             preferred_element_type=jnp.float32,
         )
         * dense_scale

time: 160 us -> 164 us (1.025)
  waiting for transfers between devices: 34.8 us -> 30.1 us
  matrix products: 28.9 us -> 33.4 us
  other arithmetic: 13.5 us -> 16.9 us
  starting transfers between devices: 34.4 us -> 31.5 us
  local copies, waits for them, and re-layouts: 25.6 us -> 27.7 us
    all_to_all x1, waiting for transfers between devices: 13.9 us -> 8.36 us  [from_everyone(): return lax.all_to_all(copies, axis, split_axis=0, concat_axis=0, tiled=True)]
    scatter-add x2, local copies, waits for them, and re-layouts: 0.42 us -> 3.17 us  [body(): grad_x = along_x[:, :, :size_x].at[:, :, 0].add(-lift_half * left_face).a...]
    transpose x1 -> x0, local copies, waits for them, and re-layouts: 1.76 us -> none  [gather_in_order(): tiles = tiles.transpose(*back, *range(len(axes), tiles.ndim))]
    all_to_all x1, starting transfers between devices: 6.15 us -> 4.4 us  [from_everyone(): return lax.all_to_all(copies, axis, split_axis=0, concat_axis=0, tiled=True)]
    dot_general x1, matrix products: 0.6 us -> 2.28 us  [body(): jnp.dot(columns_here.T, stacked.reshape(-1, FEATS), preferred_element_typ...]
    unnamed x48 -> x38, local copies, waits for them, and re-layouts: 4.31 us -> 4.29 us
  transfers between devices with their start and end apart: 10 -> 10, of which waited for: 5 -> 5; matrix products, arithmetic and copies ran while one was open for 22% -> 27% of each run, Pallas kernels for 0% -> 0%
where the time goes in v11:
time: 164 us; the launch traced here: 162 us
  matrix products  33.4 us (20%)
  starting transfers between devices  31.5 us (19%)
  waiting for transfers between devices  30.1 us (18%)
  local copies, waits for them, and re-layouts  27.7 us (17%)
  other arithmetic  16.9 us (10%)
  between operations  15.3 us (9%)
  blocking collectives  6.78 us (4%)
    all_to_all x1, waiting for transfers between devices, owner_sums(): lax.all_to_all(both, axis, split_axis=0, concat_axis=0, tiled=True)  15.5 us
    transpose x2, matrix products, conv_filter(): return jnp.moveaxis(taps, 0, 3)  10.2 us
    all_to_all x1, waiting for transfers between devices, from_everyone(): return lax.all_to_all(copies, axis, split_axis=0, concat_axis=0, tiled=True)  8.36 us
    ppermute x2, starting transfers between devices, extended(): lax.ppermute(first, axis, [(b, a) for a, b in up])  7.98 us
    all_to_all x1, starting transfers between devices, owner_sums(): lax.all_to_all(both, axis, split_axis=0, concat_axis=0, tiled=True)  7.28 us
    all_gather x1, blocking collectives, body(): stacked = lax.all_gather(stacked, STREAM[k])  6.78 us
    all_to_all x1, starting transfers between devices, in_one_piece(): lax.all_to_all(both, axis, split_axis=split_dim, concat_axis=concat_dim,...  5.88 us
    conv_general_dilated x2, matrix products, conv_taps(): lax.conv_general_dilated(grid, kernel, (1, 1, 1), SAME, dimension_numbers...  5.7 us
  transfers between devices with their start and end apart: 10, of which 5 were waited for; matrix products, arithmetic and copies ran while one was open for 27% of the time, Pallas kernels for 0%

profile of v11, /device:TPU:2, one launch (start us, length us, event | category | flops | bytes accessed | tf_op | source)
XLA Modules:
  0.0 161.8 jit_solution(7671534674165759874)
XLA Ops:
  8.0 1.5 collective-permute-start.2
  10.4 1.0 fusion.50
  11.4 7.1 %collective-permute-start.1 = (f32[3,8,1,128]{3,1,0,2:T(8,128)S(1)}, f32[3,8,1,128]{3,1,0,2:T(8,128)S(1)}, u32[]{:S(2)}, u32[]{:S(2)}) collective-permute-start(f32[3,8,1,128]{3,1,0,2:T(8,128)S(1)} %bitcast.164), channel_id=1, source_target_pairs={{1,0},{2,1},{3,2},{4,3},{5,4},{6,5},{7,6},{8,7},{9,8},{10,9},{11,1... | collective-permute-start | bytes 36872 | tf_op jit(solution)/shard_map/ppermute | solution.py:35
  20.8 1.5 fusion.25
  24.5 1.2 reshape.312
  28.6 1.1 reshape.315
  31.8 5.9 %all-to-all-start = ((bf16[8,2,259]{2,1,0:T(2,128)(2,1)}), bf16[8,2,259]{2,1,0:T(2,128)(2,1)S(1)}, u32[]{:S(2)}, u32[]{:S(2)}) async-start(bf16[8,2,259]{2,1,0:T(2,128)(2,1)} %pad_maximum_fusion.4), calls=%async_computation | async-start | bytes 24576 | tf_op jit(solution)/shard_map/all_to_all | solution.py:51
  39.3 3.2 %all-to-all-done = bf16[8,2,259]{2,1,0:T(2,128)(2,1)S(1)} async-done(((bf16[8,2,259]{2,1,0:T(2,128)(2,1)}), bf16[8,2,259]{2,1,0:T(2,128)(2,1)S(1)}, u32[]{:S(2)}, u32[]{:S(2)}) %all-to-all-start) | async-done | bytes 8320 | tf_op jit(solution)/shard_map/all_to_all | solution.py:51
  43.8 4.8 %fusion.17 = (f32[16,4,4,8,64]{4,0,3,2,1:T(8,128)}, f32[16,4,4,8,64]{4,0,3,2,1:T(8,128)}) fusion(bf16[3,3,3,64,64]{4,3,2,1,0:T(8,128)(2,1)} %bitcast.168, f32[16,4,4,8,64]{4,0,3,2,1:T(8,128)S(1)} %convolution_multiply_fusion.4), kind=kOutput, calls=%fused_computation.32 | convolution fusion | flops 289669120 | bytes 1794048 | tf_op jit(solution)/shard_map/conv_general_dilated | solution.py:137
  48.6 1.3 reduce_sum.84
  50.2 4.6 %multiply_convert_fusion.3 = (bf16[16,2048]{1,0:T(8,128)(2,1)S(1)}, f32[16,2048]{1,0:T(8,128)S(1)}) fusion(bf16[16,2048]{1,0:T(8,128)(2,1)S(1)} %convert_element_type.114, bf16[1,2048,2048]{2,1,0:T(8,128)(2,1)} %param.23), kind=kOutput, calls=%fused_computation.58 | convolution fusion | flops 134414336 | bytes 8650752 | tf_op jit(solution)/shard_map/dot_general | solution.py:166
  55.5 5.6 %fusion.8 = f32[16,2048]{1,0:T(8,128)S(1)} fusion(bf16[16,2048]{1,0:T(8,128)(2,1)S(1)} %fusion.11, bf16[1,2048,2048]{2,1,0:T(8,128)(2,1)} %param.23), kind=kOutput, calls=%fused_computation.10 | convolution fusion | flops 134250496 | bytes 8585216 | tf_op jit(solution)/shard_map/dot_general | solution.py:174
  61.2 6.8 %all-gather = bf16[32,2048]{1,0:T(8,128)(2,1)} all-gather(bf16[16,2048]{1,0:T(8,128)(2,1)S(1)} %fusion.11), channel_id=2, replica_groups=mesh['wall'=8,'stream_0'=8,'stream_1'=2,'stream_2'=2] {'stream_1'}, dimensions={0}, use_global_device_ids=true | all-gather | bytes 196608 | tf_op jit(solution)/shard_map/all_gather | solution.py:275
  68.3 1.6 %multiply_convert_fusion = bf16[16,4,4,8,64]{4,0,3,2,1:T(8,128)(2,1)S(1)} fusion(f32[16,4,4,8,64]{4,0,3,2,1:T(8,128)S(1)} %bitcast.141, f32[16,4,4,8,64]{4,0,3,2,1:T(8,128)} %get-tuple-element.114), kind=kLoop, calls=%fused_computation.30 | loop fusion | flops 1179648 | bytes 1310720 | tf_op jit(solution)/shard_map/convert_element_type | solution.py:177
  70.0 5.5 %fusion.16 = bf16[3,3,3,2,64]{4,3,2,1,0:T(2,128)(2,1)S(1)} fusion(bf16[16,2,4,4,8]{0,4,3,2,1:T(8,128)(2,1)S(1)} %bitcast.157, bf16[16,4,4,8,64]{4,0,3,2,1:T(8,128)(2,1)S(1)} %multiply_convert_fusion, bf16[3,3,3,64,64]{4,3,2,1,0:T(8,128)(2,1)S(1)} %bitcast.170, f32[16,4,4,8,64]{4,0,3,2,1:T(8,128)} %copy-done.3), kind=kOutput, calls=%fused_computation.24 | convolution fusion | flops 298687232 | bytes 1022720 | tf_op jit(solution)/shard_map/transpose | solution.py:148
  76.7 4.8 %fusion.15 = bf16[3,3,3,64,64]{4,3,2,1,0:T(8,128)(2,1)} fusion(bf16[16,4,4,8,64]{4,0,3,2,1:T(8,128)(2,1)S(1)} %multiply_convert_fusion, f32[16,4,4,8,64]{4,0,3,2,1:T(8,128)} %copy-done.3), kind=kOutput, calls=%fused_computation.20 | convolution fusion | flops 289234944 | bytes 1007616 | tf_op jit(solution)/shard_map/transpose | solution.py:148
  81.5 1.3 convert_element_type.123
  84.3 1.1 reshape.351
  85.4 7.3 %all-to-all-start.2 = ((bf16[32,2,2358]{2,1,0:T(2,128)(2,1)}), bf16[32,2,2358]{2,1,0:T(2,128)(2,1)S(1)}, u32[]{:S(2)}, u32[]{:S(2)}) async-start(bf16[32,2,2358]{2,1,0:T(2,128)(2,1)} %reshape.351), calls=%async_computation.2 | async-start | bytes 622592 | tf_op jit(solution)/shard_map/all_to_all | solution.py:69
  94.6 15.5 %all-to-all-done.2 = bf16[32,2,2358]{2,1,0:T(2,128)(2,1)S(1)} async-done(((bf16[32,2,2358]{2,1,0:T(2,128)(2,1)}), bf16[32,2,2358]{2,1,0:T(2,128)(2,1)S(1)}, u32[]{:S(2)}, u32[]{:S(2)}) %all-to-all-start.2) | async-done | bytes 301856 | tf_op jit(solution)/shard_map/all_to_all | solution.py:69
  110.1 4.4 %all-to-all-start.1 = ((f32[8,2,2]{1,2,0:T(2,128)}), f32[8,2,2]{1,2,0:T(2,128)S(1)}, u32[]{:S(2)}, u32[]{:S(2)}) async-start(f32[8,2,2]{1,2,0:T(2,128)} %copy.126), calls=%async_computation.1 | async-start | bytes 16384 | tf_op jit(solution)/shard_map/all_to_all | solution.py:264
  116.9 2.4 %all-to-all-done.1 = f32[8,2,2]{1,2,0:T(2,128)S(1)} async-done(((f32[8,2,2]{1,2,0:T(2,128)}), f32[8,2,2]{1,2,0:T(2,128)S(1)}, u32[]{:S(2)}, u32[]{:S(2)}) %all-to-all-start.1) | async-done | bytes 160 | tf_op jit(solution)/shard_map/all_to_all | solution.py:264
  119.3 1.0 broadcast_in_dim.48
  120.3 4.4 %all-to-all-start.3 = ((f32[32,1,3692]{2,1,0:T(1,128)}), f32[32,1,3692]{2,1,0:T(1,128)S(1)}, u32[]{:S(2)}, u32[]{:S(2)}) async-start(f32[32,1,3692]{2,1,0:T(1,128)} %broadcast_in_dim.48), calls=%async_computation.3 | async-start | bytes 950272 | tf_op jit(solution)/shard_map/all_to_all | solution.py:58
  124.8 1.6 scatter-add.16
  127.3 1.6 scatter-add.19
  128.9 1.9 %fusion.22 = f32[3,8,16,128]{3,2,1,0:T(8,128)} fusion(f32[3,8,16,128]{3,2,1,0:T(8,128)S(1)} %copy-done, f32[3,8,16,256]{3,2,1,0:T(8,128)S(1)} %convolution_bitcast_fusion.1, f32[3,16,16,128]{3,2,1,0:T(8,128)S(1)} %bitcast.148, f32[3,8,32,128]{3,2,1,0:T(8,128)S(1)} %convolution_bitcast_fusion.2, f32[3,8,16,128]{3,2,1,0:T(8,128)S(1)} %fusion.32, ...), kind=kLoop, calls=%fused_computation.47 | loop fusion | flops 589824 | bytes 1769472 | tf_op jit(solution)/shard_map/add | solution.py:257
  130.8 1.4 fusion.37
  133.1 8.4 %all-to-all-done.3 = f32[32,1,3692]{2,1,0:T(1,128)S(1)} async-done(((f32[32,1,3692]{2,1,0:T(1,128)}), f32[32,1,3692]{2,1,0:T(1,128)S(1)}, u32[]{:S(2)}, u32[]{:S(2)}) %all-to-all-start.3) | async-done | bytes 472608 | tf_op jit(solution)/shard_map/all_to_all | solution.py:58
  146.3 2.1 %broadcast_in_dim_reshape_reshape.3 = f32[1,27,64,64]{3,2,1,0:T(8,128)} reshape(f32[32,3456]{1,0:T(8,128)} %slice.239) | data formatting | bytes 884736 | tf_op jit(solution)/shard_map/broadcast_in_dim;reshape;reshape | solution.py:300
  150.8 2.3 %multiply_reduce_fusion.1 = (f32[64]{0:T(128)S(1)}, f32[64,2048]{1,0:T(8,128)S(1)}) fusion(bf16[2,8,2,16,2048]{4,3,2,1,0:T(8,128)(2,1)} %bitcast.143, bf16[8,2,2,16,64]{4,3,2,1,0:T(8,128)(2,1)} %reshape_reshape.8), kind=kOutput, calls=%fused_computation.37 | convolution fusion | flops 134610880 | bytes 2687232 | tf_op jit(solution)/shard_map/dot_general | solution.py:280
  153.1 1.9 %fusion.18 = f32[1,64,2048]{2,1,0:T(8,128)} fusion(f32[64,2048]{1,0:T(8,128)S(1)} %get-tuple-element.118, f32[64]{0:T(128)S(1)} %add_sqrt_fusion, bf16[1,2048,2048]{2,1,0:T(8,128)(2,1)} %param.23, s32[]{:T(128)S(6)} %select_n.37), kind=kLoop, calls=%fused_computation.36 | loop fusion | flops 524288 | bytes 1310980 | tf_op jit(solution)/shard_map/broadcast_in_dim | solution.py:288
  (139 shorter events, 30.5 us)
Async XLA Ops:
  7.2 30.5 %copy-start.12 = (f32[32,16,1,1]{0,1,3,2:T(8,128)S(1)}, f32[32,16,1,1]{0,1,3,2:T(8,128)}, u32[]{:S(2)}) copy-start(f32[32,16,1,1]{0,1,3,2:T(8,128)} %constant.249) | copy-start | bytes 6148
  7.2 30.5 %copy-start = (f32[3,8,16,128]{3,2,1,0:T(8,128)S(1)}, f32[3,8,16,128]{3,2,1,0:T(8,128)}, u32[]{:S(2)}) copy-start(f32[3,8,16,128]{3,2,1,0:T(8,128)} %param.18) | copy-start | bytes 589828
  7.2 31.0 %copy-start.6 = (bf16[1,54,64]{2,1,0:T(8,128)(2,1)S(1)}, bf16[1,54,64]{2,1,0:T(8,128)(2,1)}, u32[]{:S(2)}) copy-start(bf16[1,54,64]{2,1,0:T(8,128)(2,1)} %param.21) | copy-start | bytes 20740
  7.2 31.1 %copy-start.11 = (bf16[1,2048,2]{1,2,0:T(2,128)(2,1)S(1)}, bf16[1,2048,2]{1,2,0:T(2,128)(2,1)}, u32[]{:S(2)}) copy-start(bf16[1,2048,2]{1,2,0:T(2,128)(2,1)} %param.24) | copy-start | bytes 24580
  8.0 19.8 %collective-permute-start.2 = (f32[3,1,16,128]{3,2,1,0:T(8,128)S(1)}, f32[3,1,16,128]{3,2,1,0:T(8,128)S(1)}, u32[]{:S(2)}, u32[]{:S(2)}) collective-permute-start(f32[3,1,16,128]{3,2,1,0:T(8,128)S(1)} %get-tuple-element.110), channel_id=1, source_target_pairs={{0,32},{32,64},{64,96},{96,128},{128,160},{160,192},{192,224},{224... | collective-permute-start | bytes 73736 | tf_op jit(solution)/shard_map/ppermute | solution.py:34
  9.5 18.4 %collective-permute-start.3 = (f32[3,1,16,128]{3,2,1,0:T(8,128)S(1)}, f32[3,1,16,128]{3,2,1,0:T(8,128)S(1)}, u32[]{:S(2)}, u32[]{:S(2)}) collective-permute-start(f32[3,1,16,128]{3,2,1,0:T(8,128)S(1)} %get-tuple-element.109), channel_id=1, source_target_pairs={{32,0},{64,32},{96,64},{128,96},{160,128},{192,160},{224,192},{0,2... | collective-permute-start | bytes 73736 | tf_op jit(solution)/shard_map/ppermute | solution.py:35
  11.3 19.6 %collective-permute-start = (f32[3,8,1,128]{3,1,0,2:T(8,128)S(1)}, f32[3,8,1,128]{3,1,0,2:T(8,128)S(1)}, u32[]{:S(2)}, u32[]{:S(2)}) collective-permute-start(f32[3,8,1,128]{3,1,0,2:T(8,128)S(1)} %bitcast.165), channel_id=1, source_target_pairs={{0,1},{1,2},{2,3},{3,4},{4,5},{5,6},{6,7},{7,8},{8,9},{9,10},{10,1... | collective-permute-start | bytes 36872 | tf_op jit(solution)/shard_map/ppermute | solution.py:34
  11.4 19.5 %collective-permute-start.1 = (f32[3,8,1,128]{3,1,0,2:T(8,128)S(1)}, f32[3,8,1,128]{3,1,0,2:T(8,128)S(1)}, u32[]{:S(2)}, u32[]{:S(2)}) collective-permute-start(f32[3,8,1,128]{3,1,0,2:T(8,128)S(1)} %bitcast.164), channel_id=1, source_target_pairs={{1,0},{2,1},{3,2},{4,3},{5,4},{6,5},{7,6},{8,7},{9,8},{10,9},{11,1... | collective-permute-start | bytes 36872 | tf_op jit(solution)/shard_map/ppermute | solution.py:35
  24.5 24.1 %copy-start.14 = (s32[8]{0:T(128)}, s32[8]{0:T(128)S(1)}, u32[]{:S(2)}) copy-start(s32[8]{0:T(128)S(1)} %multiply_add_fusion) | copy-start | bytes 100
  27.8 0.7 copy-start.1
  30.9 17.7 %copy-start.7 = (f32[3,8,1,128]{3,1,0,2:T(8,128)}, f32[3,8,1,128]{3,1,0,2:T(8,128)S(1)}, u32[]{:S(2)}) copy-start(f32[3,8,1,128]{3,1,0,2:T(8,128)S(1)} %collective-permute-done) | copy-start | bytes 36868
  30.9 17.7 %copy-start.9 = (f32[3,8,1,128]{3,1,0,2:T(8,128)}, f32[3,8,1,128]{3,1,0,2:T(8,128)S(1)}, u32[]{:S(2)}) copy-start(f32[3,8,1,128]{3,1,0,2:T(8,128)S(1)} %collective-permute-done.1) | copy-start | bytes 36868
  31.8 10.7 %all-to-all-start = ((bf16[8,2,259]{2,1,0:T(2,128)(2,1)}), bf16[8,2,259]{2,1,0:T(2,128)(2,1)S(1)}, u32[]{:S(2)}, u32[]{:S(2)}) async-start(bf16[8,2,259]{2,1,0:T(2,128)(2,1)} %pad_maximum_fusion.4), calls=%async_computation | async-start | bytes 24576 | tf_op jit(solution)/shard_map/all_to_all | solution.py:51
  37.7 79.2 %all-gather.6.cloned.1.call-start = ((), (), s32[]{:S(2)}) async-start(), calls=%async_computation.4 | async-start | bytes 1179648 | tf_op jit(solution)/shard_map/all_gather | solution.py:275
  42.5 6.1 %copy-start.5 = (bf16[16,259]{1,0:T(8,128)(2,1)}, bf16[16,259]{1,0:T(8,128)(2,1)S(1)}, u32[]{:S(2)}) copy-start(bf16[16,259]{1,0:T(8,128)(2,1)S(1)} %all_to_all.29) | copy-start | bytes 24868
  43.8 4.8 %copy-start.3 = (f32[16,4,4,8,64]{4,0,3,2,1:T(8,128)}, f32[16,4,4,8,64]{4,0,3,2,1:T(8,128)S(1)}, u32[]{:S(2)}) copy-start(f32[16,4,4,8,64]{4,0,3,2,1:T(8,128)S(1)} %convolution_multiply_fusion.4) | copy-start | bytes 1572868
  50.0 5.0 %slice-start = ((bf16[16,259]{1,0:T(8,128)(2,1)}), bf16[16,2]{1,0:T(8,128)(2,1)S(1)}, s32[]{:S(2)}) async-start(bf16[16,259]{1,0:T(8,128)(2,1)} %copy-done.5), calls=%async_computation.6 | async-start | bytes 8192 | tf_op jit(solution)/shard_map/split | solution.py:52
  54.8 15.1 %copy-start.13 = (bf16[1,27,64,64]{3,2,1,0:T(8,128)(2,1)S(1)}, bf16[1,27,64,64]{3,2,1,0:T(8,128)(2,1)}, u32[]{:S(2)}) copy-start(bf16[1,27,64,64]{3,2,1,0:T(8,128)(2,1)} %param.22) | copy-start | bytes 663556
  76.7 16.7 %copy-start.4 = (f32[256,128,1,1]{1,0,3,2:T(8,128)S(1)}, f32[256,128,1,1]{1,0,3,2:T(8,128)}, u32[]{:S(2)}) copy-start(f32[256,128,1,1]{1,0,3,2:T(8,128)} %constant.251) | copy-start | bytes 393220
  76.7 17.2 %copy-start.8 = (f32[3,8,1,128]{3,1,0,2:T(8,128)S(1)}, f32[3,8,1,128]{3,1,0,2:T(8,128)}, u32[]{:S(2)}) copy-start(f32[3,8,1,128]{3,1,0,2:T(8,128)} %copy-done.7) | copy-start | bytes 36868
  76.7 17.2 %copy-start.10 = (f32[3,8,1,128]{3,1,0,2:T(8,128)S(1)}, f32[3,8,1,128]{3,1,0,2:T(8,128)}, u32[]{:S(2)}) copy-start(f32[3,8,1,128]{3,1,0,2:T(8,128)} %copy-done.9) | copy-start | bytes 36868
  76.7 52.2 %copy-start.2 = (f32[16,3,16,128]{3,2,0,1:T(8,128)S(1)}, f32[16,3,16,128]{3,2,0,1:T(8,128)}, u32[]{:S(2)}) copy-start(f32[16,3,16,128]{3,2,0,1:T(8,128)} %copy-done.1) | copy-start | bytes 1179652
  85.4 24.7 %all-to-all-start.2 = ((bf16[32,2,2358]{2,1,0:T(2,128)(2,1)}), bf16[32,2,2358]{2,1,0:T(2,128)(2,1)S(1)}, u32[]{:S(2)}, u32[]{:S(2)}) async-start(bf16[32,2,2358]{2,1,0:T(2,128)(2,1)} %reshape.351), calls=%async_computation.2 | async-start | bytes 622592 | tf_op jit(solution)/shard_map/all_to_all | solution.py:69
  110.1 9.2 %all-to-all-start.1 = ((f32[8,2,2]{1,2,0:T(2,128)}), f32[8,2,2]{1,2,0:T(2,128)S(1)}, u32[]{:S(2)}, u32[]{:S(2)}) async-start(f32[8,2,2]{1,2,0:T(2,128)} %copy.126), calls=%async_computation.1 | async-start | bytes 16384 | tf_op jit(solution)/shard_map/all_to_all | solution.py:264
  114.5 36.2 %all-gather.8.cloned.1.call-start = ((), (), s32[]{:S(2)}) async-start(), calls=%async_computation.5 | async-start | bytes 3145728 | tf_op jit(solution)/shard_map/all_gather | solution.py:275
  120.3 21.1 %all-to-all-start.3 = ((f32[32,1,3692]{2,1,0:T(1,128)}), f32[32,1,3692]{2,1,0:T(1,128)S(1)}, u32[]{:S(2)}, u32[]{:S(2)}) async-start(f32[32,1,3692]{2,1,0:T(1,128)} %broadcast_in_dim.48), calls=%async_computation.3 | async-start | bytes 950272 | tf_op jit(solution)/shard_map/all_to_all | solution.py:58
Sparse Core Ops, SparseCore 0:
  76.8 40.0 all-gather.5
  118.7 13.9 all-gather.7

commit v12 on v9

--- a/solution.py
+++ b/solution.py
@@ -292,7 +292,7 @@
     grad_hidden = (
         jnp.dot(
             columns_here.T,
-            gathered_by_axis(delta_three, STREAM, (1, 0, 2), 0),
+            gathered_by_axis(delta_three, STREAM, (2, 0, 1), 0),
             preferred_element_type=jnp.float32,
         )
         * dense_scale

time: 160 us -> 167 us (1.044)
  waiting for transfers between devices: 34.8 us -> 44.8 us
  blocking collectives: 6.78 us -> 2.26 us
    all_gather x2, waiting for transfers between devices: 0.96 us -> 11 us  [gather_in_order(): tiles = lax.all_gather(tiles, axes[k])]
    all_gather x1, blocking collectives: 6.78 us -> 2.26 us  [gather_in_order(): tiles = lax.all_gather(tiles, axes[k])]
  transfers between devices with their start and end apart: 10 -> 10, of which waited for: 5 -> 6; matrix products, arithmetic and copies ran while one was open for 22% -> 21% of each run, Pallas kernels for 0% -> 0%
where the time goes in v12:
time: 167 us; the launch traced here: 165 us
  waiting for transfers between devices  44.8 us (27%)
  starting transfers between devices  34.5 us (21%)
  matrix products  28.9 us (17%)
  local copies, waits for them, and re-layouts  25.6 us (15%)
  between operations  15.4 us (9%)
  other arithmetic  13.5 us (8%)
  blocking collectives  2.26 us (1%)
    all_to_all x1, waiting for transfers between devices, owner_sums(): lax.all_to_all(both, axis, split_axis=0, concat_axis=0, tiled=True)  14.6 us
    all_to_all x1, waiting for transfers between devices, from_everyone(): return lax.all_to_all(copies, axis, split_axis=0, concat_axis=0, tiled=True)  13.9 us
    all_gather x2, waiting for transfers between devices, gather_in_order(): tiles = lax.all_gather(tiles, axes[k])  11 us
    transpose x2, matrix products, conv_filter(): return jnp.moveaxis(taps, 0, 3)  9.39 us
    ppermute x2, starting transfers between devices, extended(): lax.ppermute(first, axis, [(b, a) for a, b in up])  7.98 us
    all_to_all x1, starting transfers between devices, owner_sums(): lax.all_to_all(both, axis, split_axis=0, concat_axis=0, tiled=True)  7.28 us
    all_to_all x1, starting transfers between devices, from_everyone(): return lax.all_to_all(copies, axis, split_axis=0, concat_axis=0, tiled=True)  6.16 us
    all_to_all x1, starting transfers between devices, in_one_piece(): lax.all_to_all(both, axis, split_axis=split_dim, concat_axis=concat_dim,...  5.88 us
  transfers between devices with their start and end apart: 10, of which 6 were waited for; matrix products, arithmetic and copies ran while one was open for 21% of the time, Pallas kernels for 0%

profile of v12, /device:TPU:2, one launch (start us, length us, event | category | flops | bytes accessed | tf_op | source)
XLA Modules:
  0.0 164.9 jit_solution(6560184655113838543)
XLA Ops:
  7.9 1.5 collective-permute-start.2
  10.3 1.0 fusion.48
  11.3 7.1 %collective-permute-start.1 = (f32[3,8,1,128]{3,1,0,2:T(8,128)S(1)}, f32[3,8,1,128]{3,1,0,2:T(8,128)S(1)}, u32[]{:S(2)}, u32[]{:S(2)}) collective-permute-start(f32[3,8,1,128]{3,1,0,2:T(8,128)S(1)} %bitcast.160), channel_id=1, source_target_pairs={{1,0},{2,1},{3,2},{4,3},{5,4},{6,5},{7,6},{8,7},{9,8},{10,9},{11,1... | collective-permute-start | bytes 36872 | tf_op jit(solution)/shard_map/ppermute | solution.py:35
  19.8 0.9 fusion.47
  20.7 1.5 fusion.25
  24.4 1.2 reshape.313
  28.5 1.1 reshape.316
  31.8 5.9 %all-to-all-start = ((bf16[8,2,259]{2,1,0:T(2,128)(2,1)}), bf16[8,2,259]{2,1,0:T(2,128)(2,1)S(1)}, u32[]{:S(2)}, u32[]{:S(2)}) async-start(bf16[8,2,259]{2,1,0:T(2,128)(2,1)} %pad_maximum_fusion.4), calls=%async_computation | async-start | bytes 24576 | tf_op jit(solution)/shard_map/all_to_all | solution.py:51
  39.3 3.2 %all-to-all-done = bf16[8,2,259]{2,1,0:T(2,128)(2,1)S(1)} async-done(((bf16[8,2,259]{2,1,0:T(2,128)(2,1)}), bf16[8,2,259]{2,1,0:T(2,128)(2,1)S(1)}, u32[]{:S(2)}, u32[]{:S(2)}) %all-to-all-start) | async-done | bytes 8320 | tf_op jit(solution)/shard_map/all_to_all | solution.py:51
  42.8 0.9 convolution_multiply_fusion.4
  43.7 3.5 %fusion.17 = (f32[16,4,4,8,64]{4,0,3,2,1:T(8,128)}, f32[16,4,4,8,64]{4,0,3,2,1:T(8,128)}) fusion(bf16[3,3,3,64,64]{4,3,2,1,0:T(8,128)(2,1)S(1)} %bitcast.165, f32[16,4,4,8,64]{4,0,3,2,1:T(8,128)S(1)} %convolution_multiply_fusion.4), kind=kOutput, calls=%fused_computation.31 | convolution fusion | flops 289669120 | bytes 1794048 | tf_op jit(solution)/shard_map/conv_general_dilated | solution.py:157
  47.2 1.3 reduce_sum.84
  48.8 4.6 %multiply_convert_fusion.3 = (bf16[16,2048]{1,0:T(8,128)(2,1)S(1)}, f32[16,2048]{1,0:T(8,128)S(1)}) fusion(bf16[16,2048]{1,0:T(8,128)(2,1)S(1)} %convert_element_type.114, bf16[1,2048,2048]{2,1,0:T(8,128)(2,1)} %param.23), kind=kOutput, calls=%fused_computation.55 | convolution fusion | flops 134414336 | bytes 8650752 | tf_op jit(solution)/shard_map/dot_general | solution.py:186
  54.1 5.6 %fusion.8 = f32[16,2048]{1,0:T(8,128)S(1)} fusion(bf16[16,2048]{1,0:T(8,128)(2,1)S(1)} %fusion.11, bf16[1,2048,2048]{2,1,0:T(8,128)(2,1)} %param.23), kind=kOutput, calls=%fused_computation.9 | convolution fusion | flops 134250496 | bytes 8585216 | tf_op jit(solution)/shard_map/dot_general | solution.py:194
  59.7 2.3 %all-gather = bf16[32,2048]{1,0:T(8,128)(2,1)} all-gather(bf16[16,2048]{1,0:T(8,128)(2,1)S(1)} %fusion.11), channel_id=2, replica_groups=mesh['wall'=8,'stream_0'=8,'stream_1'=2,'stream_2'=2] {'stream_2'}, dimensions={0}, use_global_device_ids=true | all-gather | bytes 196608 | tf_op jit(solution)/shard_map/all_gather | solution.py:65
  62.4 1.6 multiply_convert_fusion
  64.0 5.4 %fusion.16 = bf16[3,3,3,2,64]{4,3,2,1,0:T(2,128)(2,1)S(1)} fusion(bf16[16,2,4,4,8]{0,4,3,2,1:T(8,128)(2,1)S(1)} %bitcast.153, bf16[16,4,4,8,64]{4,0,3,2,1:T(8,128)(2,1)S(1)} %multiply_convert_fusion, bf16[3,3,3,64,64]{4,3,2,1,0:T(8,128)(2,1)S(1)} %bitcast.166, f32[16,4,4,8,64]{4,0,3,2,1:T(8,128)} %copy-done.3), kind=kOutput, calls=%fused_computation.23 | convolution fusion | flops 298687232 | bytes 1022720 | tf_op jit(solution)/shard_map/transpose | solution.py:168
  70.7 3.9 %fusion.15 = bf16[3,3,3,64,64]{4,3,2,1,0:T(8,128)(2,1)S(1)} fusion(bf16[16,4,4,8,64]{4,0,3,2,1:T(8,128)(2,1)S(1)} %multiply_convert_fusion, f32[16,4,4,8,64]{4,0,3,2,1:T(8,128)} %copy-done.3), kind=kOutput, calls=%fused_computation.19 | convolution fusion | flops 289234944 | bytes 1007616 | tf_op jit(solution)/shard_map/transpose | solution.py:168
  76.5 1.1 reshape.352
  77.5 7.3 %all-to-all-start.2 = ((bf16[32,2,2358]{2,1,0:T(2,128)(2,1)}), bf16[32,2,2358]{2,1,0:T(2,128)(2,1)S(1)}, u32[]{:S(2)}, u32[]{:S(2)}) async-start(bf16[32,2,2358]{2,1,0:T(2,128)(2,1)} %reshape.352), calls=%async_computation.2 | async-start | bytes 622592 | tf_op jit(solution)/shard_map/all_to_all | solution.py:89
  86.7 14.6 %all-to-all-done.2 = bf16[32,2,2358]{2,1,0:T(2,128)(2,1)S(1)} async-done(((bf16[32,2,2358]{2,1,0:T(2,128)(2,1)}), bf16[32,2,2358]{2,1,0:T(2,128)(2,1)S(1)}, u32[]{:S(2)}, u32[]{:S(2)}) %all-to-all-start.2) | async-done | bytes 301856 | tf_op jit(solution)/shard_map/all_to_all | solution.py:89
  101.3 5.6 %all-to-all-start.1 = ((f32[8,2,2]{1,2,0:T(2,128)}), f32[8,2,2]{1,2,0:T(2,128)S(1)}, u32[]{:S(2)}, u32[]{:S(2)}) async-start(f32[8,2,2]{1,2,0:T(2,128)} %copy.125), calls=%async_computation.1 | async-start | bytes 16384 | tf_op jit(solution)/shard_map/all_to_all | solution.py:284
  108.8 1.0 all-gather.6.cloned.1.call-done
  109.8 2.0 %all-to-all-done.1 = f32[8,2,2]{1,2,0:T(2,128)S(1)} async-done(((f32[8,2,2]{1,2,0:T(2,128)}), f32[8,2,2]{1,2,0:T(2,128)S(1)}, u32[]{:S(2)}, u32[]{:S(2)}) %all-to-all-start.1) | async-done | bytes 160 | tf_op jit(solution)/shard_map/all_to_all | solution.py:284
  111.7 1.0 broadcast_in_dim.48
  112.7 6.2 %all-to-all-start.3 = ((f32[32,1,3692]{2,1,0:T(1,128)}), f32[32,1,3692]{2,1,0:T(1,128)S(1)}, u32[]{:S(2)}, u32[]{:S(2)}) async-start(f32[32,1,3692]{2,1,0:T(1,128)} %broadcast_in_dim.48), calls=%async_computation.3 | async-start | bytes 950272 | tf_op jit(solution)/shard_map/all_to_all | solution.py:78
  122.0 13.9 %all-to-all-done.3 = f32[32,1,3692]{2,1,0:T(1,128)S(1)} async-done(((f32[32,1,3692]{2,1,0:T(1,128)}), f32[32,1,3692]{2,1,0:T(1,128)S(1)}, u32[]{:S(2)}, u32[]{:S(2)}) %all-to-all-start.3) | async-done | bytes 472608 | tf_op jit(solution)/shard_map/all_to_all | solution.py:78
  139.8 0.9 copy.135
  140.7 2.1 %broadcast_in_dim_reshape_reshape.3 = f32[1,27,64,64]{3,2,1,0:T(8,128)} reshape(f32[32,3456]{1,0:T(8,128)} %slice.239) | data formatting | bytes 884736 | tf_op jit(solution)/shard_map/broadcast_in_dim;reshape;reshape | solution.py:313
  143.7 10.1 %all-gather.8.cloned.1.call-done = bf16[16,2,16,2048]{3,2,1,0:T(8,128)(2,1)} async-done(((bf16[8,2,16,2048]{3,2,1,0:T(8,128)(2,1)}), bf16[16,2,16,2048]{3,2,1,0:T(8,128)(2,1)}) %all-gather.8.cloned.1.call-update) | async-done | bytes 2097168 | tf_op jit(solution)/shard_map/all_gather | solution.py:65
  153.8 1.8 %copy.132 = bf16[8,2,2,16,2048]{4,3,2,1,0:T(8,128)(2,1)S(1)} copy(bf16[8,2,2,16,2048]{4,3,2,0,1:T(8,128)(2,1)} %bitcast.139) | data formatting | bytes 4194304 | tf_op jit(solution)/shard_map/transpose | solution.py:68
  156.2 1.9 %fusion.18 = f32[1,64,2048]{2,1,0:T(8,128)} fusion(f32[64,2048]{1,0:T(8,128)S(1)} %get-tuple-element.118, f32[64]{0:T(128)S(1)} %add_sqrt_fusion, bf16[1,2048,2048]{2,1,0:T(8,128)(2,1)} %param.23, s32[]{:T(128)S(6)} %select_n.37), kind=kLoop, calls=%fused_computation.35 | loop fusion | flops 524288 | bytes 1310980 | tf_op jit(solution)/shard_map/broadcast_in_dim | solution.py:301
  (150 shorter events, 27.6 us)
Async XLA Ops:
  7.9 19.8 %collective-permute-start.2 = (f32[3,1,16,128]{3,2,1,0:T(8,128)S(1)}, f32[3,1,16,128]{3,2,1,0:T(8,128)S(1)}, u32[]{:S(2)}, u32[]{:S(2)}) collective-permute-start(f32[3,1,16,128]{3,2,1,0:T(8,128)S(1)} %get-tuple-element.110), channel_id=1, source_target_pairs={{0,32},{32,64},{64,96},{96,128},{128,160},{160,192},{192,224},{224... | collective-permute-start | bytes 73736 | tf_op jit(solution)/shard_map/ppermute | solution.py:34
  9.4 18.4 %collective-permute-start.3 = (f32[3,1,16,128]{3,2,1,0:T(8,128)S(1)}, f32[3,1,16,128]{3,2,1,0:T(8,128)S(1)}, u32[]{:S(2)}, u32[]{:S(2)}) collective-permute-start(f32[3,1,16,128]{3,2,1,0:T(8,128)S(1)} %get-tuple-element.109), channel_id=1, source_target_pairs={{32,0},{64,32},{96,64},{128,96},{160,128},{192,160},{224,192},{0,2... | collective-permute-start | bytes 73736 | tf_op jit(solution)/shard_map/ppermute | solution.py:35
  11.2 19.6 %collective-permute-start = (f32[3,8,1,128]{3,1,0,2:T(8,128)S(1)}, f32[3,8,1,128]{3,1,0,2:T(8,128)S(1)}, u32[]{:S(2)}, u32[]{:S(2)}) collective-permute-start(f32[3,8,1,128]{3,1,0,2:T(8,128)S(1)} %bitcast.161), channel_id=1, source_target_pairs={{0,1},{1,2},{2,3},{3,4},{4,5},{5,6},{6,7},{7,8},{8,9},{9,10},{10,1... | collective-permute-start | bytes 36872 | tf_op jit(solution)/shard_map/ppermute | solution.py:34
  11.3 19.5 %collective-permute-start.1 = (f32[3,8,1,128]{3,1,0,2:T(8,128)S(1)}, f32[3,8,1,128]{3,1,0,2:T(8,128)S(1)}, u32[]{:S(2)}, u32[]{:S(2)}) collective-permute-start(f32[3,8,1,128]{3,1,0,2:T(8,128)S(1)} %bitcast.160), channel_id=1, source_target_pairs={{1,0},{2,1},{3,2},{4,3},{5,4},{6,5},{7,6},{8,7},{9,8},{10,9},{11,1... | collective-permute-start | bytes 36872 | tf_op jit(solution)/shard_map/ppermute | solution.py:35
  24.4 6.2 %copy-start.18 = (s32[8]{0:T(128)}, s32[8]{0:T(128)S(1)}, u32[]{:S(2)}) copy-start(s32[8]{0:T(128)S(1)} %multiply_add_fusion) | copy-start | bytes 100
  27.7 0.7 copy-start.1
  28.5 9.2 %copy-start = (f32[3,8,16,128]{3,2,1,0:T(8,128)S(1)}, f32[3,8,16,128]{3,2,1,0:T(8,128)}, u32[]{:S(2)}) copy-start(f32[3,8,16,128]{3,2,1,0:T(8,128)} %param.18) | copy-start | bytes 589828
  28.5 9.2 %copy-start.16 = (f32[32,16,1,1]{0,1,3,2:T(8,128)S(1)}, f32[32,16,1,1]{0,1,3,2:T(8,128)}, u32[]{:S(2)}) copy-start(f32[32,16,1,1]{0,1,3,2:T(8,128)} %constant.249) | copy-start | bytes 6148
  28.5 9.7 %copy-start.12 = (bf16[1,54,64]{2,1,0:T(8,128)(2,1)S(1)}, bf16[1,54,64]{2,1,0:T(8,128)(2,1)}, u32[]{:S(2)}) copy-start(bf16[1,54,64]{2,1,0:T(8,128)(2,1)} %param.21) | copy-start | bytes 20740
  29.6 8.6 %copy-start.15 = (bf16[1,2048,2]{1,2,0:T(2,128)(2,1)S(1)}, bf16[1,2048,2]{1,2,0:T(2,128)(2,1)}, u32[]{:S(2)}) copy-start(bf16[1,2048,2]{1,2,0:T(2,128)(2,1)} %param.24) | copy-start | bytes 24580
  29.9 13.8 %copy-start.17 = (bf16[1,27,64,64]{3,2,1,0:T(8,128)(2,1)S(1)}, bf16[1,27,64,64]{3,2,1,0:T(8,128)(2,1)}, u32[]{:S(2)}) copy-start(bf16[1,27,64,64]{3,2,1,0:T(8,128)(2,1)} %param.22) | copy-start | bytes 663556
  30.9 16.3 %copy-start.13 = (f32[3,8,1,128]{3,1,0,2:T(8,128)}, f32[3,8,1,128]{3,1,0,2:T(8,128)S(1)}, u32[]{:S(2)}) copy-start(f32[3,8,1,128]{3,1,0,2:T(8,128)S(1)} %collective-permute-done.1) | copy-start | bytes 36868
  31.8 10.7 %all-to-all-start = ((bf16[8,2,259]{2,1,0:T(2,128)(2,1)}), bf16[8,2,259]{2,1,0:T(2,128)(2,1)S(1)}, u32[]{:S(2)}, u32[]{:S(2)}) async-start(bf16[8,2,259]{2,1,0:T(2,128)(2,1)} %pad_maximum_fusion.4), calls=%async_computation | async-start | bytes 24576 | tf_op jit(solution)/shard_map/all_to_all | solution.py:51
  37.7 72.1 %all-gather.6.cloned.1.call-start = ((), (), s32[]{:S(2)}) async-start(), calls=%async_computation.4 | async-start | bytes 1179648 | tf_op jit(solution)/shard_map/all_gather | solution.py:65
  42.5 4.7 %copy-start.11 = (bf16[16,259]{1,0:T(8,128)(2,1)}, bf16[16,259]{1,0:T(8,128)(2,1)S(1)}, u32[]{:S(2)}) copy-start(bf16[16,259]{1,0:T(8,128)(2,1)S(1)} %all_to_all.29) | copy-start | bytes 24868
  43.7 3.5 %copy-start.3 = (f32[16,4,4,8,64]{4,0,3,2,1:T(8,128)}, f32[16,4,4,8,64]{4,0,3,2,1:T(8,128)S(1)}, u32[]{:S(2)}) copy-start(f32[16,4,4,8,64]{4,0,3,2,1:T(8,128)S(1)} %convolution_multiply_fusion.4) | copy-start | bytes 1572868
  48.8 4.8 %slice-start = ((bf16[16,259]{1,0:T(8,128)(2,1)}), bf16[16,2]{1,0:T(8,128)(2,1)S(1)}, s32[]{:S(2)}) async-start(bf16[16,259]{1,0:T(8,128)(2,1)} %copy-done.11), calls=%async_computation.6 | async-start | bytes 8192 | tf_op jit(solution)/shard_map/split | solution.py:52
  74.6 10.9 %copy-start.10 = (f32[256,128,1,1]{1,0,3,2:T(8,128)S(1)}, f32[256,128,1,1]{1,0,3,2:T(8,128)}, u32[]{:S(2)}) copy-start(f32[256,128,1,1]{1,0,3,2:T(8,128)} %constant.251) | copy-start | bytes 393220
  74.6 11.3 %copy-start.14 = (f32[3,8,1,128]{3,1,0,2:T(8,128)S(1)}, f32[3,8,1,128]{3,1,0,2:T(8,128)}, u32[]{:S(2)}) copy-start(f32[3,8,1,128]{3,1,0,2:T(8,128)} %copy-done.13) | copy-start | bytes 36868
  77.5 23.8 %all-to-all-start.2 = ((bf16[32,2,2358]{2,1,0:T(2,128)(2,1)}), bf16[32,2,2358]{2,1,0:T(2,128)(2,1)S(1)}, u32[]{:S(2)}, u32[]{:S(2)}) async-start(bf16[32,2,2358]{2,1,0:T(2,128)(2,1)} %reshape.352), calls=%async_computation.2 | async-start | bytes 622592 | tf_op jit(solution)/shard_map/all_to_all | solution.py:89
  101.3 10.4 %all-to-all-start.1 = ((f32[8,2,2]{1,2,0:T(2,128)}), f32[8,2,2]{1,2,0:T(2,128)S(1)}, u32[]{:S(2)}, u32[]{:S(2)}) async-start(f32[8,2,2]{1,2,0:T(2,128)} %copy.125), calls=%async_computation.1 | async-start | bytes 16384 | tf_op jit(solution)/shard_map/all_to_all | solution.py:284
  106.9 46.8 %all-gather.8.cloned.1.call-start = ((), (), s32[]{:S(2)}) async-start(), calls=%async_computation.5 | async-start | bytes 3145728 | tf_op jit(solution)/shard_map/all_gather | solution.py:65
  107.4 12.0 %copy-start.2 = (f32[16,3,16,128]{3,2,0,1:T(8,128)S(1)}, f32[16,3,16,128]{3,2,0,1:T(8,128)}, u32[]{:S(2)}) copy-start(f32[16,3,16,128]{3,2,0,1:T(8,128)} %copy-done.1) | copy-start | bytes 1179652
  107.5 11.5 %copy-start.4 = (f32[3,8,16,128]{3,2,1,0:T(8,128)S(1)}, f32[3,8,16,128]{3,2,1,0:T(8,128)}, u32[]{:S(2)}) copy-start(f32[3,8,16,128]{3,2,1,0:T(8,128)} %slice.222) | copy-start | bytes 589828
  107.5 11.9 %copy-start.6 = (f32[8,16,128]{2,1,0:T(8,128)S(1)}, f32[8,16,128]{2,1,0:T(8,128)}, u32[]{:S(2)}) copy-start(f32[8,16,128]{2,1,0:T(8,128)} %get-tuple-element.100) | copy-start | bytes 196612
  107.5 11.9 %copy-start.7 = (f32[8,16,128]{2,1,0:T(8,128)S(1)}, f32[8,16,128]{2,1,0:T(8,128)}, u32[]{:S(2)}) copy-start(f32[8,16,128]{2,1,0:T(8,128)} %get-tuple-element.101) | copy-start | bytes 196612
  107.5 11.9 %copy-start.8 = (f32[8,16,128]{2,1,0:T(8,128)S(1)}, f32[8,16,128]{2,1,0:T(8,128)}, u32[]{:S(2)}) copy-start(f32[8,16,128]{2,1,0:T(8,128)} %get-tuple-element.102) | copy-start | bytes 196612
  109.7 10.6 %copy-start.19 = (s32[8]{0:T(128)S(1)}, s32[8]{0:T(128)}, u32[]{:S(2)}) copy-start(s32[8]{0:T(128)} %copy-done.18) | copy-start | bytes 100
  112.7 23.1 %all-to-all-start.3 = ((f32[32,1,3692]{2,1,0:T(1,128)}), f32[32,1,3692]{2,1,0:T(1,128)S(1)}, u32[]{:S(2)}, u32[]{:S(2)}) async-start(f32[32,1,3692]{2,1,0:T(1,128)} %broadcast_in_dim.48), calls=%async_computation.3 | async-start | bytes 950272 | tf_op jit(solution)/shard_map/all_to_all | solution.py:78
  139.7 3.1 %copy-start.9 = (f32[118,64]{1,0:T(8,128)S(1)}, f32[118,64]{1,0:T(8,128)}, u32[]{:S(2)}) copy-start(f32[118,64]{1,0:T(8,128)} %slice.212) | copy-start | bytes 90628
  153.8 1.8 %copy-start.5 = (bf16[512,64]{1,0:T(8,128)(2,1)S(1)}, bf16[512,64]{1,0:T(8,128)(2,1)}, u32[]{:S(2)}) copy-start(bf16[512,64]{1,0:T(8,128)(2,1)} %reshape.325) | copy-start | bytes 196612
Sparse Core Ops, SparseCore 0:
  70.8 38.8 all-gather.5
  111.5 42.1 all-gather.7

commit v13 on v9

--- a/solution.py
+++ b/solution.py
@@ -282,6 +282,7 @@
         recv_rows, recv_aims, recv_valid, k_first[0], k_second[0], w_hidden[0], w_out[0]
     )
     back = lax.all_to_all(pred, "wall", split_axis=0, concat_axis=0, tiled=True)
+    back, grad_one, grad_two, grad_out = lax.optimization_barrier((back, grad_one, grad_two, grad_out))
     stress_local = jnp.dot(select.T, back, precision=highest)
     stress = stress_local.T[:, None, :]
     share_rows = FEATS // flow_count

time: 160 us -> 160 us (level); the launches traced: 159 us -> 158 us
  starting transfers between devices: 34.4 us -> 31.9 us
  waiting for transfers between devices: 34.8 us -> 37.3 us
    all_to_all x1, waiting for transfers between devices: 1.97 us -> 4.65 us  [body(): back = lax.all_to_all(pred, 'wall', split_axis=0, concat_axis=0, tiled=True)]
    all_to_all x1, starting transfers between devices: 6.15 us -> 4.47 us  [from_everyone(): return lax.all_to_all(copies, axis, split_axis=0, concat_axis=0, tiled=True)]
  transfers between devices with their start and end apart: 10 -> 10, of which waited for: 5 -> 4; matrix products, arithmetic and copies ran while one was open for 22% -> 21% of each run, Pallas kernels for 0% -> 0%
where the time goes in v13:
time: 160 us; the launch traced here: 158 us
  waiting for transfers between devices  37.3 us (23%)
  starting transfers between devices  31.9 us (20%)
  matrix products  27.9 us (17%)
  local copies, waits for them, and re-layouts  26.3 us (16%)
  between operations  15.4 us (10%)
  other arithmetic  12.3 us (8%)
  blocking collectives  6.55 us (4%)
    all_to_all x1, waiting for transfers between devices, owner_sums(): lax.all_to_all(both, axis, split_axis=0, concat_axis=0, tiled=True)  15.3 us
    all_to_all x1, waiting for transfers between devices, from_everyone(): return lax.all_to_all(copies, axis, split_axis=0, concat_axis=0, tiled=True)  13.5 us
    transpose x2, matrix products, conv_filter(): return jnp.moveaxis(taps, 0, 3)  8.4 us
    ppermute x2, starting transfers between devices, extended(): lax.ppermute(first, axis, [(b, a) for a, b in up])  7.98 us
    all_to_all x1, starting transfers between devices, owner_sums(): lax.all_to_all(both, axis, split_axis=0, concat_axis=0, tiled=True)  7.28 us
    all_gather x1, blocking collectives, gather_in_order(): tiles = lax.all_gather(tiles, axes[k])  6.55 us
    all_to_all x1, starting transfers between devices, in_one_piece(): lax.all_to_all(both, axis, split_axis=split_dim, concat_axis=concat_dim,...  5.88 us
    dot_general x1, matrix products, forward_back(): jnp.dot(delta_three, w_hidden.T, preferred_element_type=jnp.float32)  5.65 us
  transfers between devices with their start and end apart: 10, of which 4 were waited for; matrix products, arithmetic and copies ran while one was open for 21% of the time, Pallas kernels for 0%

profile of v13, /device:TPU:2, one launch (start us, length us, event | category | flops | bytes accessed | tf_op | source)
XLA Modules:
  0.0 157.6 jit_solution(15307553996791907829)
XLA Ops:
  7.9 1.5 collective-permute-start.2
  9.4 0.8 collective-permute-start.3
  10.3 1.0 fusion.45
  11.3 7.1 %collective-permute-start.1 = (f32[3,8,1,128]{3,1,0,2:T(8,128)S(1)}, f32[3,8,1,128]{3,1,0,2:T(8,128)S(1)}, u32[]{:S(2)}, u32[]{:S(2)}) collective-permute-start(f32[3,8,1,128]{3,1,0,2:T(8,128)S(1)} %bitcast.160), channel_id=1, source_target_pairs={{1,0},{2,1},{3,2},{4,3},{5,4},{6,5},{7,6},{8,7},{9,8},{10,9},{11,1... | collective-permute-start | bytes 36872 | tf_op jit(solution)/shard_map/ppermute | solution.py:35
  19.8 0.9 fusion.44
  20.7 1.5 fusion.22
  24.4 1.2 reshape.323
  28.5 1.1 reshape.326
  31.8 5.9 %all-to-all-start = ((bf16[8,2,259]{2,1,0:T(2,128)(2,1)}), bf16[8,2,259]{2,1,0:T(2,128)(2,1)S(1)}, u32[]{:S(2)}, u32[]{:S(2)}) async-start(bf16[8,2,259]{2,1,0:T(2,128)(2,1)} %pad_maximum_fusion.4), calls=%async_computation | async-start | bytes 24576 | tf_op jit(solution)/shard_map/all_to_all | solution.py:51
  39.2 3.2 %all-to-all-done = bf16[8,2,259]{2,1,0:T(2,128)(2,1)S(1)} async-done(((bf16[8,2,259]{2,1,0:T(2,128)(2,1)}), bf16[8,2,259]{2,1,0:T(2,128)(2,1)S(1)}, u32[]{:S(2)}, u32[]{:S(2)}) %all-to-all-start) | async-done | bytes 8320 | tf_op jit(solution)/shard_map/all_to_all | solution.py:51
  42.8 0.9 convolution_multiply_fusion.4
  43.7 3.5 %fusion.14 = (f32[16,4,4,8,64]{4,0,3,2,1:T(8,128)}, f32[16,4,4,8,64]{4,0,3,2,1:T(8,128)}) fusion(bf16[3,3,3,64,64]{4,3,2,1,0:T(8,128)(2,1)S(1)} %bitcast.165, f32[16,4,4,8,64]{4,0,3,2,1:T(8,128)S(1)} %convolution_multiply_fusion.4), kind=kOutput, calls=%fused_computation.28 | convolution fusion | flops 289669120 | bytes 1794048 | tf_op jit(solution)/shard_map/conv_general_dilated | solution.py:157
  47.2 1.3 reduce_sum.84
  48.8 4.6 %multiply_convert_fusion.3 = (bf16[16,2048]{1,0:T(8,128)(2,1)S(1)}, f32[16,2048]{1,0:T(8,128)S(1)}) fusion(bf16[16,2048]{1,0:T(8,128)(2,1)S(1)} %convert_element_type.114, bf16[1,2048,2048]{2,1,0:T(8,128)(2,1)} %param.23), kind=kOutput, calls=%fused_computation.52 | convolution fusion | flops 134414336 | bytes 8650752 | tf_op jit(solution)/shard_map/dot_general | solution.py:186
  53.9 5.6 %fusion.8 = f32[16,2048]{1,0:T(8,128)S(1)} fusion(bf16[16,2048]{1,0:T(8,128)(2,1)S(1)} %fusion.11, bf16[1,2048,2048]{2,1,0:T(8,128)(2,1)} %param.23), kind=kOutput, calls=%fused_computation.9 | convolution fusion | flops 134250496 | bytes 8585216 | tf_op jit(solution)/shard_map/dot_general | solution.py:194
  60.0 0.9 copy-done.5
  61.3 2.7 %convolution_multiply_fusion.5 = bf16[3,3,3,64,64]{4,3,2,1,0:T(8,128)(2,1)S(1)} fusion(bf16[16,4,4,8,64]{4,0,3,2,1:T(8,128)(2,1)S(1)} %multiply_convert_fusion, f32[16,4,4,8,64]{4,0,3,2,1:T(8,128)S(1)} %copy-done.4), kind=kOutput, calls=%fused_computation.16 | convolution fusion | flops 289234944 | bytes 1007616 | tf_op jit(solution)/shard_map/transpose | solution.py:168
  64.0 5.7 %convolution_multiply_fusion.6 = bf16[3,3,3,2,64]{4,3,2,1,0:T(2,128)(2,1)S(1)} fusion(bf16[16,2,4,4,8]{0,4,3,2,1:T(8,128)(2,1)S(1)} %bitcast.153, bf16[16,4,4,8,64]{4,0,3,2,1:T(8,128)(2,1)S(1)} %multiply_convert_fusion, bf16[3,3,3,64,64]{4,3,2,1,0:T(8,128)(2,1)S(1)} %bitcast.166, f32[16,4,4,8,64]{4,0,3,2,1:T(8,128)} %copy-done.3), kind=kOutput, calls=%fused_computation.20 | convolution fusion | flops 298687232 | bytes 1022720 | tf_op jit(solution)/shard_map/transpose | solution.py:168
  69.7 6.6 %all-gather = bf16[32,2048]{1,0:T(8,128)(2,1)} all-gather(bf16[16,2048]{1,0:T(8,128)(2,1)S(1)} %fusion.11), channel_id=2, replica_groups=mesh['wall'=8,'stream_0'=8,'stream_1'=2,'stream_2'=2] {'stream_1'}, dimensions={0}, use_global_device_ids=true | all-gather | bytes 196608 | tf_op jit(solution)/shard_map/all_gather | solution.py:65
  77.2 4.7 %all-to-all-start.1 = ((f32[8,2,2]{1,2,0:T(2,128)}), f32[8,2,2]{1,2,0:T(2,128)S(1)}, u32[]{:S(2)}, u32[]{:S(2)}) async-start(f32[8,2,2]{1,2,0:T(2,128)} %copy.125), calls=%async_computation.1 | async-start | bytes 16384 | tf_op jit(solution)/shard_map/all_to_all | solution.py:284
  82.0 4.6 %all-to-all-done.1 = f32[8,2,2]{1,2,0:T(2,128)S(1)} async-done(((f32[8,2,2]{1,2,0:T(2,128)}), f32[8,2,2]{1,2,0:T(2,128)S(1)}, u32[]{:S(2)}, u32[]{:S(2)}) %all-to-all-start.1) | async-done | bytes 160 | tf_op jit(solution)/shard_map/all_to_all | solution.py:284
  89.6 1.1 reshape.365
  90.7 7.3 %all-to-all-start.2 = ((bf16[32,2,2358]{2,1,0:T(2,128)(2,1)}), bf16[32,2,2358]{2,1,0:T(2,128)(2,1)S(1)}, u32[]{:S(2)}, u32[]{:S(2)}) async-start(bf16[32,2,2358]{2,1,0:T(2,128)(2,1)} %reshape.365), calls=%async_computation.2 | async-start | bytes 622592 | tf_op jit(solution)/shard_map/all_to_all | solution.py:89
  99.2 15.3 %all-to-all-done.2 = bf16[32,2,2358]{2,1,0:T(2,128)(2,1)S(1)} async-done(((bf16[32,2,2358]{2,1,0:T(2,128)(2,1)}), bf16[32,2,2358]{2,1,0:T(2,128)(2,1)S(1)}, u32[]{:S(2)}, u32[]{:S(2)}) %all-to-all-start.2) | async-done | bytes 301856 | tf_op jit(solution)/shard_map/all_to_all | solution.py:89
  116.2 1.0 broadcast_in_dim.48
  117.3 4.5 %all-to-all-start.3 = ((f32[32,1,3692]{2,1,0:T(1,128)}), f32[32,1,3692]{2,1,0:T(1,128)S(1)}, u32[]{:S(2)}, u32[]{:S(2)}) async-start(f32[32,1,3692]{2,1,0:T(1,128)} %broadcast_in_dim.48), calls=%async_computation.3 | async-start | bytes 950272 | tf_op jit(solution)/shard_map/all_to_all | solution.py:78
  125.2 13.5 %all-to-all-done.3 = f32[32,1,3692]{2,1,0:T(1,128)S(1)} async-done(((f32[32,1,3692]{2,1,0:T(1,128)}), f32[32,1,3692]{2,1,0:T(1,128)S(1)}, u32[]{:S(2)}, u32[]{:S(2)}) %all-to-all-start.3) | async-done | bytes 472608 | tf_op jit(solution)/shard_map/all_to_all | solution.py:78
  140.9 0.9 multiply_reduce_fusion
  142.6 0.9 copy.135
  143.5 2.1 %broadcast_in_dim_reshape_reshape.3 = f32[1,27,64,64]{3,2,1,0:T(8,128)} reshape(f32[32,3456]{1,0:T(8,128)} %slice.239) | data formatting | bytes 884736 | tf_op jit(solution)/shard_map/broadcast_in_dim;reshape;reshape | solution.py:314
  146.5 1.8 %copy.132 = bf16[8,2,2,16,2048]{4,3,2,1,0:T(8,128)(2,1)S(1)} copy(bf16[8,2,2,16,2048]{4,3,1,0,2:T(8,128)(2,1)} %bitcast.138) | data formatting | bytes 4194304 | tf_op jit(solution)/shard_map/transpose | solution.py:68
  148.9 1.9 %fusion.15 = f32[1,64,2048]{2,1,0:T(8,128)} fusion(f32[64,2048]{1,0:T(8,128)S(1)} %get-tuple-element.126, f32[64]{0:T(128)S(1)} %add_sqrt_fusion, bf16[1,2048,2048]{2,1,0:T(8,128)(2,1)} %param.23, s32[]{:T(128)S(6)} %select_n.37), kind=kLoop, calls=%fused_computation.32 | loop fusion | flops 524288 | bytes 1310980 | tf_op jit(solution)/shard_map/broadcast_in_dim | solution.py:302
  (151 shorter events, 26.7 us)
Async XLA Ops:
  7.9 19.8 %collective-permute-start.2 = (f32[3,1,16,128]{3,2,1,0:T(8,128)S(1)}, f32[3,1,16,128]{3,2,1,0:T(8,128)S(1)}, u32[]{:S(2)}, u32[]{:S(2)}) collective-permute-start(f32[3,1,16,128]{3,2,1,0:T(8,128)S(1)} %get-tuple-element.118), channel_id=1, source_target_pairs={{0,32},{32,64},{64,96},{96,128},{128,160},{160,192},{192,224},{224... | collective-permute-start | bytes 73736 | tf_op jit(solution)/shard_map/ppermute | solution.py:34
  9.4 18.4 %collective-permute-start.3 = (f32[3,1,16,128]{3,2,1,0:T(8,128)S(1)}, f32[3,1,16,128]{3,2,1,0:T(8,128)S(1)}, u32[]{:S(2)}, u32[]{:S(2)}) collective-permute-start(f32[3,1,16,128]{3,2,1,0:T(8,128)S(1)} %get-tuple-element.117), channel_id=1, source_target_pairs={{32,0},{64,32},{96,64},{128,96},{160,128},{192,160},{224,192},{0,2... | collective-permute-start | bytes 73736 | tf_op jit(solution)/shard_map/ppermute | solution.py:35
  11.2 19.6 %collective-permute-start = (f32[3,8,1,128]{3,1,0,2:T(8,128)S(1)}, f32[3,8,1,128]{3,1,0,2:T(8,128)S(1)}, u32[]{:S(2)}, u32[]{:S(2)}) collective-permute-start(f32[3,8,1,128]{3,1,0,2:T(8,128)S(1)} %bitcast.161), channel_id=1, source_target_pairs={{0,1},{1,2},{2,3},{3,4},{4,5},{5,6},{6,7},{7,8},{8,9},{9,10},{10,1... | collective-permute-start | bytes 36872 | tf_op jit(solution)/shard_map/ppermute | solution.py:34
  11.3 19.5 %collective-permute-start.1 = (f32[3,8,1,128]{3,1,0,2:T(8,128)S(1)}, f32[3,8,1,128]{3,1,0,2:T(8,128)S(1)}, u32[]{:S(2)}, u32[]{:S(2)}) collective-permute-start(f32[3,8,1,128]{3,1,0,2:T(8,128)S(1)} %bitcast.160), channel_id=1, source_target_pairs={{1,0},{2,1},{3,2},{4,3},{5,4},{6,5},{7,6},{8,7},{9,8},{10,9},{11,1... | collective-permute-start | bytes 36872 | tf_op jit(solution)/shard_map/ppermute | solution.py:35
  27.7 0.7 copy-start.1
  28.5 9.2 %copy-start = (f32[3,8,16,128]{3,2,1,0:T(8,128)S(1)}, f32[3,8,16,128]{3,2,1,0:T(8,128)}, u32[]{:S(2)}) copy-start(f32[3,8,16,128]{3,2,1,0:T(8,128)} %param.18) | copy-start | bytes 589828
  28.5 9.2 %copy-start.18 = (f32[32,16,1,1]{0,1,3,2:T(8,128)S(1)}, f32[32,16,1,1]{0,1,3,2:T(8,128)}, u32[]{:S(2)}) copy-start(f32[32,16,1,1]{0,1,3,2:T(8,128)} %constant.249) | copy-start | bytes 6148
  28.5 9.7 %copy-start.14 = (bf16[1,54,64]{2,1,0:T(8,128)(2,1)S(1)}, bf16[1,54,64]{2,1,0:T(8,128)(2,1)}, u32[]{:S(2)}) copy-start(bf16[1,54,64]{2,1,0:T(8,128)(2,1)} %param.21) | copy-start | bytes 20740
  29.6 8.6 %copy-start.17 = (bf16[1,2048,2]{1,2,0:T(2,128)(2,1)S(1)}, bf16[1,2048,2]{1,2,0:T(2,128)(2,1)}, u32[]{:S(2)}) copy-start(bf16[1,2048,2]{1,2,0:T(2,128)(2,1)} %param.24) | copy-start | bytes 24580
  29.9 13.8 %copy-start.19 = (bf16[1,27,64,64]{3,2,1,0:T(8,128)(2,1)S(1)}, bf16[1,27,64,64]{3,2,1,0:T(8,128)(2,1)}, u32[]{:S(2)}) copy-start(bf16[1,27,64,64]{3,2,1,0:T(8,128)(2,1)} %param.22) | copy-start | bytes 663556
  30.9 16.3 %copy-start.15 = (f32[3,8,1,128]{3,1,0,2:T(8,128)}, f32[3,8,1,128]{3,1,0,2:T(8,128)S(1)}, u32[]{:S(2)}) copy-start(f32[3,8,1,128]{3,1,0,2:T(8,128)S(1)} %collective-permute-done.1) | copy-start | bytes 36868
  31.8 10.7 %all-to-all-start = ((bf16[8,2,259]{2,1,0:T(2,128)(2,1)}), bf16[8,2,259]{2,1,0:T(2,128)(2,1)S(1)}, u32[]{:S(2)}, u32[]{:S(2)}) async-start(bf16[8,2,259]{2,1,0:T(2,128)(2,1)} %pad_maximum_fusion.4), calls=%async_computation | async-start | bytes 24576 | tf_op jit(solution)/shard_map/all_to_all | solution.py:51
  37.6 84.2 %all-gather.6.cloned.1.call-start = ((), (), s32[]{:S(2)}) async-start(), calls=%async_computation.4 | async-start | bytes 1179648 | tf_op jit(solution)/shard_map/all_gather | solution.py:65
  42.5 4.7 %copy-start.13 = (bf16[16,259]{1,0:T(8,128)(2,1)}, bf16[16,259]{1,0:T(8,128)(2,1)S(1)}, u32[]{:S(2)}) copy-start(bf16[16,259]{1,0:T(8,128)(2,1)S(1)} %all_to_all.29) | copy-start | bytes 24868
  43.7 3.5 %copy-start.3 = (f32[16,4,4,8,64]{4,0,3,2,1:T(8,128)}, f32[16,4,4,8,64]{4,0,3,2,1:T(8,128)S(1)}, u32[]{:S(2)}) copy-start(f32[16,4,4,8,64]{4,0,3,2,1:T(8,128)S(1)} %convolution_multiply_fusion.4) | copy-start | bytes 1572868
  48.8 4.8 %slice-start = ((bf16[16,259]{1,0:T(8,128)(2,1)}), bf16[16,2]{1,0:T(8,128)(2,1)S(1)}, s32[]{:S(2)}) async-start(bf16[16,259]{1,0:T(8,128)(2,1)} %copy-done.13), calls=%async_computation.6 | async-start | bytes 8192 | tf_op jit(solution)/shard_map/split | solution.py:52
  59.7 1.2 copy-start.5
  59.8 1.5 copy-start.4
  77.2 9.4 %all-to-all-start.1 = ((f32[8,2,2]{1,2,0:T(2,128)}), f32[8,2,2]{1,2,0:T(2,128)S(1)}, u32[]{:S(2)}, u32[]{:S(2)}) async-start(f32[8,2,2]{1,2,0:T(2,128)} %copy.125), calls=%async_computation.1 | async-start | bytes 16384 | tf_op jit(solution)/shard_map/all_to_all | solution.py:284
  87.7 11.0 %copy-start.12 = (f32[256,128,1,1]{1,0,3,2:T(8,128)S(1)}, f32[256,128,1,1]{1,0,3,2:T(8,128)}, u32[]{:S(2)}) copy-start(f32[256,128,1,1]{1,0,3,2:T(8,128)} %constant.251) | copy-start | bytes 393220
  87.9 11.2 %copy-start.16 = (f32[3,8,1,128]{3,1,0,2:T(8,128)S(1)}, f32[3,8,1,128]{3,1,0,2:T(8,128)}, u32[]{:S(2)}) copy-start(f32[3,8,1,128]{3,1,0,2:T(8,128)} %copy-done.15) | copy-start | bytes 36868
  90.7 23.7 %all-to-all-start.2 = ((bf16[32,2,2358]{2,1,0:T(2,128)(2,1)}), bf16[32,2,2358]{2,1,0:T(2,128)(2,1)S(1)}, u32[]{:S(2)}, u32[]{:S(2)}) async-start(bf16[32,2,2358]{2,1,0:T(2,128)(2,1)} %reshape.365), calls=%async_computation.2 | async-start | bytes 622592 | tf_op jit(solution)/shard_map/all_to_all | solution.py:89
  114.9 7.8 %copy-start.2 = (f32[16,3,16,128]{3,2,0,1:T(8,128)S(1)}, f32[16,3,16,128]{3,2,0,1:T(8,128)}, u32[]{:S(2)}) copy-start(f32[16,3,16,128]{3,2,0,1:T(8,128)} %copy-done.1) | copy-start | bytes 1179652
  114.9 7.6 %copy-start.6 = (f32[3,8,16,128]{3,2,1,0:T(8,128)S(1)}, f32[3,8,16,128]{3,2,1,0:T(8,128)}, u32[]{:S(2)}) copy-start(f32[3,8,16,128]{3,2,1,0:T(8,128)} %slice.222) | copy-start | bytes 589828
  115.0 7.8 %copy-start.8 = (f32[8,16,128]{2,1,0:T(8,128)S(1)}, f32[8,16,128]{2,1,0:T(8,128)}, u32[]{:S(2)}) copy-start(f32[8,16,128]{2,1,0:T(8,128)} %get-tuple-element.108) | copy-start | bytes 196612
  115.0 7.8 %copy-start.9 = (f32[8,16,128]{2,1,0:T(8,128)S(1)}, f32[8,16,128]{2,1,0:T(8,128)}, u32[]{:S(2)}) copy-start(f32[8,16,128]{2,1,0:T(8,128)} %get-tuple-element.109) | copy-start | bytes 196612
  115.0 7.8 %copy-start.10 = (f32[8,16,128]{2,1,0:T(8,128)S(1)}, f32[8,16,128]{2,1,0:T(8,128)}, u32[]{:S(2)}) copy-start(f32[8,16,128]{2,1,0:T(8,128)} %get-tuple-element.110) | copy-start | bytes 196612
  117.3 21.5 %all-to-all-start.3 = ((f32[32,1,3692]{2,1,0:T(1,128)}), f32[32,1,3692]{2,1,0:T(1,128)S(1)}, u32[]{:S(2)}, u32[]{:S(2)}) async-start(f32[32,1,3692]{2,1,0:T(1,128)} %broadcast_in_dim.48), calls=%async_computation.3 | async-start | bytes 950272 | tf_op jit(solution)/shard_map/all_to_all | solution.py:78
  121.7 24.8 %all-gather.8.cloned.1.call-start = ((), (), s32[]{:S(2)}) async-start(), calls=%async_computation.5 | async-start | bytes 3145728 | tf_op jit(solution)/shard_map/all_gather | solution.py:65
  142.6 3.1 %copy-start.11 = (f32[118,64]{1,0:T(8,128)S(1)}, f32[118,64]{1,0:T(8,128)}, u32[]{:S(2)}) copy-start(f32[118,64]{1,0:T(8,128)} %slice.212) | copy-start | bytes 90628
  146.5 1.8 %copy-start.7 = (bf16[512,64]{1,0:T(8,128)(2,1)S(1)}, bf16[512,64]{1,0:T(8,128)(2,1)}, u32[]{:S(2)}) copy-start(bf16[512,64]{1,0:T(8,128)(2,1)} %reshape.338) | copy-start | bytes 196612
Sparse Core Ops, SparseCore 0:
  76.4 38.3 all-gather.5
  124.4 16.3 all-gather.7

commit v14 on v9

--- a/solution.py
+++ b/solution.py
@@ -168,7 +168,7 @@
     return jnp.moveaxis(taps, 0, 3)
 
 
-def forward_back(patches, aim_rows, valid, k_first, k_second, w_hidden, w_out):
+def forward_back(patches, aim_rows, valid, k_first, k_second, w_hidden, w_out, early):
     batch = patches.shape[0]
     channels = k_second.shape[-1]
     inputs = patches.reshape(batch, 2, PY, PX, PZ).transpose(0, 2, 3, 4, 1)
@@ -191,6 +191,7 @@
     delta_three = (
         jnp.dot(error, w_out.astype(jnp.float32).T, precision=highest) * scale_four * silu_slope(pre_three)
     ).astype(jnp.bfloat16)
+    delta_three, sent = lax.optimization_barrier((delta_three, early(pred)))
     back_feat = jnp.dot(delta_three, w_hidden.T, preferred_element_type=jnp.float32) * scale_three
     back_grid = back_feat.reshape(batch, PY // 2, 1, PX // 2, 1, PZ, channels)
     spread_back = jnp.broadcast_to(back_grid, (batch, PY // 2, 2, PX // 2, 2, PZ, channels)).reshape(pre_two.shape) * 0.25
@@ -200,7 +201,7 @@
     back_one = conv_taps(delta_two, mirrored)
     delta_one = (back_one * scale_two * silu_slope(pre_one)).astype(jnp.bfloat16)
     grad_one = (conv_filter(inputs, delta_one) * scale_one).reshape(54, channels)
-    return (pred, grad_one, grad_two, grad_out, features, delta_three)
+    return (sent, grad_one, grad_two, grad_out, features, delta_three)
 
 
 def row_update(weight, grad):
@@ -279,9 +280,10 @@
         (send_rows, send_aims, send_valid), "wall", 0, 0, 1
     )
     pred, grad_one, grad_two, grad_out, features, delta_three = forward_back(
-        recv_rows, recv_aims, recv_valid, k_first[0], k_second[0], w_hidden[0], w_out[0]
-    )
-    back = lax.all_to_all(pred, "wall", split_axis=0, concat_axis=0, tiled=True)
+        recv_rows, recv_aims, recv_valid, k_first[0], k_second[0], w_hidden[0], w_out[0],
+        lambda pred: lax.all_to_all(pred, "wall", split_axis=0, concat_axis=0, tiled=True),
+    )
+    back = pred
     stress_local = jnp.dot(select.T, back, precision=highest)
     stress = stress_local.T[:, None, :]
     share_rows = FEATS // flow_count

time: 160 us -> 160 us (level)
  starting transfers between devices: 34.4 us -> 32.6 us
    all_to_all x1, waiting for transfers between devices: 13.9 us -> 12.1 us  [from_everyone(): return lax.all_to_all(copies, axis, split_axis=0, concat_axis=0, tiled=True)]
    all_to_all x1, waiting for transfers between devices: 1.97 us -> 3.67 us  [body(): lax.all_to_all(pred, 'wall', split_axis=0, concat_axis=0, tiled=True)]
    unnamed x48 -> x42, local copies, waits for them, and re-layouts: 4.31 us -> 4.3 us
where the time goes in v14:
time: 160 us; the launch traced here: 158 us
  waiting for transfers between devices  36.2 us (23%)
  starting transfers between devices  32.6 us (20%)
  matrix products  28.9 us (18%)
  local copies, waits for them, and re-layouts  25.3 us (16%)
  between operations  15.4 us (10%)
  other arithmetic  13.5 us (8%)
  blocking collectives  6.56 us (4%)
    all_to_all x1, waiting for transfers between devices, owner_sums(): lax.all_to_all(both, axis, split_axis=0, concat_axis=0, tiled=True)  15 us
    all_to_all x1, waiting for transfers between devices, from_everyone(): return lax.all_to_all(copies, axis, split_axis=0, concat_axis=0, tiled=True)  12.1 us
    transpose x2, matrix products, conv_filter(): return jnp.moveaxis(taps, 0, 3)  9.39 us
    ppermute x2, starting transfers between devices, extended(): lax.ppermute(first, axis, [(b, a) for a, b in up])  7.98 us
    all_to_all x1, starting transfers between devices, owner_sums(): lax.all_to_all(both, axis, split_axis=0, concat_axis=0, tiled=True)  7.5 us
    all_gather x1, blocking collectives, gather_in_order(): tiles = lax.all_gather(tiles, axes[k])  6.56 us
    all_to_all x1, starting transfers between devices, in_one_piece(): lax.all_to_all(both, axis, split_axis=split_dim, concat_axis=concat_dim,...  5.88 us
    dot_general x1, matrix products, forward_back(): jnp.dot(delta_three, w_hidden.T, preferred_element_type=jnp.float32)  5.65 us
  transfers between devices with their start and end apart: 10, of which 5 were waited for; matrix products, arithmetic and copies ran while one was open for 22% of the time, Pallas kernels for 0%

profile of v14, /device:TPU:2, one launch (start us, length us, event | category | flops | bytes accessed | tf_op | source)
XLA Modules:
  0.0 158.4 jit_solution(18326703507718707320)
XLA Ops:
  7.9 1.5 collective-permute-start.2
  10.3 1.0 fusion.48
  11.3 7.1 %collective-permute-start.1 = (f32[3,8,1,128]{3,1,0,2:T(8,128)S(1)}, f32[3,8,1,128]{3,1,0,2:T(8,128)S(1)}, u32[]{:S(2)}, u32[]{:S(2)}) collective-permute-start(f32[3,8,1,128]{3,1,0,2:T(8,128)S(1)} %bitcast.160), channel_id=1, source_target_pairs={{1,0},{2,1},{3,2},{4,3},{5,4},{6,5},{7,6},{8,7},{9,8},{10,9},{11,1... | collective-permute-start | bytes 36872 | tf_op jit(solution)/shard_map/ppermute | solution.py:35
  19.8 0.9 fusion.47
  20.7 1.5 fusion.25
  24.4 1.2 reshape.313
  28.5 1.1 reshape.316
  31.8 5.9 %all-to-all-start = ((bf16[8,2,259]{2,1,0:T(2,128)(2,1)}), bf16[8,2,259]{2,1,0:T(2,128)(2,1)S(1)}, u32[]{:S(2)}, u32[]{:S(2)}) async-start(bf16[8,2,259]{2,1,0:T(2,128)(2,1)} %pad_maximum_fusion.4), calls=%async_computation | async-start | bytes 24576 | tf_op jit(solution)/shard_map/all_to_all | solution.py:51
  39.2 3.2 %all-to-all-done = bf16[8,2,259]{2,1,0:T(2,128)(2,1)S(1)} async-done(((bf16[8,2,259]{2,1,0:T(2,128)(2,1)}), bf16[8,2,259]{2,1,0:T(2,128)(2,1)S(1)}, u32[]{:S(2)}, u32[]{:S(2)}) %all-to-all-start) | async-done | bytes 8320 | tf_op jit(solution)/shard_map/all_to_all | solution.py:51
  42.8 0.9 convolution_multiply_fusion.4
  43.7 3.5 %fusion.17 = (f32[16,4,4,8,64]{4,0,3,2,1:T(8,128)}, f32[16,4,4,8,64]{4,0,3,2,1:T(8,128)}) fusion(bf16[3,3,3,64,64]{4,3,2,1,0:T(8,128)(2,1)S(1)} %bitcast.165, f32[16,4,4,8,64]{4,0,3,2,1:T(8,128)S(1)} %convolution_multiply_fusion.4), kind=kOutput, calls=%fused_computation.31 | convolution fusion | flops 289669120 | bytes 1794048 | tf_op jit(solution)/shard_map/conv_general_dilated | solution.py:157
  47.2 1.3 reduce_sum.84
  48.8 4.6 %multiply_convert_fusion.3 = (bf16[16,2048]{1,0:T(8,128)(2,1)S(1)}, f32[16,2048]{1,0:T(8,128)S(1)}) fusion(bf16[16,2048]{1,0:T(8,128)(2,1)S(1)} %convert_element_type.114, bf16[1,2048,2048]{2,1,0:T(8,128)(2,1)} %param.23), kind=kOutput, calls=%fused_computation.55 | convolution fusion | flops 134414336 | bytes 8650752 | tf_op jit(solution)/shard_map/dot_general | solution.py:186
  54.8 4.8 %all-to-all-start.1 = ((f32[8,2,2]{1,2,0:T(2,128)}), f32[8,2,2]{1,2,0:T(2,128)S(1)}, u32[]{:S(2)}, u32[]{:S(2)}) async-start(f32[8,2,2]{1,2,0:T(2,128)} %copy.126), calls=%async_computation.1 | async-start | bytes 16384 | tf_op jit(solution)/shard_map/all_to_all | solution.py:284
  60.7 3.7 %all-to-all-done.1 = f32[8,2,2]{1,2,0:T(2,128)S(1)} async-done(((f32[8,2,2]{1,2,0:T(2,128)}), f32[8,2,2]{1,2,0:T(2,128)S(1)}, u32[]{:S(2)}, u32[]{:S(2)}) %all-to-all-start.1) | async-done | bytes 160 | tf_op jit(solution)/shard_map/all_to_all | solution.py:284
  64.5 5.6 %fusion.8 = f32[16,2048]{1,0:T(8,128)S(1)} fusion(bf16[16,2048]{1,0:T(8,128)(2,1)S(1)} %fusion.11, bf16[1,2048,2048]{2,1,0:T(8,128)(2,1)} %param.23), kind=kOutput, calls=%fused_computation.9 | convolution fusion | flops 134250496 | bytes 8585216 | tf_op jit(solution)/shard_map/dot_general | solution.py:195
  70.1 6.6 %all-gather = bf16[32,2048]{1,0:T(8,128)(2,1)} all-gather(bf16[16,2048]{1,0:T(8,128)(2,1)S(1)} %fusion.11), channel_id=2, replica_groups=mesh['wall'=8,'stream_0'=8,'stream_1'=2,'stream_2'=2] {'stream_1'}, dimensions={0}, use_global_device_ids=true | all-gather | bytes 196608 | tf_op jit(solution)/shard_map/all_gather | solution.py:65
  77.1 1.7 %multiply_convert_fusion = bf16[16,4,4,8,64]{4,0,3,2,1:T(8,128)(2,1)S(1)} fusion(f32[16,4,4,8,64]{4,0,3,2,1:T(8,128)S(1)} %bitcast.137, f32[16,4,4,8,64]{4,0,3,2,1:T(8,128)} %get-tuple-element.118), kind=kLoop, calls=%fused_computation.29 | loop fusion | flops 1179648 | bytes 1310720 | tf_op jit(solution)/shard_map/convert_element_type | solution.py:198
  78.8 5.4 %fusion.16 = bf16[3,3,3,2,64]{4,3,2,1,0:T(2,128)(2,1)S(1)} fusion(bf16[16,2,4,4,8]{0,4,3,2,1:T(8,128)(2,1)S(1)} %bitcast.153, bf16[16,4,4,8,64]{4,0,3,2,1:T(8,128)(2,1)S(1)} %multiply_convert_fusion, bf16[3,3,3,64,64]{4,3,2,1,0:T(8,128)(2,1)S(1)} %bitcast.166, f32[16,4,4,8,64]{4,0,3,2,1:T(8,128)} %copy-done.3), kind=kOutput, calls=%fused_computation.23 | convolution fusion | flops 298687232 | bytes 1022720 | tf_op jit(solution)/shard_map/transpose | solution.py:168
  84.5 3.9 %fusion.15 = bf16[3,3,3,64,64]{4,3,2,1,0:T(8,128)(2,1)S(1)} fusion(bf16[16,4,4,8,64]{4,0,3,2,1:T(8,128)(2,1)S(1)} %multiply_convert_fusion, f32[16,4,4,8,64]{4,0,3,2,1:T(8,128)} %copy-done.3), kind=kOutput, calls=%fused_computation.19 | convolution fusion | flops 289234944 | bytes 1007616 | tf_op jit(solution)/shard_map/transpose | solution.py:168
  90.1 1.1 reshape.352
  91.2 7.5 %all-to-all-start.2 = ((bf16[32,2,2358]{2,1,0:T(2,128)(2,1)}), bf16[32,2,2358]{2,1,0:T(2,128)(2,1)S(1)}, u32[]{:S(2)}, u32[]{:S(2)}) async-start(bf16[32,2,2358]{2,1,0:T(2,128)(2,1)} %reshape.352), calls=%async_computation.2 | async-start | bytes 622592 | tf_op jit(solution)/shard_map/all_to_all | solution.py:89
  99.8 15.0 %all-to-all-done.2 = bf16[32,2,2358]{2,1,0:T(2,128)(2,1)S(1)} async-done(((bf16[32,2,2358]{2,1,0:T(2,128)(2,1)}), bf16[32,2,2358]{2,1,0:T(2,128)(2,1)S(1)}, u32[]{:S(2)}, u32[]{:S(2)}) %all-to-all-start.2) | async-done | bytes 301856 | tf_op jit(solution)/shard_map/all_to_all | solution.py:89
  116.7 1.0 broadcast_in_dim.48
  117.7 4.8 %all-to-all-start.3 = ((f32[32,1,3692]{2,1,0:T(1,128)}), f32[32,1,3692]{2,1,0:T(1,128)S(1)}, u32[]{:S(2)}, u32[]{:S(2)}) async-start(f32[32,1,3692]{2,1,0:T(1,128)} %broadcast_in_dim.48), calls=%async_computation.3 | async-start | bytes 950272 | tf_op jit(solution)/shard_map/all_to_all | solution.py:78
  122.6 2.1 %all-gather.6.cloned.1.call-done = bf16[16,16,2048]{2,1,0:T(8,128)(2,1)} async-done(((bf16[2,16,2048]{2,1,0:T(8,128)(2,1)}), bf16[16,16,2048]{2,1,0:T(8,128)(2,1)}) %all-gather.6.cloned.1.call-update) | async-done | bytes 1048592 | tf_op jit(solution)/shard_map/all_gather | solution.py:65
  127.4 12.1 %all-to-all-done.3 = f32[32,1,3692]{2,1,0:T(1,128)S(1)} async-done(((f32[32,1,3692]{2,1,0:T(1,128)}), f32[32,1,3692]{2,1,0:T(1,128)S(1)}, u32[]{:S(2)}, u32[]{:S(2)}) %all-to-all-start.3) | async-done | bytes 472608 | tf_op jit(solution)/shard_map/all_to_all | solution.py:78
  141.6 0.9 multiply_reduce_fusion
  143.3 0.9 copy.135
  144.3 2.1 %broadcast_in_dim_reshape_reshape.3 = f32[1,27,64,64]{3,2,1,0:T(8,128)} reshape(f32[32,3456]{1,0:T(8,128)} %slice.239) | data formatting | bytes 884736 | tf_op jit(solution)/shard_map/broadcast_in_dim;reshape;reshape | solution.py:315
  147.3 1.8 %copy.132 = bf16[8,2,2,16,2048]{4,3,2,1,0:T(8,128)(2,1)S(1)} copy(bf16[8,2,2,16,2048]{4,3,1,0,2:T(8,128)(2,1)} %bitcast.139) | data formatting | bytes 4194304 | tf_op jit(solution)/shard_map/transpose | solution.py:68
  149.7 1.9 %fusion.18 = f32[1,64,2048]{2,1,0:T(8,128)} fusion(f32[64,2048]{1,0:T(8,128)S(1)} %get-tuple-element.122, f32[64]{0:T(128)S(1)} %add_sqrt_fusion, bf16[1,2048,2048]{2,1,0:T(8,128)(2,1)} %param.23, s32[]{:T(128)S(6)} %select_n.37), kind=kLoop, calls=%fused_computation.35 | loop fusion | flops 524288 | bytes 1310980 | tf_op jit(solution)/shard_map/broadcast_in_dim | solution.py:303
  (144 shorter events, 26.4 us)
Async XLA Ops:
  7.9 19.8 %collective-permute-start.2 = (f32[3,1,16,128]{3,2,1,0:T(8,128)S(1)}, f32[3,1,16,128]{3,2,1,0:T(8,128)S(1)}, u32[]{:S(2)}, u32[]{:S(2)}) collective-permute-start(f32[3,1,16,128]{3,2,1,0:T(8,128)S(1)} %get-tuple-element.114), channel_id=1, source_target_pairs={{0,32},{32,64},{64,96},{96,128},{128,160},{160,192},{192,224},{224... | collective-permute-start | bytes 73736 | tf_op jit(solution)/shard_map/ppermute | solution.py:34
  9.4 18.4 %collective-permute-start.3 = (f32[3,1,16,128]{3,2,1,0:T(8,128)S(1)}, f32[3,1,16,128]{3,2,1,0:T(8,128)S(1)}, u32[]{:S(2)}, u32[]{:S(2)}) collective-permute-start(f32[3,1,16,128]{3,2,1,0:T(8,128)S(1)} %get-tuple-element.113), channel_id=1, source_target_pairs={{32,0},{64,32},{96,64},{128,96},{160,128},{192,160},{224,192},{0,2... | collective-permute-start | bytes 73736 | tf_op jit(solution)/shard_map/ppermute | solution.py:35
  11.2 19.6 %collective-permute-start = (f32[3,8,1,128]{3,1,0,2:T(8,128)S(1)}, f32[3,8,1,128]{3,1,0,2:T(8,128)S(1)}, u32[]{:S(2)}, u32[]{:S(2)}) collective-permute-start(f32[3,8,1,128]{3,1,0,2:T(8,128)S(1)} %bitcast.161), channel_id=1, source_target_pairs={{0,1},{1,2},{2,3},{3,4},{4,5},{5,6},{6,7},{7,8},{8,9},{9,10},{10,1... | collective-permute-start | bytes 36872 | tf_op jit(solution)/shard_map/ppermute | solution.py:34
  11.3 19.5 %collective-permute-start.1 = (f32[3,8,1,128]{3,1,0,2:T(8,128)S(1)}, f32[3,8,1,128]{3,1,0,2:T(8,128)S(1)}, u32[]{:S(2)}, u32[]{:S(2)}) collective-permute-start(f32[3,8,1,128]{3,1,0,2:T(8,128)S(1)} %bitcast.160), channel_id=1, source_target_pairs={{1,0},{2,1},{3,2},{4,3},{5,4},{6,5},{7,6},{8,7},{9,8},{10,9},{11,1... | collective-permute-start | bytes 36872 | tf_op jit(solution)/shard_map/ppermute | solution.py:35
  27.7 0.7 copy-start.1
  28.5 9.2 %copy-start = (f32[3,8,16,128]{3,2,1,0:T(8,128)S(1)}, f32[3,8,16,128]{3,2,1,0:T(8,128)}, u32[]{:S(2)}) copy-start(f32[3,8,16,128]{3,2,1,0:T(8,128)} %param.18) | copy-start | bytes 589828
  28.5 9.2 %copy-start.14 = (f32[32,16,1,1]{0,1,3,2:T(8,128)S(1)}, f32[32,16,1,1]{0,1,3,2:T(8,128)}, u32[]{:S(2)}) copy-start(f32[32,16,1,1]{0,1,3,2:T(8,128)} %constant.249) | copy-start | bytes 6148
  28.5 9.7 %copy-start.12 = (bf16[1,54,64]{2,1,0:T(8,128)(2,1)S(1)}, bf16[1,54,64]{2,1,0:T(8,128)(2,1)}, u32[]{:S(2)}) copy-start(bf16[1,54,64]{2,1,0:T(8,128)(2,1)} %param.21) | copy-start | bytes 20740
  29.6 8.6 %copy-start.13 = (bf16[1,2048,2]{1,2,0:T(2,128)(2,1)S(1)}, bf16[1,2048,2]{1,2,0:T(2,128)(2,1)}, u32[]{:S(2)}) copy-start(bf16[1,2048,2]{1,2,0:T(2,128)(2,1)} %param.24) | copy-start | bytes 24580
  29.9 13.8 %copy-start.15 = (bf16[1,27,64,64]{3,2,1,0:T(8,128)(2,1)S(1)}, bf16[1,27,64,64]{3,2,1,0:T(8,128)(2,1)}, u32[]{:S(2)}) copy-start(bf16[1,27,64,64]{3,2,1,0:T(8,128)(2,1)} %param.22) | copy-start | bytes 663556
  31.8 10.7 %all-to-all-start = ((bf16[8,2,259]{2,1,0:T(2,128)(2,1)}), bf16[8,2,259]{2,1,0:T(2,128)(2,1)S(1)}, u32[]{:S(2)}, u32[]{:S(2)}) async-start(bf16[8,2,259]{2,1,0:T(2,128)(2,1)} %pad_maximum_fusion.4), calls=%async_computation | async-start | bytes 24576 | tf_op jit(solution)/shard_map/all_to_all | solution.py:51
  42.5 4.7 %copy-start.11 = (bf16[16,259]{1,0:T(8,128)(2,1)}, bf16[16,259]{1,0:T(8,128)(2,1)S(1)}, u32[]{:S(2)}) copy-start(bf16[16,259]{1,0:T(8,128)(2,1)S(1)} %all_to_all.29) | copy-start | bytes 24868
  43.7 3.5 %copy-start.3 = (f32[16,4,4,8,64]{4,0,3,2,1:T(8,128)}, f32[16,4,4,8,64]{4,0,3,2,1:T(8,128)S(1)}, u32[]{:S(2)}) copy-start(f32[16,4,4,8,64]{4,0,3,2,1:T(8,128)S(1)} %convolution_multiply_fusion.4) | copy-start | bytes 1572868
  48.8 4.8 %slice-start = ((bf16[16,259]{1,0:T(8,128)(2,1)}), bf16[16,2]{1,0:T(8,128)(2,1)S(1)}, s32[]{:S(2)}) async-start(bf16[16,259]{1,0:T(8,128)(2,1)} %copy-done.11), calls=%async_computation.6 | async-start | bytes 8192 | tf_op jit(solution)/shard_map/split | solution.py:52
  54.8 9.6 %all-to-all-start.1 = ((f32[8,2,2]{1,2,0:T(2,128)}), f32[8,2,2]{1,2,0:T(2,128)S(1)}, u32[]{:S(2)}, u32[]{:S(2)}) async-start(f32[8,2,2]{1,2,0:T(2,128)} %copy.126), calls=%async_computation.1 | async-start | bytes 16384 | tf_op jit(solution)/shard_map/all_to_all | solution.py:284
  59.6 65.0 %all-gather.6.cloned.1.call-start = ((), (), s32[]{:S(2)}) async-start(), calls=%async_computation.4 | async-start | bytes 1179648 | tf_op jit(solution)/shard_map/all_gather | solution.py:65
  77.0 1.8 %copy-start.16 = (bf16[1,27,64,64]{3,2,1,0:T(8,128)(2,1)S(1)}, bf16[1,27,64,64]{3,2,1,0:T(8,128)(2,1)}, u32[]{:S(2)}) copy-start(bf16[1,27,64,64]{3,2,1,0:T(8,128)(2,1)} %param.22) | copy-start | bytes 663556
  88.4 10.9 %copy-start.10 = (f32[256,128,1,1]{1,0,3,2:T(8,128)S(1)}, f32[256,128,1,1]{1,0,3,2:T(8,128)}, u32[]{:S(2)}) copy-start(f32[256,128,1,1]{1,0,3,2:T(8,128)} %constant.251) | copy-start | bytes 393220
  91.2 23.7 %all-to-all-start.2 = ((bf16[32,2,2358]{2,1,0:T(2,128)(2,1)}), bf16[32,2,2358]{2,1,0:T(2,128)(2,1)S(1)}, u32[]{:S(2)}, u32[]{:S(2)}) async-start(bf16[32,2,2358]{2,1,0:T(2,128)(2,1)} %reshape.352), calls=%async_computation.2 | async-start | bytes 622592 | tf_op jit(solution)/shard_map/all_to_all | solution.py:89
  115.3 9.6 %copy-start.2 = (f32[16,3,16,128]{3,2,0,1:T(8,128)S(1)}, f32[16,3,16,128]{3,2,0,1:T(8,128)}, u32[]{:S(2)}) copy-start(f32[16,3,16,128]{3,2,0,1:T(8,128)} %copy-done.1) | copy-start | bytes 1179652
  115.4 9.3 %copy-start.4 = (f32[3,8,16,128]{3,2,1,0:T(8,128)S(1)}, f32[3,8,16,128]{3,2,1,0:T(8,128)}, u32[]{:S(2)}) copy-start(f32[3,8,16,128]{3,2,1,0:T(8,128)} %slice.222) | copy-start | bytes 589828
  115.4 9.5 %copy-start.6 = (f32[8,16,128]{2,1,0:T(8,128)S(1)}, f32[8,16,128]{2,1,0:T(8,128)}, u32[]{:S(2)}) copy-start(f32[8,16,128]{2,1,0:T(8,128)} %get-tuple-element.104) | copy-start | bytes 196612
  115.4 9.5 %copy-start.7 = (f32[8,16,128]{2,1,0:T(8,128)S(1)}, f32[8,16,128]{2,1,0:T(8,128)}, u32[]{:S(2)}) copy-start(f32[8,16,128]{2,1,0:T(8,128)} %get-tuple-element.105) | copy-start | bytes 196612
  115.4 9.5 %copy-start.8 = (f32[8,16,128]{2,1,0:T(8,128)S(1)}, f32[8,16,128]{2,1,0:T(8,128)}, u32[]{:S(2)}) copy-start(f32[8,16,128]{2,1,0:T(8,128)} %get-tuple-element.106) | copy-start | bytes 196612
  117.7 21.8 %all-to-all-start.3 = ((f32[32,1,3692]{2,1,0:T(1,128)}), f32[32,1,3692]{2,1,0:T(1,128)S(1)}, u32[]{:S(2)}, u32[]{:S(2)}) async-start(f32[32,1,3692]{2,1,0:T(1,128)} %broadcast_in_dim.48), calls=%async_computation.3 | async-start | bytes 950272 | tf_op jit(solution)/shard_map/all_to_all | solution.py:78
  122.5 24.8 %all-gather.8.cloned.1.call-start = ((), (), s32[]{:S(2)}) async-start(), calls=%async_computation.5 | async-start | bytes 3145728 | tf_op jit(solution)/shard_map/all_gather | solution.py:65
  143.3 3.1 %copy-start.9 = (f32[118,64]{1,0:T(8,128)S(1)}, f32[118,64]{1,0:T(8,128)}, u32[]{:S(2)}) copy-start(f32[118,64]{1,0:T(8,128)} %slice.212) | copy-start | bytes 90628
  147.3 1.8 %copy-start.5 = (bf16[512,64]{1,0:T(8,128)(2,1)S(1)}, bf16[512,64]{1,0:T(8,128)(2,1)}, u32[]{:S(2)}) copy-start(bf16[512,64]{1,0:T(8,128)(2,1)} %reshape.325) | copy-start | bytes 196612
Sparse Core Ops, SparseCore 0:
  84.6 40.0 all-gather.5
  126.5 14.7 all-gather.7
